TPU v7x, 512 devices: a whole 4x4x16 slice. The times are simulated.
512 devices in a mesh: ctx: 32 (over z, core), uly: 16 (over x, y).
Axes of the slice: x: 4, y: 4, z: 16, core: 2. Of those that a mesh axis runs over, the one named last changes fastest.
Arguments:
- query_heads: bfloat16 [1, 8192, 8192], P(None, 'ctx', 'uly'), may hold values from -2.5 to 2.5
- key_heads: bfloat16 [1, 8192, 8192], P(None, 'ctx', 'uly'), may hold values from -2.5 to 2.5
- value_heads: bfloat16 [1, 8192, 8192], P(None, 'ctx', 'uly'), may hold values from -2.5 to 2.5
- grad_out: bfloat16 [1, 8192, 8192], P(None, ('ctx', 'uly')), may hold values from -2.5 to 2.5
- log_decay: float32 [1, 64, 8192], P(None, 'uly', 'ctx'), as said below
Outputs:
- attended: bfloat16 [1, 8192, 8192], P(None, ('ctx', 'uly'))
- grad_query: bfloat16 [1, 8192, 8192], P(None, ('ctx', 'uly'))
- grad_key: bfloat16 [1, 8192, 8192], P(None, ('ctx', 'uly'))
- grad_value: bfloat16 [1, 8192, 8192], P(None, ('ctx', 'uly'))
Inputs may be any that keep to these rules, and one draw needn't show every extreme that they name: `log_decay`: each entry is the logarithm of the share of a head's state that the position keeps.
All inputs are finite; a program needn't handle non-finite values.
Results may differ from a plain program's by a relative error of at most 0.0063.
Values may be sent and summed in bfloat16 or wider, within the bound.
No kernel may reach another device: no remote copies, remote signals or barrier semaphores. Data moves between devices by JAX's collectives and lax.ppermute only.
A program may use at most 64 MiB of HBM per device.

v0:
```python
import jax
import jax.numpy as jnp
from jax import lax
from jax.sharding import PartitionSpec as P


def entering(value, axis, join, neutral, backward):
    count, mine = (lax.axis_size(axis), lax.axis_index(axis))
    pieces = jax.tree.map(lambda part: lax.all_gather(part, axis), value)
    if backward:
        pieces = jax.tree.map(lambda part: part[::-1], pieces)
        mine = count - 1 - mine
    so_far = jax.tree.map(
        lambda part, zero: jnp.full_like(part, 0) + jnp.asarray(zero, part.dtype), value, neutral
    )

    def hop(position, so_far):
        longer = join(so_far, jax.tree.map(lambda part: part[position], pieces))
        return jax.tree.map(lambda new, old: jnp.where(position < mine, new, old), longer, so_far)

    return lax.fori_loop(0, count - 1, hop, so_far)


def decay_tables(log_decay):
    cumulative = jnp.cumsum(log_decay, axis=-1)
    last_cum = cumulative[..., -1:]
    block_len = log_decay.shape[-1]
    row_ids = lax.broadcasted_iota(jnp.int32, (block_len, block_len), 0)
    col_ids = lax.broadcasted_iota(jnp.int32, (block_len, block_len), 1)
    lower_tri = row_ids >= col_ids
    spread = cumulative[..., :, None] - cumulative[..., None, :]
    decay_mask = jnp.where(lower_tri, jnp.exp(jnp.where(lower_tri, spread, 0.0)), 0.0)
    return (cumulative, last_cum, decay_mask)


def to_rows(table):
    return jnp.swapaxes(table, 1, 2)[..., None]


def combine(earlier, latter):
    return (earlier[0] * latter[0], latter[0][..., None, None] * earlier[1] + latter[1])


def local(query_heads, key_heads, value_heads, grad_out, log_decay):
    batch_count, positions, width_all = query_heads.shape
    head_count = log_decay.shape[1]
    head_shape = (batch_count, positions, head_count, width_all // head_count)
    q_split = query_heads.reshape(head_shape)
    k_split = key_heads.reshape(head_shape)
    v_split = value_heads.reshape(head_shape)
    incoming = lax.all_to_all(grad_out, "uly", split_axis=2, concat_axis=1, tiled=True)
    g_split = incoming.reshape(head_shape)
    cumulative, last_cum, decay_mask = decay_tables(log_decay)
    block_keep = jnp.exp(last_cum[..., 0])
    rise_rows = to_rows(jnp.exp(cumulative))
    fall_rows = to_rows(jnp.exp(last_cum - cumulative))
    scaled_query = (rise_rows * q_split).astype(jnp.bfloat16)
    scaled_key = (fall_rows * k_split).astype(jnp.bfloat16)
    update = jnp.einsum("bjhd,bjhe->bhde", scaled_key, v_split, preferred_element_type=jnp.float32)
    local_grad = jnp.einsum(
        "bihd,bihe->bhde", scaled_query, g_split, preferred_element_type=jnp.float32
    )
    state_in = entering(
        (block_keep, update),
        "ctx",
        combine,
        (jnp.ones_like(block_keep), jnp.zeros_like(update)),
        False,
    )[1]
    carried = entering(
        (block_keep, local_grad),
        "ctx",
        combine,
        (jnp.ones_like(block_keep), jnp.zeros_like(local_grad)),
        True,
    )[1]
    scores = jnp.einsum("bihd,bjhd->bhij", q_split, k_split, preferred_element_type=jnp.float32)
    attn_weights = (scores * decay_mask).astype(jnp.bfloat16)
    grad_raw = jnp.einsum("bihe,bjhe->bhij", g_split, v_split, preferred_element_type=jnp.float32)
    grad_scores = (grad_raw * decay_mask).astype(jnp.bfloat16)
    state_b = state_in.astype(jnp.bfloat16)
    attended = jnp.einsum(
        "bhij,bjhd->bihd", attn_weights, v_split, preferred_element_type=jnp.float32
    )
    attended = attended + jnp.einsum(
        "bihd,bhde->bihe", scaled_query, state_b, preferred_element_type=jnp.float32
    )
    query_part = jnp.einsum(
        "bhij,bjhd->bihd", grad_scores, k_split, preferred_element_type=jnp.float32
    )
    query_part = query_part + rise_rows * jnp.einsum(
        "bihe,bhde->bihd", g_split, state_b, preferred_element_type=jnp.float32
    )
    carried_b = carried.astype(jnp.bfloat16)
    key_part = jnp.einsum(
        "bhij,bihd->bjhd", grad_scores, q_split, preferred_element_type=jnp.float32
    )
    key_part = key_part + fall_rows * jnp.einsum(
        "bjhe,bhde->bjhd", v_split, carried_b, preferred_element_type=jnp.float32
    )
    value_part = jnp.einsum(
        "bhij,bihe->bjhe", attn_weights, g_split, preferred_element_type=jnp.float32
    )
    value_part = value_part + fall_rows * jnp.einsum(
        "bjhd,bhde->bjhe", k_split, carried_b, preferred_element_type=jnp.float32
    )

    def to_tokens(array):
        return array.astype(jnp.bfloat16).reshape(batch_count, positions, width_all)

    attended_rows, query_rows, key_rows, value_rows = (
        lax.all_to_all(to_tokens(attended), "uly", split_axis=1, concat_axis=2, tiled=True),
        lax.all_to_all(to_tokens(query_part), "uly", split_axis=1, concat_axis=2, tiled=True),
        lax.all_to_all(to_tokens(key_part), "uly", split_axis=1, concat_axis=2, tiled=True),
        lax.all_to_all(to_tokens(value_part), "uly", split_axis=1, concat_axis=2, tiled=True),
    )
    return (attended_rows, query_rows, key_rows, value_rows)


def solution(mesh):
    placed = (
        P(None, "ctx", "uly"),
        P(None, "ctx", "uly"),
        P(None, "ctx", "uly"),
        P(None, ("ctx", "uly"), None),
        P(None, "uly", "ctx"),
    )
    return jax.shard_map(
        local,
        mesh=mesh,
        in_specs=placed,
        out_specs=(
            P(None, ("ctx", "uly"), None),
            P(None, ("ctx", "uly"), None),
            P(None, ("ctx", "uly"), None),
            P(None, ("ctx", "uly"), None),
        ),
        check_vma=False,
    )
```

profile of v0, /device:TPU:2, one launch (start us, length us, event | category | flops | bytes accessed | tf_op | source)
XLA Modules:
  0.0 278.4 jit_solution(11245880832409896783)
XLA Ops:
  7.9 1.2 reduce-window.6
  9.5 1.1 reshape.285
  12.9 8.4 %copy.172 = bf16[1,16,8192]{1,0,2:T(2,128)(2,1)} copy(bf16[1,16,8192]{2,1,0:T(8,128)(2,1)} %param.12) | data formatting | bytes 524288 | tf_op args[3]
  21.9 45.3 %reduce.1 = bf16[8192,16]{1,0:T(8,128)(2,1)S(1)} reduce(bf16[8192,1,16]{2,1,0:T(2,128)(2,1)} %bitcast.171, bf16[]{:T(256)} %broadcast.69), dimensions={1}, to_apply=%bitcast.141.reduce_sub_computation | reduce | bytes 524290
  67.1 2.8 %reshape.300 = bf16[16,2,4096]{2,1,0:T(2,128)(2,1)} reshape(bf16[8192,16]{1,0:T(8,128)(2,1)S(1)} %reduce.1) | data formatting | bytes 524288
  69.9 9.3 %all-to-all-start.1 = ((bf16[16,2,4096]{2,1,0:T(2,128)(2,1)}), bf16[16,2,4096]{2,1,0:T(2,128)(2,1)S(1)}, u32[]{:S(2)}, u32[]{:S(2)}) async-start(bf16[16,2,4096]{2,1,0:T(2,128)(2,1)} %reshape.300), calls=%async_computation.1 | async-start | bytes 524288 | tf_op jit(solution)/shard_map/all_to_all | solution.py:51
  79.5 6.6 %all-to-all-done.1 = bf16[16,2,4096]{2,1,0:T(2,128)(2,1)S(1)} async-done(((bf16[16,2,4096]{2,1,0:T(2,128)(2,1)}), bf16[16,2,4096]{2,1,0:T(2,128)(2,1)S(1)}, u32[]{:S(2)}, u32[]{:S(2)}) %all-to-all-start.1) | async-done | bytes 262176 | tf_op jit(solution)/shard_map/all_to_all | solution.py:51
  86.1 7.7 %reshape.301 = bf16[8192,1,16]{2,1,0:T(2,128)(2,1)} reshape(bf16[16,2,4096]{2,1,0:T(2,128)(2,1)S(1)} %all-to-all-done.1) | data formatting | bytes 524288
  93.8 7.9 %copy.173 = bf16[1,16,8192]{2,1,0:T(8,128)(2,1)S(1)} copy(bf16[1,16,8192]{1,0,2:T(2,128)(2,1)} %bitcast.172) | data formatting | bytes 524288 | tf_op jit(solution)/shard_map/all_to_all | solution.py:51
  103.1 34.4 %all-gather = f32[32,4,1]{1,2,0:T(1,128)S(1)} all-gather(f32[1,4,1]{1,2,0:T(1,128)S(1)} %get-tuple-element.303), channel_id=2, replica_groups=mesh['ctx'=32,'uly'=16] {'ctx'}, dimensions={0}, use_global_device_ids=true | all-gather | bytes 528 | tf_op jit(solution)/shard_map/all_gather | solution.py:9
  139.5 1.1 convolution_bitcast_fusion.5
  140.9 34.0 %while.28 = (s32[]{:T(128)}, f32[1,4,128,128]{3,2,1,0:T(8,128)S(1)}, s32[]{:T(128)}, f32[32,1,4]{2,1,0:T(1,128)S(1)}, f32[32,1,4,128,128]{4,3,2,1,0:T(8,128)}, /*index=5*/s32[]{:T(128)}, s32[]{:T(128)}) while((s32[]{:T(128)}, f32[1,4,128,128]{3,2,1,0:T(8,128)S(1)}, s32[]{:T(128)}, f32[32,1,4]{2,1,0:T(1,128)S(1)}, ...), condition=%wide.region_3.4_spmd.clone, body=%wide.region_2.3_spmd.clone.sunk | while | flops 262148 | bytes 786585 | solution.py:21
  143.1 1.1 fusion.44
  144.2 1.1 fusion.44
  147.5 1.1 fusion.44
  150.8 1.1 fusion.44
  152.9 1.1 fusion.44
  155.1 1.1 fusion.44
  157.3 1.1 fusion.44
  159.5 1.1 fusion.44
  160.6 1.1 fusion.44
  162.8 1.1 fusion.44
  165.0 1.1 fusion.44
  167.2 1.1 fusion.44
  169.4 1.1 fusion.44
  173.8 1.1 fusion.44
  174.9 1.3 fusion.12
  176.1 1.1 copy.180
  177.2 3.2 %reduce.2 = bf16[256,512]{1,0:T(8,128)(2,1)S(1)} reduce(bf16[256,1,512]{2,1,0:T(2,128)(2,1)} %bitcast.183, bf16[]{:T(256)} %broadcast.69), dimensions={1}, to_apply=%bitcast.143.reduce_sub_computation | reduce | bytes 524290
  181.3 5.4 %all-to-all-start.2 = ((bf16[16,2,4096]{2,1,0:T(2,128)(2,1)}), bf16[16,2,4096]{2,1,0:T(2,128)(2,1)S(1)}, u32[]{:S(2)}, u32[]{:S(2)}) async-start(bf16[16,2,4096]{2,1,0:T(2,128)(2,1)} %reshape.302), calls=%async_computation.2 | async-start | bytes 524288 | tf_op jit(solution)/shard_map/all_to_all | solution.py:113
  187.4 2.3 reduce
  190.6 7.7 %rev.7 = f32[32,1,4,128,128]{4,3,2,1,0:T(8,128)} reverse(f32[32,1,4,128,128]{4,3,2,1,0:T(8,128)} %bitcast.173), dimensions={0} | reverse | bytes 16777216 | tf_op jit(solution)/shard_map/rev | solution.py:11
  198.3 33.8 %while.29 = (s32[]{:T(128)}, f32[1,4,128,128]{3,2,1,0:T(8,128)S(1)}, s32[]{:T(128)}, f32[32,1,4]{2,1,0:T(1,128)S(1)}, f32[32,1,4,128,128]{4,3,2,1,0:T(8,128)}, /*index=5*/s32[]{:T(128)}, s32[]{:T(128)}) while((s32[]{:T(128)}, f32[1,4,128,128]{3,2,1,0:T(8,128)S(1)}, s32[]{:T(128)}, f32[32,1,4]{2,1,0:T(1,128)S(1)}, ...), condition=%wide.region_5.6_spmd.clone, body=%wide.region_4.5_spmd.clone.sunk | while | flops 262148 | bytes 786585 | solution.py:21
  199.4 1.1 fusion.45
  200.5 1.1 fusion.45
  202.6 1.1 fusion.45
  203.7 1.1 fusion.45
  204.8 1.1 fusion.45
  205.9 1.1 fusion.45
  207.0 1.1 fusion.45
  208.1 1.1 fusion.45
  210.3 1.1 fusion.45
  211.4 1.1 fusion.45
  212.5 1.1 fusion.45
  213.6 1.1 fusion.45
  214.7 1.1 fusion.45
  215.8 1.1 fusion.45
  216.9 1.1 fusion.45
  217.9 1.1 fusion.45
  219.0 1.1 fusion.45
  220.1 1.1 fusion.45
  221.2 1.1 fusion.45
  223.4 1.1 fusion.45
  224.5 1.1 fusion.45
  225.6 1.1 fusion.45
  226.7 1.1 fusion.45
  232.1 7.2 %all-to-all-start = ((bf16[16,2,4096]{2,1,0:T(2,128)(2,1)}), bf16[16,2,4096]{2,1,0:T(2,128)(2,1)S(1)}, u32[]{:S(2)}, u32[]{:S(2)}) async-start(bf16[16,2,4096]{2,1,0:T(2,128)(2,1)} %reshape.298), calls=%async_computation | async-start | bytes 524288 | tf_op jit(solution)/shard_map/all_to_all | solution.py:112
  240.1 2.3 reduce.3
  243.2 3.0 %all-to-all-done = bf16[16,2,4096]{2,1,0:T(2,128)(2,1)S(1)} async-done(((bf16[16,2,4096]{2,1,0:T(2,128)(2,1)}), bf16[16,2,4096]{2,1,0:T(2,128)(2,1)S(1)}, u32[]{:S(2)}, u32[]{:S(2)}) %all-to-all-start) | async-done | bytes 262176 | tf_op jit(solution)/shard_map/all_to_all | solution.py:112
  246.2 5.3 %all-to-all-start.3 = ((bf16[16,2,4096]{2,1,0:T(2,128)(2,1)}), bf16[16,2,4096]{2,1,0:T(2,128)(2,1)S(1)}, u32[]{:S(2)}, u32[]{:S(2)}) async-start(bf16[16,2,4096]{2,1,0:T(2,128)(2,1)} %reshape.304), calls=%async_computation.3 | async-start | bytes 524288 | tf_op jit(solution)/shard_map/all_to_all | solution.py:114
  252.3 2.3 reduce.4
  255.4 2.9 %all-to-all-done.3 = bf16[16,2,4096]{2,1,0:T(2,128)(2,1)S(1)} async-done(((bf16[16,2,4096]{2,1,0:T(2,128)(2,1)}), bf16[16,2,4096]{2,1,0:T(2,128)(2,1)S(1)}, u32[]{:S(2)}, u32[]{:S(2)}) %all-to-all-start.3) | async-done | bytes 262176 | tf_op jit(solution)/shard_map/all_to_all | solution.py:114
  258.3 5.3 %all-to-all-start.4 = ((bf16[16,2,4096]{2,1,0:T(2,128)(2,1)}), bf16[16,2,4096]{2,1,0:T(2,128)(2,1)S(1)}, u32[]{:S(2)}, u32[]{:S(2)}) async-start(bf16[16,2,4096]{2,1,0:T(2,128)(2,1)} %reshape.306), calls=%async_computation.4 | async-start | bytes 524288 | tf_op jit(solution)/shard_map/all_to_all | solution.py:115
  266.8 3.7 %all-to-all-done.4 = bf16[16,2,4096]{2,1,0:T(2,128)(2,1)S(1)} async-done(((bf16[16,2,4096]{2,1,0:T(2,128)(2,1)}), bf16[16,2,4096]{2,1,0:T(2,128)(2,1)S(1)}, u32[]{:S(2)}, u32[]{:S(2)}) %all-to-all-start.4) | async-done | bytes 262176 | tf_op jit(solution)/shard_map/all_to_all | solution.py:115
  (155 shorter events, 44.4 us)
Async XLA Ops:
  7.2 133.7 %all-gather.6.cloned.1.call-start = ((), (), s32[]{:S(2)}) async-start(), calls=%async_computation.5 | async-start | bytes 8650752 | tf_op jit(solution)/shard_map/all_gather | solution.py:9
  9.5 69.8 %copy-start = (bf16[1,256,512]{2,1,0:T(8,128)(2,1)S(1)}, bf16[1,256,512]{2,1,0:T(8,128)(2,1)}, u32[]{:S(2)}) copy-start(bf16[1,256,512]{2,1,0:T(8,128)(2,1)} %param.9) | copy-start | bytes 786436
  69.9 16.1 %all-to-all-start.1 = ((bf16[16,2,4096]{2,1,0:T(2,128)(2,1)}), bf16[16,2,4096]{2,1,0:T(2,128)(2,1)S(1)}, u32[]{:S(2)}, u32[]{:S(2)}) async-start(bf16[16,2,4096]{2,1,0:T(2,128)(2,1)} %reshape.300), calls=%async_computation.1 | async-start | bytes 524288 | tf_op jit(solution)/shard_map/all_to_all | solution.py:51
  79.2 111.4 %all-gather.8.cloned.1.call-start = ((), (), s32[]{:S(2)}) async-start(), calls=%async_computation.6 | async-start | bytes 8650752 | tf_op jit(solution)/shard_map/all_gather | solution.py:9
  181.3 50.8 %all-to-all-start.2 = ((bf16[16,2,4096]{2,1,0:T(2,128)(2,1)}), bf16[16,2,4096]{2,1,0:T(2,128)(2,1)S(1)}, u32[]{:S(2)}, u32[]{:S(2)}) async-start(bf16[16,2,4096]{2,1,0:T(2,128)(2,1)} %reshape.302), calls=%async_computation.2 | async-start | bytes 524288 | tf_op jit(solution)/shard_map/all_to_all | solution.py:113
  232.1 14.0 %all-to-all-start = ((bf16[16,2,4096]{2,1,0:T(2,128)(2,1)}), bf16[16,2,4096]{2,1,0:T(2,128)(2,1)S(1)}, u32[]{:S(2)}, u32[]{:S(2)}) async-start(bf16[16,2,4096]{2,1,0:T(2,128)(2,1)} %reshape.298), calls=%async_computation | async-start | bytes 524288 | tf_op jit(solution)/shard_map/all_to_all | solution.py:112
  246.2 12.1 %all-to-all-start.3 = ((bf16[16,2,4096]{2,1,0:T(2,128)(2,1)}), bf16[16,2,4096]{2,1,0:T(2,128)(2,1)S(1)}, u32[]{:S(2)}, u32[]{:S(2)}) async-start(bf16[16,2,4096]{2,1,0:T(2,128)(2,1)} %reshape.304), calls=%async_computation.3 | async-start | bytes 524288 | tf_op jit(solution)/shard_map/all_to_all | solution.py:114
  258.3 12.1 %all-to-all-start.4 = ((bf16[16,2,4096]{2,1,0:T(2,128)(2,1)}), bf16[16,2,4096]{2,1,0:T(2,128)(2,1)S(1)}, u32[]{:S(2)}, u32[]{:S(2)}) async-start(bf16[16,2,4096]{2,1,0:T(2,128)(2,1)} %reshape.306), calls=%async_computation.4 | async-start | bytes 524288 | tf_op jit(solution)/shard_map/all_to_all | solution.py:115
Sparse Core Ops, SparseCore 0:
  13.0 84.0 all-gather.5
  103.2 79.8 all-gather.7
where the time goes:
time: 282 us; the launch traced here: 278 us
  other arithmetic  122 us (43%)
  local copies, waits for them, and re-layouts  50.1 us (18%)
  blocking collectives  34.4 us (12%)
  starting transfers between devices  32.6 us (12%)
  waiting for transfers between devices  16.2 us (6%)
  between operations  14.4 us (5%)
  matrix products  6.68 us (2%)
    select_n x62, other arithmetic, hop(): jnp.where(position < mine, new, old)  65.4 us
    unnamed x7, other arithmetic  55.2 us
    all_gather x1, blocking collectives, entering(): pieces = jax.tree.map(lambda part: lax.all_gather(part, axis), value)  34.4 us
    unnamed x21, local copies, waits for them, and re-layouts  24.5 us
    all_to_all x1, starting transfers between devices, local(): lax.all_to_all(grad_out, 'uly', split_axis=2, concat_axis=1, tiled=True)  9.25 us
    all_to_all x3, local copies, waits for them, and re-layouts, local(): lax.all_to_all(grad_out, 'uly', split_axis=2, concat_axis=1, tiled=True)  8.04 us
    rev x2, local copies, waits for them, and re-layouts, entering(): pieces = jax.tree.map(lambda part: part[::-1], pieces)  7.8 us
    all_to_all x1, starting transfers between devices, local(): lax.all_to_all(to_tokens(attended), 'uly', split_axis=1, concat_axis=2, t...  7.24 us
  transfers between devices with their start and end apart: 7, of which 4 were waited for; matrix products, arithmetic and copies ran while one was open for 62% of the time, Pallas kernels for 0%

commit v1 on v0

v1 whole, which is shorter than its diff:
```python
import jax
import jax.numpy as jnp
from jax import lax
from jax.sharding import PartitionSpec as P


def decay_tables(log_decay):
    cumulative = jnp.cumsum(log_decay, axis=-1)
    last_cum = cumulative[..., -1:]
    block_len = log_decay.shape[-1]
    row_ids = lax.broadcasted_iota(jnp.int32, (block_len, block_len), 0)
    col_ids = lax.broadcasted_iota(jnp.int32, (block_len, block_len), 1)
    lower_tri = row_ids >= col_ids
    spread = cumulative[..., :, None] - cumulative[..., None, :]
    decay_mask = jnp.where(lower_tri, jnp.exp(jnp.where(lower_tri, spread, 0.0)), 0.0)
    return (cumulative, last_cum, decay_mask)


def to_rows(table):
    return jnp.swapaxes(table, 1, 2)[..., None]


def to_pieces(state, count):
    batch_count, head_count, width, _ = state.shape
    banded = state.reshape(batch_count, head_count, count, width // count, width)
    return jnp.transpose(banded, (2, 0, 1, 3, 4))


def from_pieces(pieces):
    count, batch_count, head_count, rows, width = pieces.shape
    return jnp.transpose(pieces, (1, 2, 0, 3, 4)).reshape(batch_count, head_count, count * rows, width)


def block_weights(last_all):
    count = last_all.shape[0]
    inclusive = jnp.cumsum(last_all, axis=0)
    exclusive = inclusive - last_all
    inc = jnp.transpose(inclusive, (1, 2, 0))
    exc = jnp.transpose(exclusive, (1, 2, 0))
    row_ids = lax.broadcasted_iota(jnp.int32, (count, count), 0)
    col_ids = lax.broadcasted_iota(jnp.int32, (count, count), 1)
    earlier = col_ids < row_ids
    later = col_ids > row_ids
    forward_gap = exc[..., :, None] - inc[..., None, :]
    backward_gap = exc[..., None, :] - inc[..., :, None]
    forward = jnp.where(earlier, jnp.exp(jnp.where(earlier, forward_gap, 0.0)), 0.0)
    backward = jnp.where(later, jnp.exp(jnp.where(later, backward_gap, 0.0)), 0.0)
    return forward, backward


def mix_blocks(weights, pieces):
    return jnp.einsum(
        "bhcd,dbhrx->cbhrx", weights, pieces, precision=lax.Precision.HIGHEST,
        preferred_element_type=jnp.float32,
    )


def local(query_heads, key_heads, value_heads, grad_out, log_decay):
    batch_count, positions, width_heads = query_heads.shape
    head_count = log_decay.shape[1]
    width = width_heads // head_count
    uly_count = lax.axis_size("uly")
    ctx_count = lax.axis_size("ctx")
    head_shape = (batch_count, positions, head_count, width)
    q_split = query_heads.reshape(head_shape)
    k_split = key_heads.reshape(head_shape)
    v_split = value_heads.reshape(head_shape)

    rows_in = grad_out.shape[1]
    g_parts = grad_out.reshape(batch_count, rows_in, uly_count, width_heads)
    g_parts = jnp.transpose(g_parts, (2, 0, 1, 3))
    g_parts = lax.all_to_all(g_parts, "uly", 0, 0, tiled=True)
    g_split = jnp.transpose(g_parts, (1, 0, 2, 3)).reshape(head_shape)

    cumulative, last_cum, decay_mask = decay_tables(log_decay)
    rise_rows = to_rows(jnp.exp(cumulative))
    fall_rows = to_rows(jnp.exp(last_cum - cumulative))
    scaled_query = (rise_rows * q_split).astype(jnp.bfloat16)
    scaled_key = (fall_rows * k_split).astype(jnp.bfloat16)
    update = jnp.einsum("bjhd,bjhe->bhde", scaled_key, v_split, preferred_element_type=jnp.float32)

    last_row = jnp.broadcast_to(last_cum, (batch_count, head_count, width))
    send = to_pieces(update, ctx_count)
    last_piece = jnp.broadcast_to(last_row[None, :, :, None, :], (ctx_count, batch_count, head_count, 1, width))
    send = jnp.concatenate([send, last_piece], axis=3)
    got = lax.all_to_all(send, "ctx", 0, 0, tiled=True)
    band = width // ctx_count
    forward_w, backward_w = block_weights(got[:, :, :, band, 0])
    state_pieces = mix_blocks(forward_w, got[:, :, :, :band, :])
    state_in = from_pieces(lax.all_to_all(state_pieces, "ctx", 0, 0, tiled=True))

    local_grad = jnp.einsum(
        "bihd,bihe->bhde", scaled_query, g_split, preferred_element_type=jnp.float32
    )
    got_grad = lax.all_to_all(to_pieces(local_grad, ctx_count), "ctx", 0, 0, tiled=True)
    carried_pieces = mix_blocks(backward_w, got_grad)
    carried = from_pieces(lax.all_to_all(carried_pieces, "ctx", 0, 0, tiled=True))

    scores = jnp.einsum("bihd,bjhd->bhij", q_split, k_split, preferred_element_type=jnp.float32)
    attn_weights = (scores * decay_mask).astype(jnp.bfloat16)
    grad_raw = jnp.einsum("bihe,bjhe->bhij", g_split, v_split, preferred_element_type=jnp.float32)
    grad_scores = (grad_raw * decay_mask).astype(jnp.bfloat16)
    state_b = state_in.astype(jnp.bfloat16)
    attended = jnp.einsum(
        "bhij,bjhd->bihd", attn_weights, v_split, preferred_element_type=jnp.float32
    )
    attended = attended + jnp.einsum(
        "bihd,bhde->bihe", scaled_query, state_b, preferred_element_type=jnp.float32
    )
    query_part = jnp.einsum(
        "bhij,bjhd->bihd", grad_scores, k_split, preferred_element_type=jnp.float32
    )
    query_part = query_part + rise_rows * jnp.einsum(
        "bihe,bhde->bihd", g_split, state_b, preferred_element_type=jnp.float32
    )
    carried_b = carried.astype(jnp.bfloat16)
    key_part = jnp.einsum(
        "bhij,bihd->bjhd", grad_scores, q_split, preferred_element_type=jnp.float32
    )
    key_part = key_part + fall_rows * jnp.einsum(
        "bjhe,bhde->bjhd", v_split, carried_b, preferred_element_type=jnp.float32
    )
    value_part = jnp.einsum(
        "bhij,bihe->bjhe", attn_weights, g_split, preferred_element_type=jnp.float32
    )
    value_part = value_part + fall_rows * jnp.einsum(
        "bjhd,bhde->bjhe", k_split, carried_b, preferred_element_type=jnp.float32
    )

    outs = jnp.stack([attended, query_part, key_part, value_part]).astype(jnp.bfloat16)
    outs = outs.reshape(4, batch_count, uly_count, positions // uly_count, width_heads)
    outs = jnp.transpose(outs, (2, 0, 1, 3, 4))
    outs = lax.all_to_all(outs, "uly", 0, 0, tiled=True)
    outs = jnp.transpose(outs, (1, 2, 3, 0, 4)).reshape(
        4, batch_count, positions // uly_count, uly_count * width_heads
    )
    return (outs[0], outs[1], outs[2], outs[3])


def solution(mesh):
    placed = (
        P(None, "ctx", "uly"),
        P(None, "ctx", "uly"),
        P(None, "ctx", "uly"),
        P(None, ("ctx", "uly"), None),
        P(None, "uly", "ctx"),
    )
    return jax.shard_map(
        local,
        mesh=mesh,
        in_specs=placed,
        out_specs=(
            P(None, ("ctx", "uly"), None),
            P(None, ("ctx", "uly"), None),
            P(None, ("ctx", "uly"), None),
            P(None, ("ctx", "uly"), None),
        ),
        check_vma=False,
    )
```

time: 282 us -> 154 us (0.55)
  the two profiles are of different devices: /device:TPU:2 before, /device:TPU:8 now
where the time goes in v1:
time: 154 us
  waiting for transfers between devices  77.5 us (50%)
  starting transfers between devices  34.6 us (22%)
  blocking collectives  20 us (13%)
  local copies, waits for them, and re-layouts  13.6 us (9%)
  matrix products  4.55 us (3%)
  other arithmetic  2.36 us (2%)
    all_to_all x1, waiting for transfers between devices, local(): got = lax.all_to_all(send, 'ctx', 0, 0, tiled=True)  23.3 us
    all_to_all x1, waiting for transfers between devices, local(): lax.all_to_all(to_pieces(local_grad, ctx_count), 'ctx', 0, 0, tiled=True)  21.1 us
    all_to_all x1, blocking collectives, local(): outs = lax.all_to_all(outs, 'uly', 0, 0, tiled=True)  20 us
    all_to_all x1, waiting for transfers between devices, local(): lax.all_to_all(carried_pieces, 'ctx', 0, 0, tiled=True)  15.7 us
    all_to_all x1, waiting for transfers between devices, local(): lax.all_to_all(state_pieces, 'ctx', 0, 0, tiled=True)  15.2 us
    all_to_all x1, starting transfers between devices, local(): got = lax.all_to_all(send, 'ctx', 0, 0, tiled=True)  13.7 us
    all_to_all x1, starting transfers between devices, local(): g_parts = lax.all_to_all(g_parts, 'uly', 0, 0, tiled=True)  9.28 us
    all_to_all x1, starting transfers between devices, local(): lax.all_to_all(to_pieces(local_grad, ctx_count), 'ctx', 0, 0, tiled=True)  3.87 us
  transfers between devices with their start and end apart: 5, of which 5 were waited for; matrix products, arithmetic and copies ran while one was open for 6% of the time, Pallas kernels for 0%

profile of v1, /device:TPU:8, one launch (start us, length us, event | category | flops | bytes accessed | tf_op | source)
XLA Modules:
  0.0 153.6 jit_solution(6740877658657368121)
XLA Ops:
  0.6 1.0 copy.312
  1.7 0.9 copy.265
  2.5 9.3 %all-to-all-start.2 = ((bf16[16,1,16,512]{3,2,1,0:T(8,128)(2,1)}), bf16[16,1,16,512]{3,2,1,0:T(8,128)(2,1)S(1)}, u32[]{:S(2)}, u32[]{:S(2)}) async-start(bf16[16,1,16,512]{3,2,1,0:T(8,128)(2,1)} %copy.265), calls=%async_computation.2 | async-start | bytes 524288 | tf_op jit(solution)/shard_map/all_to_all | solution.py:72
  11.8 1.2 reduce-window.6
  13.1 0.1 copy.307
  13.3 0.1 copy.243
  13.6 0.8 copy-done
  14.5 0.9 copy-done.1
  15.4 0.1 copy.310
  15.5 0.2 fusion.13
  15.7 0.2 copy.339
  15.9 0.1 broadcast_in_dim_broadcast_in_dim_broadcast_in_dim.2
  16.0 0.8 pad_maximum_fusion
  16.8 2.1 %all-to-all-done.2 = bf16[16,1,16,512]{3,2,1,0:T(8,128)(2,1)S(1)} async-done(((bf16[16,1,16,512]{3,2,1,0:T(8,128)(2,1)}), bf16[16,1,16,512]{3,2,1,0:T(8,128)(2,1)S(1)}, u32[]{:S(2)}, u32[]{:S(2)}) %all-to-all-start.2) | async-done | bytes 262176 | tf_op jit(solution)/shard_map/all_to_all | solution.py:72
  18.9 13.7 %all-to-all-start = ((f32[32,1,4,5,128]{4,2,3,1,0:T(4,128)}), f32[32,1,4,5,128]{4,2,3,1,0:T(4,128)S(1)}, u32[]{:S(2)}, u32[]{:S(2)}) async-start(f32[32,1,4,5,128]{4,2,3,1,0:T(4,128)} %pad_maximum_fusion), calls=%async_computation | async-start | bytes 655360 | tf_op jit(solution)/shard_map/all_to_all | solution.py:86
  32.7 0.1 copy.259
  32.8 0.8 copy-done.2
  33.6 0.1 copy.309
  33.8 0.2 fusion.17
  34.0 0.8 copy.338
  34.8 23.3 %all-to-all-done = f32[32,1,4,5,128]{4,2,3,1,0:T(4,128)S(1)} async-done(((f32[32,1,4,5,128]{4,2,3,1,0:T(4,128)}), f32[32,1,4,5,128]{4,2,3,1,0:T(4,128)S(1)}, u32[]{:S(2)}, u32[]{:S(2)}) %all-to-all-start) | async-done | bytes 327712 | tf_op jit(solution)/shard_map/all_to_all | solution.py:86
  58.1 3.9 %all-to-all-start.3 = ((f32[32,1,4,4,128]{4,3,2,1,0:T(4,128)}), f32[32,1,4,4,128]{4,3,2,1,0:T(4,128)S(1)}, u32[]{:S(2)}, u32[]{:S(2)}) async-start(f32[32,1,4,4,128]{4,3,2,1,0:T(4,128)} %bitcast.158), calls=%async_computation.3 | async-start | bytes 524288 | tf_op jit(solution)/shard_map/all_to_all | solution.py:95
  62.1 0.1 copy.252
  62.2 0.1 copy.253
  62.3 0.1 copy.255
  62.5 0.5 convolution_bitcast_fusion.8
  63.0 0.7 copy.257
  63.7 21.1 %all-to-all-done.3 = f32[32,1,4,4,128]{4,3,2,1,0:T(4,128)S(1)} async-done(((f32[32,1,4,4,128]{4,3,2,1,0:T(4,128)}), f32[32,1,4,4,128]{4,3,2,1,0:T(4,128)S(1)}, u32[]{:S(2)}, u32[]{:S(2)}) %all-to-all-start.3) | async-done | bytes 262176 | tf_op jit(solution)/shard_map/all_to_all | solution.py:95
  84.8 3.9 %all-to-all-start.1 = ((bf16[32,1,4,4,128]{4,3,2,1,0:T(4,128)(2,1)}), bf16[32,1,4,4,128]{4,3,2,1,0:T(4,128)(2,1)S(1)}, u32[]{:S(2)}, u32[]{:S(2)}) async-start(bf16[32,1,4,4,128]{4,3,2,1,0:T(4,128)(2,1)} %copy.257), calls=%async_computation.1 | async-start | bytes 262144 | tf_op jit(solution)/shard_map/all_to_all | solution.py:90
  88.7 0.5 fusion
  89.1 0.3 convolution_bitcast_fusion.6
  89.4 0.5 convolution_bitcast_fusion.7
  89.9 0.7 copy.279
  90.6 15.2 %all-to-all-done.1 = bf16[32,1,4,4,128]{4,3,2,1,0:T(4,128)(2,1)S(1)} async-done(((bf16[32,1,4,4,128]{4,3,2,1,0:T(4,128)(2,1)}), bf16[32,1,4,4,128]{4,3,2,1,0:T(4,128)(2,1)S(1)}, u32[]{:S(2)}, u32[]{:S(2)}) %all-to-all-start.1) | async-done | bytes 131104 | tf_op jit(solution)/shard_map/all_to_all | solution.py:90
  105.8 3.9 %all-to-all-start.4 = ((bf16[32,1,4,4,128]{4,3,2,1,0:T(4,128)(2,1)}), bf16[32,1,4,4,128]{4,3,2,1,0:T(4,128)(2,1)S(1)}, u32[]{:S(2)}, u32[]{:S(2)}) async-start(bf16[32,1,4,4,128]{4,3,2,1,0:T(4,128)(2,1)} %copy.279), calls=%async_computation.4 | async-start | bytes 262144 | tf_op jit(solution)/shard_map/all_to_all | solution.py:97
  109.7 0.4 fusion.1
  110.1 0.3 convolution_bitcast_fusion.3
  110.5 0.3 convolution_bitcast_fusion.1
  110.8 0.3 convolution_bitcast_fusion.5
  111.2 15.7 %all-to-all-done.4 = bf16[32,1,4,4,128]{4,3,2,1,0:T(4,128)(2,1)S(1)} async-done(((bf16[32,1,4,4,128]{4,3,2,1,0:T(4,128)(2,1)}), bf16[32,1,4,4,128]{4,3,2,1,0:T(4,128)(2,1)S(1)}, u32[]{:S(2)}, u32[]{:S(2)}) %all-to-all-start.4) | async-done | bytes 131104 | tf_op jit(solution)/shard_map/all_to_all | solution.py:97
  126.9 0.3 fusion.8
  127.3 0.2 copy.289
  127.5 0.1 stack.18
  127.6 0.3 fusion.12
  127.9 0.2 copy.264
  128.1 0.1 stack.15
  128.2 0.2 fusion.9
  128.4 0.2 fusion.10
  128.7 0.2 copy.272
  128.9 0.1 stack.16
  129.0 0.2 copy.283
  129.2 0.1 stack.17
  129.3 0.1 maximum_bitcast_fusion
  129.5 0.1 copy.290
  129.6 20.0 %all_to_all.30 = bf16[16,4,1,16,512]{4,3,2,1,0:T(8,128)(2,1)S(1)} all-to-all(bf16[16,4,1,16,512]{4,3,2,1,0:T(8,128)(2,1)S(1)} %copy.290), channel_id=1, replica_groups=mesh['ctx'=32,'uly'=16] {'uly'}, dimensions={0} | all-to-all | bytes 2097152 | tf_op jit(solution)/shard_map/all_to_all | solution.py:133
  149.6 0.1 fusion.46
  149.6 0.2 copy.294
  149.8 0.8 squeeze.19
  150.6 0.1 copy.293
  150.8 0.8 squeeze.18
  151.6 0.1 copy.292
  151.8 0.8 squeeze.17
  152.6 0.1 copy.291
  152.7 0.8 squeeze.16
  (29 shorter events, 0.8 us)
Async XLA Ops:
  2.5 9.3 %copy-start.3 = (f32[1,4,256]{2,1,0:T(4,128)S(1)}, f32[1,4,256]{2,1,0:T(4,128)}, u32[]{:S(2)}) copy-start(f32[1,4,256]{2,1,0:T(4,128)} %param.9) | copy-start | bytes 12292
  2.5 16.3 %all-to-all-start.2 = ((bf16[16,1,16,512]{3,2,1,0:T(8,128)(2,1)}), bf16[16,1,16,512]{3,2,1,0:T(8,128)(2,1)S(1)}, u32[]{:S(2)}, u32[]{:S(2)}) async-start(bf16[16,1,16,512]{3,2,1,0:T(8,128)(2,1)} %copy.265), calls=%async_computation.2 | async-start | bytes 524288 | tf_op jit(solution)/shard_map/all_to_all | solution.py:72
  13.5 1.0 copy-start
  14.4 0.9 copy-start.1
  18.9 39.2 %all-to-all-start = ((f32[32,1,4,5,128]{4,2,3,1,0:T(4,128)}), f32[32,1,4,5,128]{4,2,3,1,0:T(4,128)S(1)}, u32[]{:S(2)}, u32[]{:S(2)}) async-start(f32[32,1,4,5,128]{4,2,3,1,0:T(4,128)} %pad_maximum_fusion), calls=%async_computation | async-start | bytes 655360 | tf_op jit(solution)/shard_map/all_to_all | solution.py:86
  32.6 1.0 copy-start.2
  58.1 26.7 %all-to-all-start.3 = ((f32[32,1,4,4,128]{4,3,2,1,0:T(4,128)}), f32[32,1,4,4,128]{4,3,2,1,0:T(4,128)S(1)}, u32[]{:S(2)}, u32[]{:S(2)}) async-start(f32[32,1,4,4,128]{4,3,2,1,0:T(4,128)} %bitcast.158), calls=%async_computation.3 | async-start | bytes 524288 | tf_op jit(solution)/shard_map/all_to_all | solution.py:95
  84.8 21.0 %all-to-all-start.1 = ((bf16[32,1,4,4,128]{4,3,2,1,0:T(4,128)(2,1)}), bf16[32,1,4,4,128]{4,3,2,1,0:T(4,128)(2,1)S(1)}, u32[]{:S(2)}, u32[]{:S(2)}) async-start(bf16[32,1,4,4,128]{4,3,2,1,0:T(4,128)(2,1)} %copy.257), calls=%async_computation.1 | async-start | bytes 262144 | tf_op jit(solution)/shard_map/all_to_all | solution.py:90
  105.8 21.0 %all-to-all-start.4 = ((bf16[32,1,4,4,128]{4,3,2,1,0:T(4,128)(2,1)}), bf16[32,1,4,4,128]{4,3,2,1,0:T(4,128)(2,1)S(1)}, u32[]{:S(2)}, u32[]{:S(2)}) async-start(bf16[32,1,4,4,128]{4,3,2,1,0:T(4,128)(2,1)} %copy.279), calls=%async_computation.4 | async-start | bytes 262144 | tf_op jit(solution)/shard_map/all_to_all | solution.py:97

commit v2 on v1

--- a/solution.py
+++ b/solution.py
@@ -79,28 +79,24 @@
     scaled_key = (fall_rows * k_split).astype(jnp.bfloat16)
     update = jnp.einsum("bjhd,bjhe->bhde", scaled_key, v_split, preferred_element_type=jnp.float32)
 
-    last_row = jnp.broadcast_to(last_cum, (batch_count, head_count, width))
-    send = to_pieces(update, ctx_count)
-    last_piece = jnp.broadcast_to(last_row[None, :, :, None, :], (ctx_count, batch_count, head_count, 1, width))
-    send = jnp.concatenate([send, last_piece], axis=3)
-    got = lax.all_to_all(send, "ctx", 0, 0, tiled=True)
-    band = width // ctx_count
-    forward_w, backward_w = block_weights(got[:, :, :, band, 0])
-    state_pieces = mix_blocks(forward_w, got[:, :, :, :band, :])
-    state_in = from_pieces(lax.all_to_all(state_pieces, "ctx", 0, 0, tiled=True))
-
+    last_all = lax.all_gather(last_cum[..., 0], "ctx")
+    forward_w, backward_w = block_weights(last_all)
     local_grad = jnp.einsum(
         "bihd,bihe->bhde", scaled_query, g_split, preferred_element_type=jnp.float32
     )
-    got_grad = lax.all_to_all(to_pieces(local_grad, ctx_count), "ctx", 0, 0, tiled=True)
-    carried_pieces = mix_blocks(backward_w, got_grad)
-    carried = from_pieces(lax.all_to_all(carried_pieces, "ctx", 0, 0, tiled=True))
+    send = jnp.stack([to_pieces(update, ctx_count), to_pieces(local_grad, ctx_count)], axis=1)
+    got = lax.all_to_all(send.astype(jnp.bfloat16), "ctx", 0, 0, tiled=True)
+    mixed = jnp.stack(
+        [mix_blocks(forward_w, got[:, 0]), mix_blocks(backward_w, got[:, 1])], axis=1
+    ).astype(jnp.bfloat16)
+    back = lax.all_to_all(mixed, "ctx", 0, 0, tiled=True)
+    state_b = from_pieces(back[:, 0])
+    carried_b = from_pieces(back[:, 1])
 
     scores = jnp.einsum("bihd,bjhd->bhij", q_split, k_split, preferred_element_type=jnp.float32)
     attn_weights = (scores * decay_mask).astype(jnp.bfloat16)
     grad_raw = jnp.einsum("bihe,bjhe->bhij", g_split, v_split, preferred_element_type=jnp.float32)
     grad_scores = (grad_raw * decay_mask).astype(jnp.bfloat16)
-    state_b = state_in.astype(jnp.bfloat16)
     attended = jnp.einsum(
         "bhij,bjhd->bihd", attn_weights, v_split, preferred_element_type=jnp.float32
     )
@@ -113,7 +109,6 @@
     query_part = query_part + rise_rows * jnp.einsum(
         "bihe,bhde->bihd", g_split, state_b, preferred_element_type=jnp.float32
     )
-    carried_b = carried.astype(jnp.bfloat16)
     key_part = jnp.einsum(
         "bhij,bihd->bjhd", grad_scores, q_split, preferred_element_type=jnp.float32
     )

time: 154 us -> 135 us (0.88)
  waiting for transfers between devices: 77.5 us -> 23.6 us
  blocking collectives: 20 us -> 58.4 us
  local copies, waits for them, and re-layouts: 13.6 us -> 11.3 us
    all_to_all x4 -> x2, waiting for transfers between devices: 75.4 us -> 20.7 us  [the longest x1 20.7 us: local(): back = lax.all_to_all(mixed, 'ctx', 0, 0, tiled=True)]
    all_gather x0 -> x1, blocking collectives: none -> 38.1 us  [local(): last_all = lax.all_gather(last_cum[..., 0], 'ctx')]
    all_to_all x4 -> x2, starting transfers between devices: 25.3 us -> 24 us  [the longest x1 13.7 us: local(): got = lax.all_to_all(send.astype(jnp.bfloat16), 'ctx', 0, 0, tiled=True)]
  transfers between devices with their start and end apart: 5 -> 3, of which waited for: 5 -> 2; matrix products, arithmetic and copies ran while one was open for 6% -> 4% of each run, Pallas kernels for 0% -> 0%
where the time goes in v2:
time: 135 us
  blocking collectives  58.4 us (43%)
  starting transfers between devices  33.3 us (25%)
  waiting for transfers between devices  23.6 us (17%)
  local copies, waits for them, and re-layouts  11.3 us (8%)
  matrix products  4.53 us (3%)
  other arithmetic  2.62 us (2%)
    all_gather x1, blocking collectives, local(): last_all = lax.all_gather(last_cum[..., 0], 'ctx')  38.1 us
    all_to_all x1, waiting for transfers between devices, local(): back = lax.all_to_all(mixed, 'ctx', 0, 0, tiled=True)  20.7 us
    all_to_all x1, blocking collectives, local(): outs = lax.all_to_all(outs, 'uly', 0, 0, tiled=True)  20.3 us
    all_to_all x1, starting transfers between devices, local(): got = lax.all_to_all(send.astype(jnp.bfloat16), 'ctx', 0, 0, tiled=True)  13.7 us
    all_to_all x1, starting transfers between devices, local(): back = lax.all_to_all(mixed, 'ctx', 0, 0, tiled=True)  10.3 us
    all_to_all x1, starting transfers between devices, local(): g_parts = lax.all_to_all(g_parts, 'uly', 0, 0, tiled=True)  9.28 us
    squeeze x4, local copies, waits for them, and re-layouts, local(): return (outs[0], outs[1], outs[2], outs[3])  3.31 us
    all_to_all x1, waiting for transfers between devices, local(): g_parts = lax.all_to_all(g_parts, 'uly', 0, 0, tiled=True)  2.97 us
  transfers between devices with their start and end apart: 3, of which 2 were waited for; matrix products, arithmetic and copies ran while one was open for 4% of the time, Pallas kernels for 0%

profile of v2, /device:TPU:8, one launch (start us, length us, event | category | flops | bytes accessed | tf_op | source)
XLA Modules:
  0.0 134.8 jit_solution(4670839888624510659)
XLA Ops:
  0.6 1.0 copy.234
  1.7 0.9 copy.179
  2.5 9.3 %all-to-all-start = ((bf16[16,1,16,512]{3,2,1,0:T(8,128)(2,1)}), bf16[16,1,16,512]{3,2,1,0:T(8,128)(2,1)S(1)}, u32[]{:S(2)}, u32[]{:S(2)}) async-start(bf16[16,1,16,512]{3,2,1,0:T(8,128)(2,1)} %copy.179), calls=%async_computation | async-start | bytes 524288 | tf_op jit(solution)/shard_map/all_to_all | solution.py:72
  11.8 1.2 reduce-window.6
  13.1 0.1 slice.48
  13.2 0.1 copy.173
  13.3 0.1 exponential_bitcast_fusion
  13.4 0.2 fusion.50
  13.6 0.1 exponential_bitcast_fusion.1
  13.6 0.1 reshape.457
  13.7 0.9 copy-done.1
  14.6 0.1 reshape.464
  14.7 0.9 copy-done.2
  15.6 0.1 copy.232
  15.7 0.2 convolution_convert_fusion.1
  15.9 3.0 %all-to-all-done = bf16[16,1,16,512]{3,2,1,0:T(8,128)(2,1)S(1)} async-done(((bf16[16,1,16,512]{3,2,1,0:T(8,128)(2,1)}), bf16[16,1,16,512]{3,2,1,0:T(8,128)(2,1)S(1)}, u32[]{:S(2)}, u32[]{:S(2)}) %all-to-all-start) | async-done | bytes 262176 | tf_op jit(solution)/shard_map/all_to_all | solution.py:72
  19.0 0.5 convolution_convert_fusion
  19.5 0.1 copy_bitcast_fusion.4
  19.6 0.9 pad_maximum_fusion
  20.4 13.7 %all-to-all-start.1 = ((bf16[32,2,1,4,4,128]{5,4,3,2,1,0:T(4,128)(2,1)}), bf16[32,2,1,4,4,128]{5,4,3,2,1,0:T(4,128)(2,1)S(1)}, u32[]{:S(2)}, u32[]{:S(2)}) async-start(bf16[32,2,1,4,4,128]{5,4,3,2,1,0:T(4,128)(2,1)} %pad_maximum_fusion), calls=%async_computation.1 | async-start | bytes 524288 | tf_op jit(solution)/shard_map/all_to_all | solution.py:88
  34.2 0.1 copy.184
  34.3 38.1 %all-gather = f32[32,4,1]{1,2,0:T(1,128)S(1)} all-gather(f32[1,4,1]{1,2,0:T(1,128)S(1)} %copy.184), channel_id=2, replica_groups=mesh['ctx'=32,'uly'=16] {'ctx'}, dimensions={0}, use_global_device_ids=true | all-gather | bytes 528 | tf_op jit(solution)/shard_map/all_gather | solution.py:82
  72.4 0.1 copy.185
  72.5 0.1 copy.186
  72.6 0.1 copy.188
  72.7 0.1 copy.189
  72.9 0.1 bitcast_add_fusion
  72.9 0.1 fusion.49
  73.0 0.3 fusion.13
  73.4 0.3 fusion.14
  73.7 0.8 copy.191
  74.6 10.3 %all-to-all-start.2 = ((bf16[32,2,1,4,4,128]{5,4,3,2,1,0:T(4,128)(2,1)}), bf16[32,2,1,4,4,128]{5,4,3,2,1,0:T(4,128)(2,1)S(1)}, u32[]{:S(2)}, u32[]{:S(2)}) async-start(bf16[32,2,1,4,4,128]{5,4,3,2,1,0:T(4,128)(2,1)} %copy.191), calls=%async_computation.2 | async-start | bytes 524288 | tf_op jit(solution)/shard_map/all_to_all | solution.py:92
  84.9 0.4 fusion
  85.3 0.3 convolution_bitcast_fusion.6
  85.6 0.3 convolution_bitcast_fusion.1
  85.9 0.4 fusion.1
  86.3 0.3 convolution_bitcast_fusion.3
  86.7 0.3 convolution_bitcast_fusion.5
  87.0 20.7 %all-to-all-done.2 = bf16[32,2,1,4,4,128]{5,4,3,2,1,0:T(4,128)(2,1)S(1)} async-done(((bf16[32,2,1,4,4,128]{5,4,3,2,1,0:T(4,128)(2,1)}), bf16[32,2,1,4,4,128]{5,4,3,2,1,0:T(4,128)(2,1)S(1)}, u32[]{:S(2)}, u32[]{:S(2)}) %all-to-all-start.2) | async-done | bytes 262176 | tf_op jit(solution)/shard_map/all_to_all | solution.py:92
  107.6 0.1 slice_bitcast_fusion.1
  107.8 0.3 fusion.8
  108.2 0.2 copy.213
  108.4 0.1 stack.42
  108.5 0.3 fusion.12
  108.8 0.2 copy.195
  109.0 0.1 stack.39
  109.1 0.2 fusion.9
  109.4 0.2 fusion.10
  109.6 0.2 copy.201
  109.8 0.1 stack.40
  109.9 0.2 copy.207
  110.1 0.1 stack.41
  110.3 0.1 maximum_bitcast_fusion
  110.4 0.1 copy.214
  110.5 20.3 %all_to_all.20 = bf16[16,4,1,16,512]{4,3,2,1,0:T(8,128)(2,1)S(1)} all-to-all(bf16[16,4,1,16,512]{4,3,2,1,0:T(8,128)(2,1)S(1)} %copy.214), channel_id=1, replica_groups=mesh['ctx'=32,'uly'=16] {'uly'}, dimensions={0} | all-to-all | bytes 2097152 | tf_op jit(solution)/shard_map/all_to_all | solution.py:128
  130.8 0.1 fusion.48
  130.9 0.2 copy.218
  131.0 0.8 squeeze.25
  131.9 0.1 copy.217
  132.0 0.8 squeeze.24
  132.8 0.1 copy.216
  133.0 0.8 squeeze.23
  133.8 0.1 copy.215
  134.0 0.8 squeeze.22
  (21 shorter events, 0.4 us)
Async XLA Ops:
  2.5 9.3 %copy-start.3 = (f32[1,4,256]{2,1,0:T(4,128)S(1)}, f32[1,4,256]{2,1,0:T(4,128)}, u32[]{:S(2)}) copy-start(f32[1,4,256]{2,1,0:T(4,128)} %param.9) | copy-start | bytes 12292
  2.5 11.1 %copy-start = (bf16[1,256,512]{2,1,0:T(8,128)(2,1)S(1)}, bf16[1,256,512]{2,1,0:T(8,128)(2,1)}, u32[]{:S(2)}) copy-start(bf16[1,256,512]{2,1,0:T(8,128)(2,1)} %param.5) | copy-start | bytes 786436
  2.5 16.3 %all-to-all-start = ((bf16[16,1,16,512]{3,2,1,0:T(8,128)(2,1)}), bf16[16,1,16,512]{3,2,1,0:T(8,128)(2,1)S(1)}, u32[]{:S(2)}, u32[]{:S(2)}) async-start(bf16[16,1,16,512]{3,2,1,0:T(8,128)(2,1)} %copy.179), calls=%async_computation | async-start | bytes 524288 | tf_op jit(solution)/shard_map/all_to_all | solution.py:72
  13.6 1.0 copy-start.1
  14.6 0.9 copy-start.2
  20.4 52.5 %all-to-all-start.1 = ((bf16[32,2,1,4,4,128]{5,4,3,2,1,0:T(4,128)(2,1)}), bf16[32,2,1,4,4,128]{5,4,3,2,1,0:T(4,128)(2,1)S(1)}, u32[]{:S(2)}, u32[]{:S(2)}) async-start(bf16[32,2,1,4,4,128]{5,4,3,2,1,0:T(4,128)(2,1)} %pad_maximum_fusion), calls=%async_computation.1 | async-start | bytes 524288 | tf_op jit(solution)/shard_map/all_to_all | solution.py:88
  74.6 33.1 %all-to-all-start.2 = ((bf16[32,2,1,4,4,128]{5,4,3,2,1,0:T(4,128)(2,1)}), bf16[32,2,1,4,4,128]{5,4,3,2,1,0:T(4,128)(2,1)S(1)}, u32[]{:S(2)}, u32[]{:S(2)}) async-start(bf16[32,2,1,4,4,128]{5,4,3,2,1,0:T(4,128)(2,1)} %copy.191), calls=%async_computation.2 | async-start | bytes 524288 | tf_op jit(solution)/shard_map/all_to_all | solution.py:92

commit v3 on v2

--- a/solution.py
+++ b/solution.py
@@ -79,15 +79,23 @@
     scaled_key = (fall_rows * k_split).astype(jnp.bfloat16)
     update = jnp.einsum("bjhd,bjhe->bhde", scaled_key, v_split, preferred_element_type=jnp.float32)
 
-    last_all = lax.all_gather(last_cum[..., 0], "ctx")
-    forward_w, backward_w = block_weights(last_all)
     local_grad = jnp.einsum(
         "bihd,bihe->bhde", scaled_query, g_split, preferred_element_type=jnp.float32
     )
-    send = jnp.stack([to_pieces(update, ctx_count), to_pieces(local_grad, ctx_count)], axis=1)
-    got = lax.all_to_all(send.astype(jnp.bfloat16), "ctx", 0, 0, tiled=True)
+    band = width // ctx_count
+    last_row = jnp.broadcast_to(last_cum, (batch_count, head_count, width))
+    last_piece = jnp.broadcast_to(last_row[None, :, :, None, :], (ctx_count, batch_count, head_count, 1, width))
+    send = jnp.concatenate(
+        [to_pieces(update, ctx_count), to_pieces(local_grad, ctx_count), last_piece], axis=3
+    )
+    got = lax.all_to_all(send, "ctx", 0, 0, tiled=True)
+    forward_w, backward_w = block_weights(got[:, :, :, 2 * band, 0])
     mixed = jnp.stack(
-        [mix_blocks(forward_w, got[:, 0]), mix_blocks(backward_w, got[:, 1])], axis=1
+        [
+            mix_blocks(forward_w, got[:, :, :, :band]),
+            mix_blocks(backward_w, got[:, :, :, band : 2 * band]),
+        ],
+        axis=1,
     ).astype(jnp.bfloat16)
     back = lax.all_to_all(mixed, "ctx", 0, 0, tiled=True)
     state_b = from_pieces(back[:, 0])

time: 135 us -> 128 us (0.948)
  blocking collectives: 58.4 us -> 20.1 us
  waiting for transfers between devices: 23.6 us -> 59.3 us
  starting transfers between devices: 33.3 us -> 26.9 us
    all_gather x1 -> x0, blocking collectives: 38.1 us -> none  [local(): last_all = lax.all_gather(last_cum[..., 0], 'ctx')]
    all_to_all x1, waiting for transfers between devices: 0.01 us -> 36.4 us  [local(): got = lax.all_to_all(send, 'ctx', 0, 0, tiled=True)]
    all_to_all x1, starting transfers between devices: 10.3 us -> 3.87 us  [local(): back = lax.all_to_all(mixed, 'ctx', 0, 0, tiled=True)]
  transfers between devices with their start and end apart: 3 -> 3, of which waited for: 2 -> 3; matrix products, arithmetic and copies ran while one was open for 4% -> 4% of each run, Pallas kernels for 0% -> 0%
where the time goes in v3:
time: 128 us; the launch traced here: 127 us
  waiting for transfers between devices  59.3 us (46%)
  starting transfers between devices  26.9 us (21%)
  blocking collectives  20.1 us (16%)
  local copies, waits for them, and re-layouts  12.5 us (10%)
  matrix products  4.81 us (4%)
  other arithmetic  2.54 us (2%)
    all_to_all x1, waiting for transfers between devices, local(): got = lax.all_to_all(send, 'ctx', 0, 0, tiled=True)  36.4 us
    all_to_all x1, waiting for transfers between devices, local(): back = lax.all_to_all(mixed, 'ctx', 0, 0, tiled=True)  20.7 us
    all_to_all x1, blocking collectives, local(): outs = lax.all_to_all(outs, 'uly', 0, 0, tiled=True)  20.1 us
    all_to_all x1, starting transfers between devices, local(): got = lax.all_to_all(send, 'ctx', 0, 0, tiled=True)  13.7 us
    all_to_all x1, starting transfers between devices, local(): g_parts = lax.all_to_all(g_parts, 'uly', 0, 0, tiled=True)  9.28 us
    all_to_all x1, starting transfers between devices, local(): back = lax.all_to_all(mixed, 'ctx', 0, 0, tiled=True)  3.87 us
    unnamed x9, local copies, waits for them, and re-layouts  3.54 us
    squeeze x4, local copies, waits for them, and re-layouts, local(): return (outs[0], outs[1], outs[2], outs[3])  3.31 us
  transfers between devices with their start and end apart: 3, of which 3 were waited for; matrix products, arithmetic and copies ran while one was open for 4% of the time, Pallas kernels for 0%

profile of v3, /device:TPU:8, one launch (start us, length us, event | category | flops | bytes accessed | tf_op | source)
XLA Modules:
  0.0 127.1 jit_solution(13085027671622431575)
XLA Ops:
  0.6 1.0 copy.309
  1.7 0.9 copy.251
  2.5 9.3 %all-to-all-start = ((bf16[16,1,16,512]{3,2,1,0:T(8,128)(2,1)}), bf16[16,1,16,512]{3,2,1,0:T(8,128)(2,1)S(1)}, u32[]{:S(2)}, u32[]{:S(2)}) async-start(bf16[16,1,16,512]{3,2,1,0:T(8,128)(2,1)} %copy.251), calls=%async_computation | async-start | bytes 524288 | tf_op jit(solution)/shard_map/all_to_all | solution.py:72
  11.8 1.2 reduce-window.6
  13.1 0.1 slice.52
  13.1 0.1 copy.304
  13.3 0.1 copy.241
  13.5 0.1 copy.249
  13.6 0.1 copy.245
  13.7 0.7 copy-done
  14.4 0.1 reshape.432
  14.5 0.9 copy-done.1
  15.4 0.1 reshape.439
  15.5 0.9 copy-done.2
  16.3 0.1 copy.307
  16.5 0.2 fusion.15
  16.7 2.2 %all-to-all-done = bf16[16,1,16,512]{3,2,1,0:T(8,128)(2,1)S(1)} async-done(((bf16[16,1,16,512]{3,2,1,0:T(8,128)(2,1)}), bf16[16,1,16,512]{3,2,1,0:T(8,128)(2,1)S(1)}, u32[]{:S(2)}, u32[]{:S(2)}) %all-to-all-start) | async-done | bytes 262176 | tf_op jit(solution)/shard_map/all_to_all | solution.py:72
  19.0 0.5 fusion.17
  19.5 0.3 copy_bitcast_fusion.4
  19.8 0.1 broadcast_in_dim_broadcast_in_dim_broadcast_in_dim.2
  19.9 0.9 pad_maximum_fusion
  20.8 13.7 %all-to-all-start.1 = ((f32[32,1,4,9,128]{4,2,3,1,0:T(4,128)}), f32[32,1,4,9,128]{4,2,3,1,0:T(4,128)S(1)}, u32[]{:S(2)}, u32[]{:S(2)}) async-start(f32[32,1,4,9,128]{4,2,3,1,0:T(4,128)} %pad_maximum_fusion), calls=%async_computation.1 | async-start | bytes 1179648 | tf_op jit(solution)/shard_map/all_to_all | solution.py:91
  34.6 0.1 copy.303
  34.8 36.4 %all-to-all-done.1 = f32[32,1,4,9,128]{4,2,3,1,0:T(4,128)S(1)} async-done(((f32[32,1,4,9,128]{4,2,3,1,0:T(4,128)}), f32[32,1,4,9,128]{4,2,3,1,0:T(4,128)S(1)}, u32[]{:S(2)}, u32[]{:S(2)}) %all-to-all-start.1) | async-done | bytes 589856 | tf_op jit(solution)/shard_map/all_to_all | solution.py:91
  71.1 0.1 copy.256
  71.2 0.1 copy.257
  71.4 0.1 copy.259
  71.5 0.1 copy.260
  71.6 0.5 fusion.14
  72.1 0.5 fusion.13
  72.6 0.8 copy.262
  73.4 3.9 %all-to-all-start.2 = ((bf16[32,2,1,4,4,128]{5,4,3,2,1,0:T(4,128)(2,1)}), bf16[32,2,1,4,4,128]{5,4,3,2,1,0:T(4,128)(2,1)S(1)}, u32[]{:S(2)}, u32[]{:S(2)}) async-start(bf16[32,2,1,4,4,128]{5,4,3,2,1,0:T(4,128)(2,1)} %copy.262), calls=%async_computation.2 | async-start | bytes 524288 | tf_op jit(solution)/shard_map/all_to_all | solution.py:100
  77.3 0.4 fusion
  77.7 0.3 convolution_bitcast_fusion.6
  78.0 0.3 convolution_bitcast_fusion.1
  78.3 0.4 fusion.1
  78.7 0.3 convolution_bitcast_fusion.3
  79.1 0.3 convolution_bitcast_fusion.5
  79.4 20.7 %all-to-all-done.2 = bf16[32,2,1,4,4,128]{5,4,3,2,1,0:T(4,128)(2,1)S(1)} async-done(((bf16[32,2,1,4,4,128]{5,4,3,2,1,0:T(4,128)(2,1)}), bf16[32,2,1,4,4,128]{5,4,3,2,1,0:T(4,128)(2,1)S(1)}, u32[]{:S(2)}, u32[]{:S(2)}) %all-to-all-start.2) | async-done | bytes 262176 | tf_op jit(solution)/shard_map/all_to_all | solution.py:100
  100.1 0.1 slice_bitcast_fusion.1
  100.3 0.3 fusion.8
  100.6 0.2 copy.286
  100.8 0.1 stack.30
  100.9 0.3 fusion.12
  101.3 0.2 copy.266
  101.5 0.1 stack.27
  101.6 0.2 fusion.9
  101.8 0.2 fusion.10
  102.1 0.2 copy.273
  102.3 0.1 stack.28
  102.4 0.2 copy.280
  102.6 0.1 stack.29
  102.7 0.1 maximum_bitcast_fusion
  102.9 0.1 copy.287
  103.0 20.1 %all_to_all.20 = bf16[16,4,1,16,512]{4,3,2,1,0:T(8,128)(2,1)S(1)} all-to-all(bf16[16,4,1,16,512]{4,3,2,1,0:T(8,128)(2,1)S(1)} %copy.287), channel_id=1, replica_groups=mesh['ctx'=32,'uly'=16] {'uly'}, dimensions={0} | all-to-all | bytes 2097152 | tf_op jit(solution)/shard_map/all_to_all | solution.py:136
  123.1 0.1 fusion.50
  123.2 0.2 copy.291
  123.3 0.8 squeeze.27
  124.2 0.1 copy.290
  124.3 0.8 squeeze.26
  125.1 0.1 copy.289
  125.3 0.8 squeeze.25
  126.1 0.1 copy.288
  126.3 0.8 squeeze.24
  (25 shorter events, 0.5 us)
Async XLA Ops:
  2.5 9.3 %copy-start.3 = (f32[1,4,256]{2,1,0:T(4,128)S(1)}, f32[1,4,256]{2,1,0:T(4,128)}, u32[]{:S(2)}) copy-start(f32[1,4,256]{2,1,0:T(4,128)} %param.9) | copy-start | bytes 12292
  2.5 16.3 %all-to-all-start = ((bf16[16,1,16,512]{3,2,1,0:T(8,128)(2,1)}), bf16[16,1,16,512]{3,2,1,0:T(8,128)(2,1)S(1)}, u32[]{:S(2)}, u32[]{:S(2)}) async-start(bf16[16,1,16,512]{3,2,1,0:T(8,128)(2,1)} %copy.251), calls=%async_computation | async-start | bytes 524288 | tf_op jit(solution)/shard_map/all_to_all | solution.py:72
  13.5 1.0 copy-start
  14.4 0.9 copy-start.1
  15.4 0.9 copy-start.2
  20.8 50.3 %all-to-all-start.1 = ((f32[32,1,4,9,128]{4,2,3,1,0:T(4,128)}), f32[32,1,4,9,128]{4,2,3,1,0:T(4,128)S(1)}, u32[]{:S(2)}, u32[]{:S(2)}) async-start(f32[32,1,4,9,128]{4,2,3,1,0:T(4,128)} %pad_maximum_fusion), calls=%async_computation.1 | async-start | bytes 1179648 | tf_op jit(solution)/shard_map/all_to_all | solution.py:91
  73.4 26.7 %all-to-all-start.2 = ((bf16[32,2,1,4,4,128]{5,4,3,2,1,0:T(4,128)(2,1)}), bf16[32,2,1,4,4,128]{5,4,3,2,1,0:T(4,128)(2,1)S(1)}, u32[]{:S(2)}, u32[]{:S(2)}) async-start(bf16[32,2,1,4,4,128]{5,4,3,2,1,0:T(4,128)(2,1)} %copy.262), calls=%async_computation.2 | async-start | bytes 524288 | tf_op jit(solution)/shard_map/all_to_all | solution.py:100

commit v4 on v3

--- a/solution.py
+++ b/solution.py
@@ -1,7 +1,7 @@
 import jax
 import jax.numpy as jnp
 from jax import lax
-from jax.sharding import PartitionSpec as P
+from jax.sharding import Mesh, PartitionSpec as P
 
 
 def decay_tables(log_decay):
@@ -21,8 +21,8 @@
 
 
 def to_pieces(state, count):
-    batch_count, head_count, width, _ = state.shape
-    banded = state.reshape(batch_count, head_count, count, width // count, width)
+    batch_count, head_count, rows, width = state.shape
+    banded = state.reshape(batch_count, head_count, count, rows // count, width)
     return jnp.transpose(banded, (2, 0, 1, 3, 4))
 
 
@@ -60,7 +60,6 @@
     head_count = log_decay.shape[1]
     width = width_heads // head_count
     uly_count = lax.axis_size("uly")
-    ctx_count = lax.axis_size("ctx")
     head_shape = (batch_count, positions, head_count, width)
     q_split = query_heads.reshape(head_shape)
     k_split = key_heads.reshape(head_shape)
@@ -82,13 +81,38 @@
     local_grad = jnp.einsum(
         "bihd,bihe->bhde", scaled_query, g_split, preferred_element_type=jnp.float32
     )
-    band = width // ctx_count
-    last_row = jnp.broadcast_to(last_cum, (batch_count, head_count, width))
-    last_piece = jnp.broadcast_to(last_row[None, :, :, None, :], (ctx_count, batch_count, head_count, 1, width))
+    chip_count = lax.axis_size("z")
+    core = lax.axis_index("core")
+    second = core == 1
+    pairs = [(0, 1), (1, 0)]
+    last = last_cum[..., 0]
+    other_update, other_grad, other_last = lax.ppermute((update, local_grad, last), "core", pairs)
+
+    def order(mine, other):
+        return jnp.where(second, other, mine), jnp.where(second, mine, other)
+
+    update_lo, update_hi = order(update, other_update)
+    grad_lo, grad_hi = order(local_grad, other_grad)
+    last_lo, last_hi = order(last, other_last)
+    keep_lo = jnp.exp(last_lo)[..., None, None]
+    keep_hi = jnp.exp(last_hi)[..., None, None]
+    chip_update = keep_hi * update_lo + update_hi
+    chip_grad = keep_lo * grad_hi + grad_lo
+    half = width // 2
+    band = half // chip_count
+
+    def my_half(state):
+        return lax.dynamic_slice_in_dim(state, core * half, half, axis=2)
+
+    chip_last = jnp.broadcast_to((last_lo + last_hi)[..., None], (batch_count, head_count, width))
+    last_piece = jnp.broadcast_to(
+        chip_last[None, :, :, None, :], (chip_count, batch_count, head_count, 1, width)
+    )
     send = jnp.concatenate(
-        [to_pieces(update, ctx_count), to_pieces(local_grad, ctx_count), last_piece], axis=3
+        [to_pieces(my_half(chip_update), chip_count), to_pieces(my_half(chip_grad), chip_count), last_piece],
+        axis=3,
     )
-    got = lax.all_to_all(send, "ctx", 0, 0, tiled=True)
+    got = lax.all_to_all(send, "z", 0, 0, tiled=True)
     forward_w, backward_w = block_weights(got[:, :, :, 2 * band, 0])
     mixed = jnp.stack(
         [
@@ -96,10 +120,14 @@
             mix_blocks(backward_w, got[:, :, :, band : 2 * band]),
         ],
         axis=1,
-    ).astype(jnp.bfloat16)
-    back = lax.all_to_all(mixed, "ctx", 0, 0, tiled=True)
-    state_b = from_pieces(back[:, 0])
-    carried_b = from_pieces(back[:, 1])
+    )
+    back = lax.all_to_all(mixed, "z", 0, 0, tiled=True)
+    halves = jnp.stack([from_pieces(back[:, 0]), from_pieces(back[:, 1])])
+    other_halves = lax.ppermute(halves, "core", pairs)
+    low_rows, high_rows = order(halves, other_halves)
+    entering = jnp.concatenate([low_rows, high_rows], axis=3)
+    state_b = jnp.where(second, keep_lo * entering[0] + update_lo, entering[0]).astype(jnp.bfloat16)
+    carried_b = jnp.where(second, entering[1], keep_hi * entering[1] + grad_hi).astype(jnp.bfloat16)
 
     scores = jnp.einsum("bihd,bjhd->bhij", q_split, k_split, preferred_element_type=jnp.float32)
     attn_weights = (scores * decay_mask).astype(jnp.bfloat16)
@@ -141,22 +169,25 @@
 
 
 def solution(mesh):
+    ctx_count, uly_count = mesh.shape["ctx"], mesh.shape["uly"]
+    grid = mesh.devices.reshape(ctx_count // 2, 2, uly_count)
+    chips = Mesh(grid, ("z", "core", "uly"))
     placed = (
-        P(None, "ctx", "uly"),
-        P(None, "ctx", "uly"),
-        P(None, "ctx", "uly"),
-        P(None, ("ctx", "uly"), None),
-        P(None, "uly", "ctx"),
+        P(None, ("z", "core"), "uly"),
+        P(None, ("z", "core"), "uly"),
+        P(None, ("z", "core"), "uly"),
+        P(None, ("z", "core", "uly"), None),
+        P(None, "uly", ("z", "core")),
     )
     return jax.shard_map(
         local,
-        mesh=mesh,
+        mesh=chips,
         in_specs=placed,
         out_specs=(
-            P(None, ("ctx", "uly"), None),
-            P(None, ("ctx", "uly"), None),
-            P(None, ("ctx", "uly"), None),
-            P(None, ("ctx", "uly"), None),
+            P(None, ("z", "core", "uly"), None),
+            P(None, ("z", "core", "uly"), None),
+            P(None, ("z", "core", "uly"), None),
+            P(None, ("z", "core", "uly"), None),
         ),
         check_vma=False,
     )

time: 128 us -> 124 us (0.969)
  the two profiles are of different devices: /device:TPU:8 before, /device:TPU:32 now
where the time goes in v4:
time: 124 us; the launch traced here: 123 us
  waiting for transfers between devices  41.6 us (34%)
  starting transfers between devices  36.8 us (30%)
  blocking collectives  21.2 us (17%)
  local copies, waits for them, and re-layouts  14.4 us (12%)
  matrix products  5.55 us (4%)
  other arithmetic  2.08 us (2%)
    all_to_all x1, blocking collectives, local(): outs = lax.all_to_all(outs, 'uly', 0, 0, tiled=True)  21.2 us
    all_to_all x1, waiting for transfers between devices, local(): got = lax.all_to_all(send, 'z', 0, 0, tiled=True)  19.1 us
    all_to_all x1, waiting for transfers between devices, local(): back = lax.all_to_all(mixed, 'z', 0, 0, tiled=True)  16.6 us
    all_to_all x1, starting transfers between devices, local(): got = lax.all_to_all(send, 'z', 0, 0, tiled=True)  15.2 us
    all_to_all x1, starting transfers between devices, local(): g_parts = lax.all_to_all(g_parts, 'uly', 0, 0, tiled=True)  7.03 us
    all_to_all x1, starting transfers between devices, local(): back = lax.all_to_all(mixed, 'z', 0, 0, tiled=True)  6.68 us
    ppermute x3, starting transfers between devices, local(): lax.ppermute((update, local_grad, last), 'core', pairs)  5.97 us
    all_to_all x1, waiting for transfers between devices, local(): g_parts = lax.all_to_all(g_parts, 'uly', 0, 0, tiled=True)  4.56 us
  transfers between devices with their start and end apart: 7, of which 4 were waited for; matrix products, arithmetic and copies ran while one was open for 5% of the time, Pallas kernels for 0%

profile of v4, /device:TPU:32, one launch (start us, length us, event | category | flops | bytes accessed | tf_op | source)
XLA Modules:
  0.0 122.8 jit_solution(10180312966543719545)
XLA Ops:
  0.6 0.7 reshape.416
  1.3 1.2 reduce-window.6
  2.6 0.1 copy.301
  2.8 0.1 copy.239
  3.0 1.9 %collective-permute-start = (f32[1,4]{1,0:T(1,128)S(1)}, f32[1,4]{1,0:T(1,128)S(1)}, u32[]{:S(2)}, u32[]{:S(2)}) collective-permute-start(f32[1,4]{1,0:T(1,128)S(1)} %get-tuple-element.22), channel_id=1, source_target_pairs={{0,16},{16,0},{1,17},{17,1},{2,18},{18,2},{3,19},{19,3},{4,20},{20... | collective-permute-start | bytes 56 | tf_op jit(solution)/shard_map/ppermute | solution.py:89
  5.0 0.9 copy.248
  5.9 7.0 %all-to-all-start = ((bf16[16,1,16,512]{3,2,1,0:T(8,128)(2,1)}), bf16[16,1,16,512]{3,2,1,0:T(8,128)(2,1)S(1)}, u32[]{:S(2)}, u32[]{:S(2)}) async-start(bf16[16,1,16,512]{3,2,1,0:T(8,128)(2,1)} %copy.248), calls=%async_computation | async-start | bytes 524288 | tf_op jit(solution)/shard_map/all_to_all | solution.py:71
  13.0 0.8 copy-done.6
  13.9 0.9 copy-done.7
  14.8 0.1 copy.304
  15.0 0.2 convolution_bitcast_fusion.8
  15.2 2.1 %collective-permute-start.1 = (f32[1,4,128,128]{3,2,1,0:T(8,128)S(1)}, f32[1,4,128,128]{3,2,1,0:T(8,128)S(1)}, u32[]{:S(2)}, u32[]{:S(2)}) collective-permute-start(f32[1,4,128,128]{3,2,1,0:T(8,128)S(1)} %convolution_bitcast_fusion.8), channel_id=1, source_target_pairs={{0,16},{16,0},{1,17},{17,1},{2,18},{18,2},{3,19},{19,3},{4,20},{20... | collective-permute-start | bytes 786440 | tf_op jit(solution)/shard_map/ppermute | solution.py:89
  17.5 4.6 %all-to-all-done = bf16[16,1,16,512]{3,2,1,0:T(8,128)(2,1)S(1)} async-done(((bf16[16,1,16,512]{3,2,1,0:T(8,128)(2,1)}), bf16[16,1,16,512]{3,2,1,0:T(8,128)(2,1)S(1)}, u32[]{:S(2)}, u32[]{:S(2)}) %all-to-all-start) | async-done | bytes 262176 | tf_op jit(solution)/shard_map/all_to_all | solution.py:71
  22.1 0.5 convolution_bitcast_fusion.7
  22.6 1.9 %collective-permute-start.2 = (f32[1,4,128,128]{3,2,1,0:T(8,128)S(1)}, f32[1,4,128,128]{3,2,1,0:T(8,128)S(1)}, u32[]{:S(2)}, u32[]{:S(2)}) collective-permute-start(f32[1,4,128,128]{3,2,1,0:T(8,128)S(1)} %convolution_bitcast_fusion.7), channel_id=1, source_target_pairs={{0,16},{16,0},{1,17},{17,1},{2,18},{18,2},{3,19},{19,3},{4,20},{20... | collective-permute-start | bytes 786440 | tf_op jit(solution)/shard_map/ppermute | solution.py:89
  24.6 0.1 fusion.31
  24.7 1.4 %collective-permute-done.2 = f32[1,4,128,128]{3,2,1,0:T(8,128)S(1)} collective-permute-done((f32[1,4,128,128]{3,2,1,0:T(8,128)S(1)}, f32[1,4,128,128]{3,2,1,0:T(8,128)S(1)}, u32[]{:S(2)}, u32[]{:S(2)}) %collective-permute-start.2) | collective-permute-done | bytes 262176 | tf_op jit(solution)/shard_map/ppermute | solution.py:89
  26.1 0.1 fusion.30
  26.2 0.6 copy-done.1
  26.9 0.1 pad_maximum_fusion
  27.0 0.9 copy.251
  27.9 15.2 %all-to-all-start.1 = ((f32[16,1,4,9,128]{4,2,3,1,0:T(4,128)}), f32[16,1,4,9,128]{4,2,3,1,0:T(4,128)S(1)}, u32[]{:S(2)}, u32[]{:S(2)}) async-start(f32[16,1,4,9,128]{4,2,3,1,0:T(4,128)} %copy.251), calls=%async_computation.1 | async-start | bytes 589824 | tf_op jit(solution)/shard_map/all_to_all | solution.py:115
  43.2 19.1 %all-to-all-done.1 = f32[16,1,4,9,128]{4,2,3,1,0:T(4,128)S(1)} async-done(((f32[16,1,4,9,128]{4,2,3,1,0:T(4,128)}), f32[16,1,4,9,128]{4,2,3,1,0:T(4,128)S(1)}, u32[]{:S(2)}, u32[]{:S(2)}) %all-to-all-start.1) | async-done | bytes 294944 | tf_op jit(solution)/shard_map/all_to_all | solution.py:115
  62.3 0.1 copy.253
  62.4 0.1 copy.254
  62.7 0.3 convolution_bitcast_fusion.9
  63.0 0.3 convolution_bitcast_fusion.10
  63.4 0.8 copy.259
  64.2 6.7 %all-to-all-start.2 = ((f32[16,2,1,4,4,128]{5,4,3,2,1,0:T(4,128)}), f32[16,2,1,4,4,128]{5,4,3,2,1,0:T(4,128)S(1)}, u32[]{:S(2)}, u32[]{:S(2)}) async-start(f32[16,2,1,4,4,128]{5,4,3,2,1,0:T(4,128)} %copy.259), calls=%async_computation.2 | async-start | bytes 524288 | tf_op jit(solution)/shard_map/all_to_all | solution.py:124
  70.9 0.4 fusion
  71.3 0.3 convolution_bitcast_fusion.6
  71.6 0.3 convolution_bitcast_fusion.1
  72.0 0.4 fusion.1
  72.4 16.6 %all-to-all-done.2 = f32[16,2,1,4,4,128]{5,4,3,2,1,0:T(4,128)S(1)} async-done(((f32[16,2,1,4,4,128]{5,4,3,2,1,0:T(4,128)}), f32[16,2,1,4,4,128]{5,4,3,2,1,0:T(4,128)S(1)}, u32[]{:S(2)}, u32[]{:S(2)}) %all-to-all-start.2) | async-done | bytes 262176 | tf_op jit(solution)/shard_map/all_to_all | solution.py:124
  89.1 1.9 %collective-permute-start.3 = (f32[2,1,4,64,128]{4,3,2,1,0:T(8,128)S(1)}, f32[2,1,4,64,128]{4,3,2,1,0:T(8,128)S(1)}, u32[]{:S(2)}, u32[]{:S(2)}) collective-permute-start(f32[2,1,4,64,128]{4,3,2,1,0:T(8,128)S(1)} %pad_maximum_fusion.3), channel_id=1, source_target_pairs={{0,16},{16,0},{1,17},{17,1},{2,18},{18,2},{3,19},{19,3},{4,20},{20... | collective-permute-start | bytes 786440 | tf_op jit(solution)/shard_map/ppermute | solution.py:126
  91.0 0.3 convolution_bitcast_fusion.3
  91.4 1.3 %convolution_bitcast_fusion.5 = f32[1,256,4,128]{3,1,2,0:T(8,128)S(1)} fusion(bf16[4,256,256]{2,1,0:T(8,128)(2,1)} %copy-done, bf16[256,4,128]{0,2,1:T(8,128)(2,1)S(1)} %bitcast.197), kind=kOutput, calls=%fused_computation.9 | convolution fusion | flops 67108864 | bytes 1310720 | tf_op jit(solution)/shard_map/bhij,bjhd->bihd/dot_general | solution.py:142
  92.8 0.9 copy-done.2
  93.7 0.1 select_convert_fusion.1
  93.8 0.3 fusion.8
  94.1 0.3 copy-done.3
  94.5 0.2 copy.283
  94.7 0.1 stack.34
  94.8 0.3 fusion.12
  95.1 0.2 copy.264
  95.3 0.1 stack.31
  95.4 0.8 copy-done.4
  96.2 0.2 fusion.9
  96.5 0.2 fusion.10
  96.7 0.2 copy.271
  96.9 0.1 stack.32
  97.0 0.2 copy.277
  97.3 0.1 stack.33
  97.4 0.1 maximum_bitcast_fusion
  97.5 0.1 copy.284
  97.6 21.2 %all_to_all.20 = bf16[16,4,1,16,512]{4,3,2,1,0:T(8,128)(2,1)S(1)} all-to-all(bf16[16,4,1,16,512]{4,3,2,1,0:T(8,128)(2,1)S(1)} %copy.284), channel_id=1, replica_groups=mesh['z'=16,'core'=2,'uly'=16] {'uly'}, dimensions={0} | all-to-all | bytes 2097152 | tf_op jit(solution)/shard_map/all_to_all | solution.py:164
  118.9 0.2 copy.288
  119.0 0.8 squeeze.41
  119.9 0.1 copy.287
  120.0 0.8 squeeze.40
  120.9 0.1 copy.286
  121.0 0.8 squeeze.39
  121.8 0.1 copy.285
  122.0 0.8 squeeze.38
  (51 shorter events, 1.4 us)
Async XLA Ops:
  2.6 2.3 %copy-start.5 = (bf16[1,16,8192]{2,1,0:T(8,128)(2,1)S(1)}, bf16[1,16,8192]{2,1,0:T(8,128)(2,1)}, u32[]{:S(2)}) copy-start(bf16[1,16,8192]{2,1,0:T(8,128)(2,1)} %param.8) | copy-start | bytes 786436
  3.0 14.5 %collective-permute-start = (f32[1,4]{1,0:T(1,128)S(1)}, f32[1,4]{1,0:T(1,128)S(1)}, u32[]{:S(2)}, u32[]{:S(2)}) collective-permute-start(f32[1,4]{1,0:T(1,128)S(1)} %get-tuple-element.22), channel_id=1, source_target_pairs={{0,16},{16,0},{1,17},{17,1},{2,18},{18,2},{3,19},{19,3},{4,20},{20... | collective-permute-start | bytes 56 | tf_op jit(solution)/shard_map/ppermute | solution.py:89
  5.9 16.2 %all-to-all-start = ((bf16[16,1,16,512]{3,2,1,0:T(8,128)(2,1)}), bf16[16,1,16,512]{3,2,1,0:T(8,128)(2,1)S(1)}, u32[]{:S(2)}, u32[]{:S(2)}) async-start(bf16[16,1,16,512]{3,2,1,0:T(8,128)(2,1)} %copy.248), calls=%async_computation | async-start | bytes 524288 | tf_op jit(solution)/shard_map/all_to_all | solution.py:71
  12.9 1.0 copy-start.6
  13.9 0.9 copy-start.7
  14.9 2.4 %copy-start.8 = (bf16[1,256,512]{2,1,0:T(8,128)(2,1)S(1)}, bf16[1,256,512]{2,1,0:T(8,128)(2,1)}, u32[]{:S(2)}) copy-start(bf16[1,256,512]{2,1,0:T(8,128)(2,1)} %param.5) | copy-start | bytes 786436
  15.2 9.4 %collective-permute-start.1 = (f32[1,4,128,128]{3,2,1,0:T(8,128)S(1)}, f32[1,4,128,128]{3,2,1,0:T(8,128)S(1)}, u32[]{:S(2)}, u32[]{:S(2)}) collective-permute-start(f32[1,4,128,128]{3,2,1,0:T(8,128)S(1)} %convolution_bitcast_fusion.8), channel_id=1, source_target_pairs={{0,16},{16,0},{1,17},{17,1},{2,18},{18,2},{3,19},{19,3},{4,20},{20... | collective-permute-start | bytes 786440 | tf_op jit(solution)/shard_map/ppermute | solution.py:89
  22.6 3.4 %collective-permute-start.2 = (f32[1,4,128,128]{3,2,1,0:T(8,128)S(1)}, f32[1,4,128,128]{3,2,1,0:T(8,128)S(1)}, u32[]{:S(2)}, u32[]{:S(2)}) collective-permute-start(f32[1,4,128,128]{3,2,1,0:T(8,128)S(1)} %convolution_bitcast_fusion.7), channel_id=1, source_target_pairs={{0,16},{16,0},{1,17},{17,1},{2,18},{18,2},{3,19},{19,3},{4,20},{20... | collective-permute-start | bytes 786440 | tf_op jit(solution)/shard_map/ppermute | solution.py:89
  26.1 0.7 copy-start.1
  27.9 34.4 %all-to-all-start.1 = ((f32[16,1,4,9,128]{4,2,3,1,0:T(4,128)}), f32[16,1,4,9,128]{4,2,3,1,0:T(4,128)S(1)}, u32[]{:S(2)}, u32[]{:S(2)}) async-start(f32[16,1,4,9,128]{4,2,3,1,0:T(4,128)} %copy.251), calls=%async_computation.1 | async-start | bytes 589824 | tf_op jit(solution)/shard_map/all_to_all | solution.py:115
  64.2 24.8 %all-to-all-start.2 = ((f32[16,2,1,4,4,128]{5,4,3,2,1,0:T(4,128)}), f32[16,2,1,4,4,128]{5,4,3,2,1,0:T(4,128)S(1)}, u32[]{:S(2)}, u32[]{:S(2)}) async-start(f32[16,2,1,4,4,128]{5,4,3,2,1,0:T(4,128)} %copy.259), calls=%async_computation.2 | async-start | bytes 524288 | tf_op jit(solution)/shard_map/all_to_all | solution.py:124
  72.4 18.6 %copy-start = (bf16[4,256,256]{2,1,0:T(8,128)(2,1)}, bf16[4,256,256]{2,1,0:T(8,128)(2,1)S(1)}, u32[]{:S(2)}) copy-start(bf16[4,256,256]{2,1,0:T(8,128)(2,1)S(1)} %fusion.1) | copy-start | bytes 1572868
  89.1 3.6 %collective-permute-start.3 = (f32[2,1,4,64,128]{4,3,2,1,0:T(8,128)S(1)}, f32[2,1,4,64,128]{4,3,2,1,0:T(8,128)S(1)}, u32[]{:S(2)}, u32[]{:S(2)}) collective-permute-start(f32[2,1,4,64,128]{4,3,2,1,0:T(8,128)S(1)} %pad_maximum_fusion.3), channel_id=1, source_target_pairs={{0,16},{16,0},{1,17},{17,1},{2,18},{18,2},{3,19},{19,3},{4,20},{20... | collective-permute-start | bytes 786440 | tf_op jit(solution)/shard_map/ppermute | solution.py:126
  92.7 1.0 copy-start.2
  93.8 0.7 copy-start.3
  95.3 0.9 copy-start.4

commit v5 on v4

--- a/solution.py
+++ b/solution.py
@@ -104,16 +104,18 @@
     def my_half(state):
         return lax.dynamic_slice_in_dim(state, core * half, half, axis=2)
 
-    chip_last = jnp.broadcast_to((last_lo + last_hi)[..., None], (batch_count, head_count, width))
-    last_piece = jnp.broadcast_to(
-        chip_last[None, :, :, None, :], (chip_count, batch_count, head_count, 1, width)
+    chip_last = (last_lo + last_hi).reshape(1, batch_count * head_count)
+    chip_last = jnp.pad(chip_last, ((0, 0), (0, width - batch_count * head_count)))
+    last_piece = jnp.broadcast_to(chip_last, (chip_count, width))
+    sent = jnp.concatenate(
+        [to_pieces(my_half(chip_update), chip_count), to_pieces(my_half(chip_grad), chip_count)], axis=3
     )
-    send = jnp.concatenate(
-        [to_pieces(my_half(chip_update), chip_count), to_pieces(my_half(chip_grad), chip_count), last_piece],
-        axis=3,
-    )
+    piece_shape = sent.shape
+    send = jnp.concatenate([sent.reshape(chip_count, -1), last_piece], axis=1)
     got = lax.all_to_all(send, "z", 0, 0, tiled=True)
-    forward_w, backward_w = block_weights(got[:, :, :, 2 * band, 0])
+    got_last = got[:, -width:][:, : batch_count * head_count].reshape(chip_count, batch_count, head_count)
+    got = got[:, :-width].reshape(piece_shape)
+    forward_w, backward_w = block_weights(got_last)
     mixed = jnp.stack(
         [
             mix_blocks(forward_w, got[:, :, :, :band]),
@@ -162,10 +164,13 @@
     outs = outs.reshape(4, batch_count, uly_count, positions // uly_count, width_heads)
     outs = jnp.transpose(outs, (2, 0, 1, 3, 4))
     outs = lax.all_to_all(outs, "uly", 0, 0, tiled=True)
-    outs = jnp.transpose(outs, (1, 2, 3, 0, 4)).reshape(
-        4, batch_count, positions // uly_count, uly_count * width_heads
-    )
-    return (outs[0], outs[1], outs[2], outs[3])
+
+    def to_tokens(index):
+        return jnp.transpose(outs[:, index], (1, 2, 0, 3)).reshape(
+            batch_count, positions // uly_count, uly_count * width_heads
+        )
+
+    return (to_tokens(0), to_tokens(1), to_tokens(2), to_tokens(3))
 
 
 def solution(mesh):

time: 124 us -> 131 us (1.056)
  matrix products: 5.55 us -> 9.44 us
  waiting for transfers between devices: 41.6 us -> 44.1 us
    all_to_all x1, waiting for transfers between devices: 4.56 us -> 8.46 us  [local(): g_parts = lax.all_to_all(g_parts, 'uly', 0, 0, tiled=True)]
    dot_general x2, matrix products: 0.64 us -> 4.5 us  [mix_blocks(): jnp.einsum('bhcd,dbhrx->cbhrx', weights, pieces, precision=lax.Precision....]
    unnamed x19 -> x18, local copies, waits for them, and re-layouts: 4.43 us -> 0.99 us
    squeeze x5 -> x0, local copies, waits for them, and re-layouts: 3.39 us -> none  [the longest x4 3.31 us: local(): return (outs[0], outs[1], outs[2], outs[3])]
    reshape x1 -> x8, local copies, waits for them, and re-layouts: 0.7 us -> 3.76 us  [the longest x4 2.88 us: to_tokens(): jnp.transpose(outs[:, index], (1, 2, 0, 3))]
    all_to_all x0 -> x2, local copies, waits for them, and re-layouts: none -> 2.9 us  [local(): got = lax.all_to_all(send, 'z', 0, 0, tiled=True)]
    another operation x12, local copies, waits for them, and re-layouts: 1.26 us -> 3.17 us
  transfers between devices with their start and end apart: 7 -> 7, of which waited for: 4 -> 4; matrix products, arithmetic and copies ran while one was open for 5% -> 4% of each run, Pallas kernels for 0% -> 0%
where the time goes in v5:
time: 131 us
  waiting for transfers between devices  44.1 us (34%)
  starting transfers between devices  36.9 us (28%)
  blocking collectives  21.2 us (16%)
  local copies, waits for them, and re-layouts  15.2 us (12%)
  matrix products  9.44 us (7%)
  other arithmetic  2.69 us (2%)
    all_to_all x1, blocking collectives, local(): outs = lax.all_to_all(outs, 'uly', 0, 0, tiled=True)  21.2 us
    all_to_all x1, waiting for transfers between devices, local(): got = lax.all_to_all(send, 'z', 0, 0, tiled=True)  18.4 us
    all_to_all x1, waiting for transfers between devices, local(): back = lax.all_to_all(mixed, 'z', 0, 0, tiled=True)  15.8 us
    all_to_all x1, starting transfers between devices, local(): got = lax.all_to_all(send, 'z', 0, 0, tiled=True)  15.2 us
    all_to_all x1, waiting for transfers between devices, local(): g_parts = lax.all_to_all(g_parts, 'uly', 0, 0, tiled=True)  8.46 us
    all_to_all x1, starting transfers between devices, local(): g_parts = lax.all_to_all(g_parts, 'uly', 0, 0, tiled=True)  7.04 us
    all_to_all x1, starting transfers between devices, local(): back = lax.all_to_all(mixed, 'z', 0, 0, tiled=True)  6.33 us
    ppermute x3, starting transfers between devices, local(): lax.ppermute((update, local_grad, last), 'core', pairs)  6.25 us
  transfers between devices with their start and end apart: 7, of which 4 were waited for; matrix products, arithmetic and copies ran while one was open for 4% of the time, Pallas kernels for 0%

profile of v5, /device:TPU:32, one launch (start us, length us, event | category | flops | bytes accessed | tf_op | source)
XLA Modules:
  0.0 130.7 jit_solution(729097763140827321)
XLA Ops:
  0.6 0.7 reshape.415
  1.4 1.2 reduce-window.6
  2.6 0.1 slice.64
  2.7 0.1 copy.253
  2.8 0.1 copy.190
  3.1 0.1 copy.194
  3.1 1.1 copy.259
  4.2 1.0 reshape.420
  5.2 0.2 convolution_bitcast_fusion.8
  5.5 1.9 %collective-permute-start.1 = (f32[1,4,128,128]{3,2,1,0:T(8,128)S(1)}, f32[1,4,128,128]{3,2,1,0:T(8,128)S(1)}, u32[]{:S(2)}, u32[]{:S(2)}) collective-permute-start(f32[1,4,128,128]{3,2,1,0:T(8,128)S(1)} %convolution_bitcast_fusion.8), channel_id=1, source_target_pairs={{0,16},{16,0},{1,17},{17,1},{2,18},{18,2},{3,19},{19,3},{4,20},{20... | collective-permute-start | bytes 786440 | tf_op jit(solution)/shard_map/ppermute | solution.py:89
  7.4 2.4 %collective-permute-start = (f32[1,4]{1,0:T(1,128)S(1)}, f32[1,4]{1,0:T(1,128)S(1)}, u32[]{:S(2)}, u32[]{:S(2)}) collective-permute-start(f32[1,4]{1,0:T(1,128)S(1)} %get-tuple-element.20), channel_id=1, source_target_pairs={{0,16},{16,0},{1,17},{17,1},{2,18},{18,2},{3,19},{19,3},{4,20},{20... | collective-permute-start | bytes 56 | tf_op jit(solution)/shard_map/ppermute | solution.py:89
  9.8 0.1 copy.265
  9.9 0.9 copy.199
  10.8 7.0 %all-to-all-start = ((bf16[16,1,16,512]{3,2,1,0:T(8,128)(2,1)}), bf16[16,1,16,512]{3,2,1,0:T(8,128)(2,1)S(1)}, u32[]{:S(2)}, u32[]{:S(2)}) async-start(bf16[16,1,16,512]{3,2,1,0:T(8,128)(2,1)} %copy.199), calls=%async_computation | async-start | bytes 524288 | tf_op jit(solution)/shard_map/all_to_all | solution.py:71
  17.8 0.1 copy.197
  17.9 0.1 reshape.413
  18.0 8.5 %all-to-all-done = bf16[16,1,16,512]{3,2,1,0:T(8,128)(2,1)S(1)} async-done(((bf16[16,1,16,512]{3,2,1,0:T(8,128)(2,1)}), bf16[16,1,16,512]{3,2,1,0:T(8,128)(2,1)S(1)}, u32[]{:S(2)}, u32[]{:S(2)}) %all-to-all-start) | async-done | bytes 262176 | tf_op jit(solution)/shard_map/all_to_all | solution.py:71
  26.6 0.5 convolution_bitcast_fusion.7
  27.1 1.9 %collective-permute-start.2 = (f32[1,4,128,128]{3,2,1,0:T(8,128)S(1)}, f32[1,4,128,128]{3,2,1,0:T(8,128)S(1)}, u32[]{:S(2)}, u32[]{:S(2)}) collective-permute-start(f32[1,4,128,128]{3,2,1,0:T(8,128)S(1)} %convolution_bitcast_fusion.7), channel_id=1, source_target_pairs={{0,16},{16,0},{1,17},{17,1},{2,18},{18,2},{3,19},{19,3},{4,20},{20... | collective-permute-start | bytes 786440 | tf_op jit(solution)/shard_map/ppermute | solution.py:89
  29.1 0.1 fusion.31
  29.2 1.4 %collective-permute-done.2 = f32[1,4,128,128]{3,2,1,0:T(8,128)S(1)} collective-permute-done((f32[1,4,128,128]{3,2,1,0:T(8,128)S(1)}, f32[1,4,128,128]{3,2,1,0:T(8,128)S(1)}, u32[]{:S(2)}, u32[]{:S(2)}) %collective-permute-start.2) | collective-permute-done | bytes 262176 | tf_op jit(solution)/shard_map/ppermute | solution.py:89
  30.6 0.1 fusion.30
  30.8 1.0 copy.203
  31.8 15.2 %all-to-all-start.1 = ((f32[16,1,4224]{2,1,0:T(1,128)}), f32[16,1,4224]{2,1,0:T(1,128)}, u32[]{:S(2)}, u32[]{:S(2)}) async-start(f32[16,1,4224]{2,1,0:T(1,128)} %copy.203), calls=%async_computation.1 | async-start | bytes 540672 | tf_op jit(solution)/shard_map/all_to_all | solution.py:115
  47.2 18.4 %all-to-all-done.1 = f32[16,1,4224]{2,1,0:T(1,128)} async-done(((f32[16,1,4224]{2,1,0:T(1,128)}), f32[16,1,4224]{2,1,0:T(1,128)}, u32[]{:S(2)}, u32[]{:S(2)}) %all-to-all-start.1) | async-done | bytes 270368 | tf_op jit(solution)/shard_map/all_to_all | solution.py:115
  65.6 1.9 %copy.204 = f32[16,1,4224]{0,2,1:T(8,128)S(1)} copy(f32[16,1,4224]{2,1,0:T(1,128)} %all-to-all-done.1) | data formatting | bytes 540672 | tf_op jit(solution)/shard_map/all_to_all | solution.py:115
  67.6 1.5 %slice.66 = f32[16,4096]{0,1:T(8,128)} slice(f32[16,4224]{0,1:T(8,128)S(1)} %bitcast.229), slice={[0:16], [0:4096]} | slice | bytes 524288 | tf_op jit(solution)/shard_map/slice | solution.py:117
  69.0 0.1 copy.207
  69.1 0.1 copy.208
  69.2 0.1 copy.209
  69.3 2.2 %convolution_bitcast_fusion.10 = f32[16,1,1,4,4,128]{5,0,4,3,2,1:T(8,128)S(1)} fusion(f32[16,1,4,8,128]{0,4,3,2,1:T(8,128)} %bitcast.231, f32[4,16]{1,0:T(4,128)S(1)} %bitcast.251, f32[4,16]{1,0:T(4,128)S(1)} %fusion.52, pred[16,16]{1,0:T(8,128)(4,1)S(1)} %iota_compare_fusion.2), kind=kOutput, calls=%fused_computation.26 | convolution fusion | flops 6294528 | bytes 1180416 | tf_op jit(solution)/shard_map/bhcd,dbhrx->cbhrx/dot_general | solution.py:52
  71.5 2.3 %convolution_bitcast_fusion.9 = f32[16,1,1,4,4,128]{5,0,4,3,2,1:T(8,128)S(1)} fusion(f32[16,1,4,8,128]{0,4,3,2,1:T(8,128)} %bitcast.232, f32[4,16]{1,0:T(4,128)S(1)} %bitcast.252, f32[4,16]{1,0:T(4,128)S(1)} %fusion.52, pred[16,16]{1,0:T(8,128)(4,1)S(1)} %iota_compare_fusion.1), kind=kOutput, calls=%fused_computation.25 | convolution fusion | flops 6294528 | bytes 1180416 | tf_op jit(solution)/shard_map/bhcd,dbhrx->cbhrx/dot_general | solution.py:52
  73.8 0.8 copy.211
  74.6 6.3 %all-to-all-start.2 = ((f32[16,2,1,4,4,128]{5,4,3,2,1,0:T(4,128)}), f32[16,2,1,4,4,128]{5,4,3,2,1,0:T(4,128)S(1)}, u32[]{:S(2)}, u32[]{:S(2)}) async-start(f32[16,2,1,4,4,128]{5,4,3,2,1,0:T(4,128)} %copy.211), calls=%async_computation.2 | async-start | bytes 524288 | tf_op jit(solution)/shard_map/all_to_all | solution.py:126
  81.0 0.4 fusion
  81.4 0.3 convolution_bitcast_fusion.6
  81.7 0.4 fusion.1
  82.1 0.8 copy-done.2
  82.9 0.3 convolution_bitcast_fusion.5
  83.2 15.8 %all-to-all-done.2 = f32[16,2,1,4,4,128]{5,4,3,2,1,0:T(4,128)S(1)} async-done(((f32[16,2,1,4,4,128]{5,4,3,2,1,0:T(4,128)}), f32[16,2,1,4,4,128]{5,4,3,2,1,0:T(4,128)S(1)}, u32[]{:S(2)}, u32[]{:S(2)}) %all-to-all-start.2) | async-done | bytes 262176 | tf_op jit(solution)/shard_map/all_to_all | solution.py:126
  99.2 2.1 %collective-permute-start.3 = (f32[2,1,4,64,128]{4,3,2,1,0:T(8,128)S(1)}, f32[2,1,4,64,128]{4,3,2,1,0:T(8,128)S(1)}, u32[]{:S(2)}, u32[]{:S(2)}) collective-permute-start(f32[2,1,4,64,128]{4,3,2,1,0:T(8,128)S(1)} %pad_maximum_fusion.3), channel_id=1, source_target_pairs={{0,16},{16,0},{1,17},{17,1},{2,18},{18,2},{3,19},{19,3},{4,20},{20... | collective-permute-start | bytes 786440 | tf_op jit(solution)/shard_map/ppermute | solution.py:128
  101.2 1.4 %convolution_bitcast_fusion.3 = f32[1,256,4,128]{3,1,2,0:T(8,128)S(1)} fusion(bf16[4,256,256]{2,1,0:T(8,128)(2,1)} %copy-done.2, bf16[256,4,128]{2,1,0:T(4,128)(2,1)S(1)} %reshape.413), kind=kOutput, calls=%fused_computation.7 | convolution fusion | flops 67108864 | bytes 1310720 | tf_op jit(solution)/shard_map/bhij,bihd->bjhd/dot_general | solution.py:150
  102.6 0.3 convolution_bitcast_fusion.1
  103.0 0.8 select_convert_fusion.1
  103.8 0.2 fusion.10
  104.1 0.2 copy.223
  104.3 0.1 stack.32
  104.4 0.3 fusion.12
  104.7 0.2 copy.216
  104.9 0.1 stack.31
  105.0 0.2 fusion.9
  105.3 0.2 copy.229
  105.5 0.1 stack.33
  105.6 0.3 fusion.8
  105.9 0.2 copy.235
  106.1 0.1 stack.34
  106.3 0.1 maximum_bitcast_fusion
  106.4 0.1 copy.236
  106.5 21.2 %all_to_all.27 = bf16[16,4,1,16,512]{4,3,2,1,0:T(8,128)(2,1)S(1)} all-to-all(bf16[16,4,1,16,512]{4,3,2,1,0:T(8,128)(2,1)S(1)} %copy.236), channel_id=1, replica_groups=mesh['z'=16,'core'=2,'uly'=16] {'uly'}, dimensions={0} | all-to-all | bytes 2097152 | tf_op jit(solution)/shard_map/all_to_all | solution.py:166
  127.7 0.1 slice_bitcast_fusion.4
  127.8 0.7 copy.260
  128.5 0.7 copy.261
  129.2 0.7 copy.262
  129.9 0.7 copy.263
  (49 shorter events, 0.8 us)
Async XLA Ops:
  0.6 9.2 %copy-start.6 = (bf16[1,16,8192]{2,1,0:T(8,128)(2,1)S(1)}, bf16[1,16,8192]{2,1,0:T(8,128)(2,1)}, u32[]{:S(2)}) copy-start(bf16[1,16,8192]{2,1,0:T(8,128)(2,1)} %param.8) | copy-start | bytes 786436
  3.0 14.9 %copy-start.7 = (bf16[1,256,512]{2,1,0:T(8,128)(2,1)S(1)}, bf16[1,256,512]{2,1,0:T(8,128)(2,1)}, u32[]{:S(2)}) copy-start(bf16[1,256,512]{2,1,0:T(8,128)(2,1)} %param.5) | copy-start | bytes 786436
  5.5 23.5 %collective-permute-start.1 = (f32[1,4,128,128]{3,2,1,0:T(8,128)S(1)}, f32[1,4,128,128]{3,2,1,0:T(8,128)S(1)}, u32[]{:S(2)}, u32[]{:S(2)}) collective-permute-start(f32[1,4,128,128]{3,2,1,0:T(8,128)S(1)} %convolution_bitcast_fusion.8), channel_id=1, source_target_pairs={{0,16},{16,0},{1,17},{17,1},{2,18},{18,2},{3,19},{19,3},{4,20},{20... | collective-permute-start | bytes 786440 | tf_op jit(solution)/shard_map/ppermute | solution.py:89
  7.4 10.6 %collective-permute-start = (f32[1,4]{1,0:T(1,128)S(1)}, f32[1,4]{1,0:T(1,128)S(1)}, u32[]{:S(2)}, u32[]{:S(2)}) collective-permute-start(f32[1,4]{1,0:T(1,128)S(1)} %get-tuple-element.20), channel_id=1, source_target_pairs={{0,16},{16,0},{1,17},{17,1},{2,18},{18,2},{3,19},{19,3},{4,20},{20... | collective-permute-start | bytes 56 | tf_op jit(solution)/shard_map/ppermute | solution.py:89
  10.8 15.7 %all-to-all-start = ((bf16[16,1,16,512]{3,2,1,0:T(8,128)(2,1)}), bf16[16,1,16,512]{3,2,1,0:T(8,128)(2,1)S(1)}, u32[]{:S(2)}, u32[]{:S(2)}) async-start(bf16[16,1,16,512]{3,2,1,0:T(8,128)(2,1)} %copy.199), calls=%async_computation | async-start | bytes 524288 | tf_op jit(solution)/shard_map/all_to_all | solution.py:71
  27.1 3.4 %collective-permute-start.2 = (f32[1,4,128,128]{3,2,1,0:T(8,128)S(1)}, f32[1,4,128,128]{3,2,1,0:T(8,128)S(1)}, u32[]{:S(2)}, u32[]{:S(2)}) collective-permute-start(f32[1,4,128,128]{3,2,1,0:T(8,128)S(1)} %convolution_bitcast_fusion.7), channel_id=1, source_target_pairs={{0,16},{16,0},{1,17},{17,1},{2,18},{18,2},{3,19},{19,3},{4,20},{20... | collective-permute-start | bytes 786440 | tf_op jit(solution)/shard_map/ppermute | solution.py:89
  30.5 16.6 %copy-start.3 = (f32[1,4,128,128]{3,2,1,0:T(8,128)}, f32[1,4,128,128]{3,2,1,0:T(8,128)S(1)}, u32[]{:S(2)}) copy-start(f32[1,4,128,128]{3,2,1,0:T(8,128)S(1)} %broadcast_select_fusion.2) | copy-start | bytes 786436
  31.8 33.8 %all-to-all-start.1 = ((f32[16,1,4224]{2,1,0:T(1,128)}), f32[16,1,4224]{2,1,0:T(1,128)}, u32[]{:S(2)}, u32[]{:S(2)}) async-start(f32[16,1,4224]{2,1,0:T(1,128)} %copy.203), calls=%async_computation.1 | async-start | bytes 540672 | tf_op jit(solution)/shard_map/all_to_all | solution.py:115
  74.6 24.4 %all-to-all-start.2 = ((f32[16,2,1,4,4,128]{5,4,3,2,1,0:T(4,128)}), f32[16,2,1,4,4,128]{5,4,3,2,1,0:T(4,128)S(1)}, u32[]{:S(2)}, u32[]{:S(2)}) async-start(f32[16,2,1,4,4,128]{5,4,3,2,1,0:T(4,128)} %copy.211), calls=%async_computation.2 | async-start | bytes 524288 | tf_op jit(solution)/shard_map/all_to_all | solution.py:126
  81.4 1.8 %copy-start = (bf16[4,256,256]{2,1,0:T(8,128)(2,1)}, bf16[4,256,256]{2,1,0:T(8,128)(2,1)S(1)}, u32[]{:S(2)}) copy-start(bf16[4,256,256]{2,1,0:T(8,128)(2,1)S(1)} %fusion) | copy-start | bytes 1572868
  82.1 0.8 copy-start.2
  99.0 3.6 %copy-start.1 = (bf16[4,256,256]{2,1,0:T(8,128)(2,1)S(1)}, bf16[4,256,256]{2,1,0:T(8,128)(2,1)}, u32[]{:S(2)}) copy-start(bf16[4,256,256]{2,1,0:T(8,128)(2,1)} %copy-done) | copy-start | bytes 1572868
  99.1 3.9 %copy-start.4 = (f32[1,4,128,128]{3,2,1,0:T(8,128)S(1)}, f32[1,4,128,128]{3,2,1,0:T(8,128)}, u32[]{:S(2)}) copy-start(f32[1,4,128,128]{3,2,1,0:T(8,128)} %copy-done.3) | copy-start | bytes 786436
  99.2 3.8 %collective-permute-start.3 = (f32[2,1,4,64,128]{4,3,2,1,0:T(8,128)S(1)}, f32[2,1,4,64,128]{4,3,2,1,0:T(8,128)S(1)}, u32[]{:S(2)}, u32[]{:S(2)}) collective-permute-start(f32[2,1,4,64,128]{4,3,2,1,0:T(8,128)S(1)} %pad_maximum_fusion.3), channel_id=1, source_target_pairs={{0,16},{16,0},{1,17},{17,1},{2,18},{18,2},{3,19},{19,3},{4,20},{20... | collective-permute-start | bytes 786440 | tf_op jit(solution)/shard_map/ppermute | solution.py:128
  103.8 1.2 copy-start.5

commit v6 on v4

--- a/solution.py
+++ b/solution.py
@@ -81,7 +81,8 @@
     local_grad = jnp.einsum(
         "bihd,bihe->bhde", scaled_query, g_split, preferred_element_type=jnp.float32
     )
-    chip_count = lax.axis_size("z")
+    group_count = lax.axis_size("zg")
+    inner_count = lax.axis_size("zl")
     core = lax.axis_index("core")
     second = core == 1
     pairs = [(0, 1), (1, 0)]
@@ -99,29 +100,47 @@
     chip_update = keep_hi * update_lo + update_hi
     chip_grad = keep_lo * grad_hi + grad_lo
     half = width // 2
-    band = half // chip_count
+    band = half // inner_count
 
     def my_half(state):
         return lax.dynamic_slice_in_dim(state, core * half, half, axis=2)
 
     chip_last = jnp.broadcast_to((last_lo + last_hi)[..., None], (batch_count, head_count, width))
     last_piece = jnp.broadcast_to(
-        chip_last[None, :, :, None, :], (chip_count, batch_count, head_count, 1, width)
+        chip_last[None, :, :, None, :], (inner_count, batch_count, head_count, 1, width)
     )
     send = jnp.concatenate(
-        [to_pieces(my_half(chip_update), chip_count), to_pieces(my_half(chip_grad), chip_count), last_piece],
+        [to_pieces(my_half(chip_update), inner_count), to_pieces(my_half(chip_grad), inner_count), last_piece],
         axis=3,
     )
-    got = lax.all_to_all(send, "z", 0, 0, tiled=True)
-    forward_w, backward_w = block_weights(got[:, :, :, 2 * band, 0])
-    mixed = jnp.stack(
-        [
-            mix_blocks(forward_w, got[:, :, :, :band]),
-            mix_blocks(backward_w, got[:, :, :, band : 2 * band]),
-        ],
-        axis=1,
-    )
-    back = lax.all_to_all(mixed, "z", 0, 0, tiled=True)
+    got = lax.all_to_all(send, "zl", 0, 0, tiled=True)
+    chip_states = got[:, :, :, :band]
+    chip_grads = got[:, :, :, band : 2 * band]
+    chip_lasts = got[:, :, :, 2 * band, 0]
+    forward_w, backward_w = block_weights(chip_lasts)
+    within_state = mix_blocks(forward_w, chip_states)
+    within_grad = mix_blocks(backward_w, chip_grads)
+    inclusive = jnp.cumsum(chip_lasts, axis=0)
+    exclusive = inclusive - chip_lasts
+    total = inclusive[-1]
+    after_rise = jnp.exp(total[None] - inclusive)[..., None, None]
+    before_rise = jnp.exp(exclusive)[..., None, None]
+    group_state = jnp.sum(after_rise * chip_states, axis=0)
+    group_grad = jnp.sum(before_rise * chip_grads, axis=0)
+    group_keep = jnp.exp(total)[..., None, None]
+    upward = [(index, index + 1) for index in range(group_count - 1)]
+    downward = [(index + 1, index) for index in range(group_count - 1)]
+    entering_group = jnp.zeros_like(group_state)
+    leaving_group = jnp.zeros_like(group_grad)
+    for _ in range(group_count - 1):
+        entering_group, leaving_group = (
+            lax.ppermute(group_keep * entering_group + group_state, "zg", upward),
+            lax.ppermute(group_keep * leaving_group + group_grad, "zg", downward),
+        )
+    state_pieces = within_state + before_rise * entering_group[None]
+    grad_pieces = within_grad + after_rise * leaving_group[None]
+    mixed = jnp.stack([state_pieces, grad_pieces], axis=1)
+    back = lax.all_to_all(mixed, "zl", 0, 0, tiled=True)
     halves = jnp.stack([from_pieces(back[:, 0]), from_pieces(back[:, 1])])
     other_halves = lax.ppermute(halves, "core", pairs)
     low_rows, high_rows = order(halves, other_halves)
@@ -170,24 +189,25 @@
 
 def solution(mesh):
     ctx_count, uly_count = mesh.shape["ctx"], mesh.shape["uly"]
-    grid = mesh.devices.reshape(ctx_count // 2, 2, uly_count)
-    chips = Mesh(grid, ("z", "core", "uly"))
+    inner = 4 if ctx_count % 8 == 0 else 1
+    grid = mesh.devices.reshape(ctx_count // (2 * inner), inner, 2, uly_count)
+    chips = Mesh(grid, ("zg", "zl", "core", "uly"))
     placed = (
-        P(None, ("z", "core"), "uly"),
-        P(None, ("z", "core"), "uly"),
-        P(None, ("z", "core"), "uly"),
-        P(None, ("z", "core", "uly"), None),
-        P(None, "uly", ("z", "core")),
+        P(None, ("zg", "zl", "core"), "uly"),
+        P(None, ("zg", "zl", "core"), "uly"),
+        P(None, ("zg", "zl", "core"), "uly"),
+        P(None, ("zg", "zl", "core", "uly"), None),
+        P(None, "uly", ("zg", "zl", "core")),
     )
     return jax.shard_map(
         local,
         mesh=chips,
         in_specs=placed,
         out_specs=(
-            P(None, ("z", "core", "uly"), None),
-            P(None, ("z", "core", "uly"), None),
-            P(None, ("z", "core", "uly"), None),
-            P(None, ("z", "core", "uly"), None),
+            P(None, ("zg", "zl", "core", "uly"), None),
+            P(None, ("zg", "zl", "core", "uly"), None),
+            P(None, ("zg", "zl", "core", "uly"), None),
+            P(None, ("zg", "zl", "core", "uly"), None),
         ),
         check_vma=False,
     )

time: 124 us -> 130 us (1.048)
  starting transfers between devices: 36.8 us -> 56.1 us
  waiting for transfers between devices: 41.6 us -> 27.9 us
    ppermute x0 -> x6, starting transfers between devices: none -> 29.9 us  [the longest x3 26 us: local(): lax.ppermute(group_keep * entering_group + group_state, 'zg', upward)]
    all_to_all x2, waiting for transfers between devices: 35.6 us -> 12 us  [the longest x1 7.2 us: local(): got = lax.all_to_all(send, 'zl', 0, 0, tiled=True)]
    all_to_all x2, starting transfers between devices: 21.9 us -> 11.3 us  [the longest x1 6 us: local(): got = lax.all_to_all(send, 'zl', 0, 0, tiled=True)]
    ppermute x0 -> x6, waiting for transfers between devices: none -> 9.97 us  [the longest x3 7.98 us: local(): lax.ppermute(group_keep * leaving_group + group_grad, 'zg', downward)]
    unnamed x19 -> x20, local copies, waits for them, and re-layouts: 4.43 us -> 4.54 us
  transfers between devices with their start and end apart: 7 -> 13, of which waited for: 4 -> 8; matrix products, arithmetic and copies ran while one was open for 5% -> 5% of each run, Pallas kernels for 0% -> 0%
where the time goes in v6:
time: 130 us; the launch traced here: 129 us
  starting transfers between devices  56.1 us (43%)
  waiting for transfers between devices  27.9 us (21%)
  blocking collectives  21.2 us (16%)
  local copies, waits for them, and re-layouts  14.4 us (11%)
  matrix products  5.79 us (4%)
  other arithmetic  2.73 us (2%)
    ppermute x3, starting transfers between devices, local(): lax.ppermute(group_keep * entering_group + group_state, 'zg', upward)  26 us
    all_to_all x1, blocking collectives, local(): outs = lax.all_to_all(outs, 'uly', 0, 0, tiled=True)  21.2 us
    ppermute x3, waiting for transfers between devices, local(): lax.ppermute(group_keep * leaving_group + group_grad, 'zg', downward)  7.98 us
    all_to_all x1, waiting for transfers between devices, local(): got = lax.all_to_all(send, 'zl', 0, 0, tiled=True)  7.2 us
    all_to_all x1, starting transfers between devices, local(): g_parts = lax.all_to_all(g_parts, 'uly', 0, 0, tiled=True)  7.03 us
    all_to_all x1, starting transfers between devices, local(): got = lax.all_to_all(send, 'zl', 0, 0, tiled=True)  6 us
    ppermute x3, starting transfers between devices, local(): lax.ppermute((update, local_grad, last), 'core', pairs)  5.97 us
    all_to_all x1, starting transfers between devices, local(): back = lax.all_to_all(mixed, 'zl', 0, 0, tiled=True)  5.25 us
  transfers between devices with their start and end apart: 13, of which 8 were waited for; matrix products, arithmetic and copies ran while one was open for 5% of the time, Pallas kernels for 0%

profile of v6, /device:TPU:32, one launch (start us, length us, event | category | flops | bytes accessed | tf_op | source)
XLA Modules:
  0.0 129.3 jit_solution(11678894743188566385)
XLA Ops:
  0.6 0.7 reshape.495
  1.3 1.2 reduce-window.6
  2.6 0.1 copy.310
  3.0 1.9 %collective-permute-start = (f32[1,4]{1,0:T(1,128)S(1)}, f32[1,4]{1,0:T(1,128)S(1)}, u32[]{:S(2)}, u32[]{:S(2)}) collective-permute-start(f32[1,4]{1,0:T(1,128)S(1)} %get-tuple-element.22), channel_id=1, source_target_pairs={{0,16},{16,0},{1,17},{17,1},{2,18},{18,2},{3,19},{19,3},{4,20},{20... | collective-permute-start | bytes 56 | tf_op jit(solution)/shard_map/ppermute | solution.py:90
  5.0 0.9 copy.257
  5.9 7.0 %all-to-all-start = ((bf16[16,1,16,512]{3,2,1,0:T(8,128)(2,1)}), bf16[16,1,16,512]{3,2,1,0:T(8,128)(2,1)S(1)}, u32[]{:S(2)}, u32[]{:S(2)}) async-start(bf16[16,1,16,512]{3,2,1,0:T(8,128)(2,1)} %copy.257), calls=%async_computation | async-start | bytes 524288 | tf_op jit(solution)/shard_map/all_to_all | solution.py:71
  13.0 0.8 copy-done.6
  13.9 0.9 copy-done.7
  14.8 0.1 copy.314
  15.0 0.2 convolution_bitcast_fusion.8
  15.2 2.1 %collective-permute-start.1 = (f32[1,4,128,128]{3,2,1,0:T(8,128)S(1)}, f32[1,4,128,128]{3,2,1,0:T(8,128)S(1)}, u32[]{:S(2)}, u32[]{:S(2)}) collective-permute-start(f32[1,4,128,128]{3,2,1,0:T(8,128)S(1)} %convolution_bitcast_fusion.8), channel_id=1, source_target_pairs={{0,16},{16,0},{1,17},{17,1},{2,18},{18,2},{3,19},{19,3},{4,20},{20... | collective-permute-start | bytes 786440 | tf_op jit(solution)/shard_map/ppermute | solution.py:90
  17.5 4.6 %all-to-all-done = bf16[16,1,16,512]{3,2,1,0:T(8,128)(2,1)S(1)} async-done(((bf16[16,1,16,512]{3,2,1,0:T(8,128)(2,1)}), bf16[16,1,16,512]{3,2,1,0:T(8,128)(2,1)S(1)}, u32[]{:S(2)}, u32[]{:S(2)}) %all-to-all-start) | async-done | bytes 262176 | tf_op jit(solution)/shard_map/all_to_all | solution.py:71
  22.1 0.5 convolution_bitcast_fusion.7
  22.6 1.9 %collective-permute-start.2 = (f32[1,4,128,128]{3,2,1,0:T(8,128)S(1)}, f32[1,4,128,128]{3,2,1,0:T(8,128)S(1)}, u32[]{:S(2)}, u32[]{:S(2)}) collective-permute-start(f32[1,4,128,128]{3,2,1,0:T(8,128)S(1)} %convolution_bitcast_fusion.7), channel_id=1, source_target_pairs={{0,16},{16,0},{1,17},{17,1},{2,18},{18,2},{3,19},{19,3},{4,20},{20... | collective-permute-start | bytes 786440 | tf_op jit(solution)/shard_map/ppermute | solution.py:90
  24.7 1.4 %collective-permute-done.2 = f32[1,4,128,128]{3,2,1,0:T(8,128)S(1)} collective-permute-done((f32[1,4,128,128]{3,2,1,0:T(8,128)S(1)}, f32[1,4,128,128]{3,2,1,0:T(8,128)S(1)}, u32[]{:S(2)}, u32[]{:S(2)}) %collective-permute-start.2) | collective-permute-done | bytes 262176 | tf_op jit(solution)/shard_map/ppermute | solution.py:90
  26.2 0.6 copy-done.1
  26.9 0.9 copy.260
  27.8 6.0 %all-to-all-start.1 = ((f32[4,1,4,33,128]{4,2,3,1,0:T(4,128)}), f32[4,1,4,33,128]{4,2,3,1,0:T(4,128)S(1)}, u32[]{:S(2)}, u32[]{:S(2)}) async-start(f32[4,1,4,33,128]{4,2,3,1,0:T(4,128)} %copy.260), calls=%async_computation.1 | async-start | bytes 540672 | tf_op jit(solution)/shard_map/all_to_all | solution.py:116
  33.9 7.2 %all-to-all-done.1 = f32[4,1,4,33,128]{4,2,3,1,0:T(4,128)S(1)} async-done(((f32[4,1,4,33,128]{4,2,3,1,0:T(4,128)}), f32[4,1,4,33,128]{4,2,3,1,0:T(4,128)S(1)}, u32[]{:S(2)}, u32[]{:S(2)}) %all-to-all-start.1) | async-done | bytes 270368 | tf_op jit(solution)/shard_map/all_to_all | solution.py:116
  41.5 0.3 multiply_reduce_fusion
  42.0 9.1 %collective-permute-start.3 = (f32[1,4,16,128]{3,2,1,0:T(8,128)S(1)}, f32[1,4,16,128]{3,2,1,0:T(8,128)S(1)}, u32[]{:S(2)}, u32[]{:S(2)}) collective-permute-start(f32[1,4,16,128]{3,2,1,0:T(8,128)S(1)} %get-tuple-element.27), channel_id=1, source_target_pairs={{0,128},{128,256},{256,384},{1,129},{129,257},{257,385},{2,130},{1... | collective-permute-start | bytes 98312 | tf_op jit(solution)/shard_map/ppermute | solution.py:137
  51.1 1.3 collective-permute-start.6
  52.4 0.3 collective-permute-done.3
  52.7 8.2 %collective-permute-start.4 = (f32[1,4,16,128]{3,2,1,0:T(8,128)S(1)}, f32[1,4,16,128]{3,2,1,0:T(8,128)S(1)}, u32[]{:S(2)}, u32[]{:S(2)}) collective-permute-start(f32[1,4,16,128]{3,2,1,0:T(8,128)S(1)} %bitcast_add_fusion.5), channel_id=1, source_target_pairs={{0,128},{128,256},{256,384},{1,129},{129,257},{257,385},{2,130},{1... | collective-permute-start | bytes 98312 | tf_op jit(solution)/shard_map/ppermute | solution.py:137
  60.9 1.5 %collective-permute-done.4 = f32[1,4,16,128]{3,2,1,0:T(8,128)S(1)} collective-permute-done((f32[1,4,16,128]{3,2,1,0:T(8,128)S(1)}, f32[1,4,16,128]{3,2,1,0:T(8,128)S(1)}, u32[]{:S(2)}, u32[]{:S(2)}) %collective-permute-start.4) | collective-permute-done | bytes 32800 | tf_op jit(solution)/shard_map/ppermute | solution.py:137
  62.6 1.3 collective-permute-start.7
  64.0 8.7 %collective-permute-start.5 = (f32[1,4,16,128]{3,2,1,0:T(8,128)S(1)}, f32[1,4,16,128]{3,2,1,0:T(8,128)S(1)}, u32[]{:S(2)}, u32[]{:S(2)}) collective-permute-start(f32[1,4,16,128]{3,2,1,0:T(8,128)S(1)} %get-tuple-element.25), channel_id=1, source_target_pairs={{0,128},{128,256},{256,384},{1,129},{129,257},{257,385},{2,130},{1... | collective-permute-start | bytes 98312 | tf_op jit(solution)/shard_map/ppermute | solution.py:137
  72.9 1.3 collective-permute-start.8
  74.2 0.2 collective-permute-done.5
  74.4 0.4 add_bitcast_fusion.1
  74.8 7.9 %collective-permute-done.8 = f32[1,4,16,128]{3,2,1,0:T(8,128)S(1)} collective-permute-done((f32[1,4,16,128]{3,2,1,0:T(8,128)S(1)}, f32[1,4,16,128]{3,2,1,0:T(8,128)S(1)}, u32[]{:S(2)}, u32[]{:S(2)}) %collective-permute-start.8) | collective-permute-done | bytes 32800 | tf_op jit(solution)/shard_map/ppermute | solution.py:138
  82.8 0.4 add_bitcast_fusion
  83.3 0.7 copy.268
  84.0 5.3 %all-to-all-start.2 = ((f32[4,2,1,4,16,128]{5,4,3,2,1,0:T(8,128)}), f32[4,2,1,4,16,128]{5,4,3,2,1,0:T(8,128)S(1)}, u32[]{:S(2)}, u32[]{:S(2)}) async-start(f32[4,2,1,4,16,128]{5,4,3,2,1,0:T(8,128)} %copy.268), calls=%async_computation.2 | async-start | bytes 524288 | tf_op jit(solution)/shard_map/all_to_all | solution.py:143
  89.3 0.4 fusion
  89.7 0.3 convolution_bitcast_fusion.6
  90.0 0.3 convolution_bitcast_fusion.1
  90.3 0.4 fusion.1
  90.7 4.8 %all-to-all-done.2 = f32[4,2,1,4,16,128]{5,4,3,2,1,0:T(8,128)S(1)} async-done(((f32[4,2,1,4,16,128]{5,4,3,2,1,0:T(8,128)}), f32[4,2,1,4,16,128]{5,4,3,2,1,0:T(8,128)S(1)}, u32[]{:S(2)}, u32[]{:S(2)}) %all-to-all-start.2) | async-done | bytes 262176 | tf_op jit(solution)/shard_map/all_to_all | solution.py:143
  95.6 1.9 %collective-permute-start.9 = (f32[2,1,4,64,128]{4,3,2,1,0:T(8,128)S(1)}, f32[2,1,4,64,128]{4,3,2,1,0:T(8,128)S(1)}, u32[]{:S(2)}, u32[]{:S(2)}) collective-permute-start(f32[2,1,4,64,128]{4,3,2,1,0:T(8,128)S(1)} %pad_maximum_fusion.3), channel_id=1, source_target_pairs={{0,16},{16,0},{1,17},{17,1},{2,18},{18,2},{3,19},{19,3},{4,20},{20... | collective-permute-start | bytes 786440 | tf_op jit(solution)/shard_map/ppermute | solution.py:145
  97.5 0.3 convolution_bitcast_fusion.3
  97.9 1.3 %convolution_bitcast_fusion.5 = f32[1,256,4,128]{3,1,2,0:T(8,128)S(1)} fusion(bf16[4,256,256]{2,1,0:T(8,128)(2,1)} %copy-done, bf16[256,4,128]{0,2,1:T(8,128)(2,1)S(1)} %bitcast.237), kind=kOutput, calls=%fused_computation.9 | convolution fusion | flops 67108864 | bytes 1310720 | tf_op jit(solution)/shard_map/bhij,bjhd->bihd/dot_general | solution.py:161
  99.3 0.9 copy-done.2
  100.1 0.1 select_convert_fusion.1
  100.3 0.3 fusion.8
  100.6 0.3 copy-done.3
  101.0 0.2 copy.292
  101.3 0.3 fusion.12
  101.6 0.2 copy.273
  101.9 0.8 copy-done.4
  102.7 0.2 fusion.9
  103.0 0.2 fusion.10
  103.2 0.2 copy.280
  103.5 0.2 copy.286
  103.9 0.1 maximum_bitcast_fusion
  104.1 21.2 %all_to_all.20 = bf16[16,4,1,16,512]{4,3,2,1,0:T(8,128)(2,1)S(1)} all-to-all(bf16[16,4,1,16,512]{4,3,2,1,0:T(8,128)(2,1)S(1)} %copy.293), channel_id=1, replica_groups=mesh['zg'=4,'zl'=4,'core'=2,'uly'=16] {'uly'}, dimensions={0} | all-to-all | bytes 2097152 | tf_op jit(solution)/shard_map/all_to_all | solution.py:183
  125.4 0.2 copy.297
  125.5 0.8 squeeze.45
  126.4 0.1 copy.296
  126.5 0.8 squeeze.44
  127.3 0.1 copy.295
  127.5 0.8 squeeze.43
  128.3 0.1 copy.294
  128.5 0.8 squeeze.42
  (73 shorter events, 2.9 us)
Async XLA Ops:
  2.6 2.3 %copy-start.5 = (bf16[1,16,8192]{2,1,0:T(8,128)(2,1)S(1)}, bf16[1,16,8192]{2,1,0:T(8,128)(2,1)}, u32[]{:S(2)}) copy-start(bf16[1,16,8192]{2,1,0:T(8,128)(2,1)} %param.8) | copy-start | bytes 786436
  3.0 14.5 %collective-permute-start = (f32[1,4]{1,0:T(1,128)S(1)}, f32[1,4]{1,0:T(1,128)S(1)}, u32[]{:S(2)}, u32[]{:S(2)}) collective-permute-start(f32[1,4]{1,0:T(1,128)S(1)} %get-tuple-element.22), channel_id=1, source_target_pairs={{0,16},{16,0},{1,17},{17,1},{2,18},{18,2},{3,19},{19,3},{4,20},{20... | collective-permute-start | bytes 56 | tf_op jit(solution)/shard_map/ppermute | solution.py:90
  5.9 16.2 %all-to-all-start = ((bf16[16,1,16,512]{3,2,1,0:T(8,128)(2,1)}), bf16[16,1,16,512]{3,2,1,0:T(8,128)(2,1)S(1)}, u32[]{:S(2)}, u32[]{:S(2)}) async-start(bf16[16,1,16,512]{3,2,1,0:T(8,128)(2,1)} %copy.257), calls=%async_computation | async-start | bytes 524288 | tf_op jit(solution)/shard_map/all_to_all | solution.py:71
  12.9 1.0 copy-start.6
  13.9 0.9 copy-start.7
  14.9 2.4 %copy-start.8 = (bf16[1,256,512]{2,1,0:T(8,128)(2,1)S(1)}, bf16[1,256,512]{2,1,0:T(8,128)(2,1)}, u32[]{:S(2)}) copy-start(bf16[1,256,512]{2,1,0:T(8,128)(2,1)} %param.5) | copy-start | bytes 786436
  15.2 9.4 %collective-permute-start.1 = (f32[1,4,128,128]{3,2,1,0:T(8,128)S(1)}, f32[1,4,128,128]{3,2,1,0:T(8,128)S(1)}, u32[]{:S(2)}, u32[]{:S(2)}) collective-permute-start(f32[1,4,128,128]{3,2,1,0:T(8,128)S(1)} %convolution_bitcast_fusion.8), channel_id=1, source_target_pairs={{0,16},{16,0},{1,17},{17,1},{2,18},{18,2},{3,19},{19,3},{4,20},{20... | collective-permute-start | bytes 786440 | tf_op jit(solution)/shard_map/ppermute | solution.py:90
  22.6 3.4 %collective-permute-start.2 = (f32[1,4,128,128]{3,2,1,0:T(8,128)S(1)}, f32[1,4,128,128]{3,2,1,0:T(8,128)S(1)}, u32[]{:S(2)}, u32[]{:S(2)}) collective-permute-start(f32[1,4,128,128]{3,2,1,0:T(8,128)S(1)} %convolution_bitcast_fusion.7), channel_id=1, source_target_pairs={{0,16},{16,0},{1,17},{17,1},{2,18},{18,2},{3,19},{19,3},{4,20},{20... | collective-permute-start | bytes 786440 | tf_op jit(solution)/shard_map/ppermute | solution.py:90
  26.1 0.7 copy-start.1
  27.8 13.3 %all-to-all-start.1 = ((f32[4,1,4,33,128]{4,2,3,1,0:T(4,128)}), f32[4,1,4,33,128]{4,2,3,1,0:T(4,128)S(1)}, u32[]{:S(2)}, u32[]{:S(2)}) async-start(f32[4,1,4,33,128]{4,2,3,1,0:T(4,128)} %copy.260), calls=%async_computation.1 | async-start | bytes 540672 | tf_op jit(solution)/shard_map/all_to_all | solution.py:116
  42.0 10.7 %collective-permute-start.3 = (f32[1,4,16,128]{3,2,1,0:T(8,128)S(1)}, f32[1,4,16,128]{3,2,1,0:T(8,128)S(1)}, u32[]{:S(2)}, u32[]{:S(2)}) collective-permute-start(f32[1,4,16,128]{3,2,1,0:T(8,128)S(1)} %get-tuple-element.27), channel_id=1, source_target_pairs={{0,128},{128,256},{256,384},{1,129},{129,257},{257,385},{2,130},{1... | collective-permute-start | bytes 98312 | tf_op jit(solution)/shard_map/ppermute | solution.py:137
  51.1 9.9 %collective-permute-start.6 = (f32[1,4,16,128]{3,2,1,0:T(8,128)S(1)}, f32[1,4,16,128]{3,2,1,0:T(8,128)S(1)}, u32[]{:S(2)}, u32[]{:S(2)}) collective-permute-start(f32[1,4,16,128]{3,2,1,0:T(8,128)S(1)} %get-tuple-element.28), channel_id=1, source_target_pairs={{128,0},{256,128},{384,256},{129,1},{257,129},{385,257},{130,2},{2... | collective-permute-start | bytes 98312 | tf_op jit(solution)/shard_map/ppermute | solution.py:138
  52.7 9.8 %collective-permute-start.4 = (f32[1,4,16,128]{3,2,1,0:T(8,128)S(1)}, f32[1,4,16,128]{3,2,1,0:T(8,128)S(1)}, u32[]{:S(2)}, u32[]{:S(2)}) collective-permute-start(f32[1,4,16,128]{3,2,1,0:T(8,128)S(1)} %bitcast_add_fusion.5), channel_id=1, source_target_pairs={{0,128},{128,256},{256,384},{1,129},{129,257},{257,385},{2,130},{1... | collective-permute-start | bytes 98312 | tf_op jit(solution)/shard_map/ppermute | solution.py:137
  62.6 10.2 %collective-permute-start.7 = (f32[1,4,16,128]{3,2,1,0:T(8,128)S(1)}, f32[1,4,16,128]{3,2,1,0:T(8,128)S(1)}, u32[]{:S(2)}, u32[]{:S(2)}) collective-permute-start(f32[1,4,16,128]{3,2,1,0:T(8,128)S(1)} %get-tuple-element.26), channel_id=1, source_target_pairs={{128,0},{256,128},{384,256},{129,1},{257,129},{385,257},{130,2},{2... | collective-permute-start | bytes 98312 | tf_op jit(solution)/shard_map/ppermute | solution.py:138
  64.0 10.3 %collective-permute-start.5 = (f32[1,4,16,128]{3,2,1,0:T(8,128)S(1)}, f32[1,4,16,128]{3,2,1,0:T(8,128)S(1)}, u32[]{:S(2)}, u32[]{:S(2)}) collective-permute-start(f32[1,4,16,128]{3,2,1,0:T(8,128)S(1)} %get-tuple-element.25), channel_id=1, source_target_pairs={{0,128},{128,256},{256,384},{1,129},{129,257},{257,385},{2,130},{1... | collective-permute-start | bytes 98312 | tf_op jit(solution)/shard_map/ppermute | solution.py:137
  72.9 9.9 %collective-permute-start.8 = (f32[1,4,16,128]{3,2,1,0:T(8,128)S(1)}, f32[1,4,16,128]{3,2,1,0:T(8,128)S(1)}, u32[]{:S(2)}, u32[]{:S(2)}) collective-permute-start(f32[1,4,16,128]{3,2,1,0:T(8,128)S(1)} %bitcast_add_fusion.1), channel_id=1, source_target_pairs={{128,0},{256,128},{384,256},{129,1},{257,129},{385,257},{130,2},{2... | collective-permute-start | bytes 98312 | tf_op jit(solution)/shard_map/ppermute | solution.py:138
  84.0 11.5 %all-to-all-start.2 = ((f32[4,2,1,4,16,128]{5,4,3,2,1,0:T(8,128)}), f32[4,2,1,4,16,128]{5,4,3,2,1,0:T(8,128)S(1)}, u32[]{:S(2)}, u32[]{:S(2)}) async-start(f32[4,2,1,4,16,128]{5,4,3,2,1,0:T(8,128)} %copy.268), calls=%async_computation.2 | async-start | bytes 524288 | tf_op jit(solution)/shard_map/all_to_all | solution.py:143
  90.7 6.8 %copy-start = (bf16[4,256,256]{2,1,0:T(8,128)(2,1)}, bf16[4,256,256]{2,1,0:T(8,128)(2,1)S(1)}, u32[]{:S(2)}) copy-start(bf16[4,256,256]{2,1,0:T(8,128)(2,1)S(1)} %fusion.1) | copy-start | bytes 1572868
  95.6 3.6 %collective-permute-start.9 = (f32[2,1,4,64,128]{4,3,2,1,0:T(8,128)S(1)}, f32[2,1,4,64,128]{4,3,2,1,0:T(8,128)S(1)}, u32[]{:S(2)}, u32[]{:S(2)}) collective-permute-start(f32[2,1,4,64,128]{4,3,2,1,0:T(8,128)S(1)} %pad_maximum_fusion.3), channel_id=1, source_target_pairs={{0,16},{16,0},{1,17},{17,1},{2,18},{18,2},{3,19},{19,3},{4,20},{20... | collective-permute-start | bytes 786440 | tf_op jit(solution)/shard_map/ppermute | solution.py:145
  99.2 1.0 copy-start.2
  100.3 0.7 copy-start.3
  101.8 0.9 copy-start.4

commit v7 on v6

--- a/solution.py
+++ b/solution.py
@@ -127,16 +127,26 @@
     before_rise = jnp.exp(exclusive)[..., None, None]
     group_state = jnp.sum(after_rise * chip_states, axis=0)
     group_grad = jnp.sum(before_rise * chip_grads, axis=0)
-    group_keep = jnp.exp(total)[..., None, None]
-    upward = [(index, index + 1) for index in range(group_count - 1)]
-    downward = [(index + 1, index) for index in range(group_count - 1)]
-    entering_group = jnp.zeros_like(group_state)
-    leaving_group = jnp.zeros_like(group_grad)
-    for _ in range(group_count - 1):
-        entering_group, leaving_group = (
-            lax.ppermute(group_keep * entering_group + group_state, "zg", upward),
-            lax.ppermute(group_keep * leaving_group + group_grad, "zg", downward),
-        )
+    group_last = jnp.broadcast_to(total[..., None], (batch_count, head_count, width))
+    group_last = jnp.broadcast_to(
+        group_last[None, :, :, None, :], (group_count, batch_count, head_count, 1, width)
+    )
+    cut = band // group_count
+    send_groups = jnp.concatenate(
+        [to_pieces(group_state, group_count), to_pieces(group_grad, group_count), group_last], axis=3
+    )
+    got_groups = lax.all_to_all(send_groups, "zg", 0, 0, tiled=True)
+    forward_g, backward_g = block_weights(got_groups[:, :, :, 2 * cut, 0])
+    mixed_groups = jnp.stack(
+        [
+            mix_blocks(forward_g, got_groups[:, :, :, :cut]),
+            mix_blocks(backward_g, got_groups[:, :, :, cut : 2 * cut]),
+        ],
+        axis=1,
+    )
+    back_groups = lax.all_to_all(mixed_groups, "zg", 0, 0, tiled=True)
+    entering_group = from_pieces(back_groups[:, 0])
+    leaving_group = from_pieces(back_groups[:, 1])
     state_pieces = within_state + before_rise * entering_group[None]
     grad_pieces = within_grad + after_rise * leaving_group[None]
     mixed = jnp.stack([state_pieces, grad_pieces], axis=1)

time: 130 us -> 134 us (1.031)
  waiting for transfers between devices: 27.9 us -> 43.9 us
  starting transfers between devices: 56.1 us -> 42.1 us
  local copies, waits for them, and re-layouts: 14.4 us -> 16.1 us
    ppermute x6 -> x0, starting transfers between devices: 29.9 us -> none  [the longest x3 26 us: local(): lax.ppermute(group_keep * entering_group + group_state, 'zg', upward)]
    all_to_all x0 -> x2, waiting for transfers between devices: none -> 26 us  [the longest x1 13.2 us: local(): back_groups = lax.all_to_all(mixed_groups, 'zg', 0, 0, tiled=True)]
    all_to_all x0 -> x2, starting transfers between devices: none -> 16.2 us  [the longest x1 12.9 us: local(): got_groups = lax.all_to_all(send_groups, 'zg', 0, 0, tiled=True)]
    ppermute x6 -> x0, waiting for transfers between devices: 9.97 us -> none  [the longest x3 7.98 us: local(): lax.ppermute(group_keep * leaving_group + group_grad, 'zg', downward)]
  transfers between devices with their start and end apart: 13 -> 9, of which waited for: 8 -> 6; matrix products, arithmetic and copies ran while one was open for 5% -> 4% of each run, Pallas kernels for 0% -> 0%
where the time goes in v7:
time: 134 us; the launch traced here: 133 us
  waiting for transfers between devices  43.9 us (33%)
  starting transfers between devices  42.1 us (31%)
  blocking collectives  21.2 us (16%)
  local copies, waits for them, and re-layouts  16.1 us (12%)
  matrix products  6.32 us (5%)
  other arithmetic  2.5 us (2%)
    all_to_all x1, blocking collectives, local(): outs = lax.all_to_all(outs, 'uly', 0, 0, tiled=True)  21.2 us
    all_to_all x1, waiting for transfers between devices, local(): back_groups = lax.all_to_all(mixed_groups, 'zg', 0, 0, tiled=True)  13.2 us
    all_to_all x1, starting transfers between devices, local(): got_groups = lax.all_to_all(send_groups, 'zg', 0, 0, tiled=True)  12.9 us
    all_to_all x1, waiting for transfers between devices, local(): got_groups = lax.all_to_all(send_groups, 'zg', 0, 0, tiled=True)  12.9 us
    all_to_all x1, waiting for transfers between devices, local(): got = lax.all_to_all(send, 'zl', 0, 0, tiled=True)  7.19 us
    all_to_all x1, starting transfers between devices, local(): g_parts = lax.all_to_all(g_parts, 'uly', 0, 0, tiled=True)  7.03 us
    all_to_all x1, starting transfers between devices, local(): got = lax.all_to_all(send, 'zl', 0, 0, tiled=True)  6 us
    ppermute x3, starting transfers between devices, local(): lax.ppermute((update, local_grad, last), 'core', pairs)  5.97 us
  transfers between devices with their start and end apart: 9, of which 6 were waited for; matrix products, arithmetic and copies ran while one was open for 4% of the time, Pallas kernels for 0%

profile of v7, /device:TPU:32, one launch (start us, length us, event | category | flops | bytes accessed | tf_op | source)
XLA Modules:
  0.0 133.4 jit_solution(5481342302320464570)
XLA Ops:
  0.6 0.7 reshape.520
  1.3 1.2 reduce-window.6
  2.6 0.1 copy.353
  3.0 1.9 %collective-permute-start = (f32[1,4]{1,0:T(1,128)S(1)}, f32[1,4]{1,0:T(1,128)S(1)}, u32[]{:S(2)}, u32[]{:S(2)}) collective-permute-start(f32[1,4]{1,0:T(1,128)S(1)} %get-tuple-element.22), channel_id=1, source_target_pairs={{0,16},{16,0},{1,17},{17,1},{2,18},{18,2},{3,19},{19,3},{4,20},{20... | collective-permute-start | bytes 56 | tf_op jit(solution)/shard_map/ppermute | solution.py:90
  5.0 0.9 copy.290
  5.9 7.0 %all-to-all-start = ((bf16[16,1,16,512]{3,2,1,0:T(8,128)(2,1)}), bf16[16,1,16,512]{3,2,1,0:T(8,128)(2,1)S(1)}, u32[]{:S(2)}, u32[]{:S(2)}) async-start(bf16[16,1,16,512]{3,2,1,0:T(8,128)(2,1)} %copy.290), calls=%async_computation | async-start | bytes 524288 | tf_op jit(solution)/shard_map/all_to_all | solution.py:71
  13.0 0.8 copy-done.6
  13.9 0.9 copy-done.7
  14.8 0.1 copy.359
  15.0 0.2 convolution_bitcast_fusion.8
  15.2 2.1 %collective-permute-start.1 = (f32[1,4,128,128]{3,2,1,0:T(8,128)S(1)}, f32[1,4,128,128]{3,2,1,0:T(8,128)S(1)}, u32[]{:S(2)}, u32[]{:S(2)}) collective-permute-start(f32[1,4,128,128]{3,2,1,0:T(8,128)S(1)} %convolution_bitcast_fusion.8), channel_id=1, source_target_pairs={{0,16},{16,0},{1,17},{17,1},{2,18},{18,2},{3,19},{19,3},{4,20},{20... | collective-permute-start | bytes 786440 | tf_op jit(solution)/shard_map/ppermute | solution.py:90
  17.5 4.6 %all-to-all-done = bf16[16,1,16,512]{3,2,1,0:T(8,128)(2,1)S(1)} async-done(((bf16[16,1,16,512]{3,2,1,0:T(8,128)(2,1)}), bf16[16,1,16,512]{3,2,1,0:T(8,128)(2,1)S(1)}, u32[]{:S(2)}, u32[]{:S(2)}) %all-to-all-start) | async-done | bytes 262176 | tf_op jit(solution)/shard_map/all_to_all | solution.py:71
  22.1 0.5 convolution_bitcast_fusion.7
  22.6 1.9 %collective-permute-start.2 = (f32[1,4,128,128]{3,2,1,0:T(8,128)S(1)}, f32[1,4,128,128]{3,2,1,0:T(8,128)S(1)}, u32[]{:S(2)}, u32[]{:S(2)}) collective-permute-start(f32[1,4,128,128]{3,2,1,0:T(8,128)S(1)} %convolution_bitcast_fusion.7), channel_id=1, source_target_pairs={{0,16},{16,0},{1,17},{17,1},{2,18},{18,2},{3,19},{19,3},{4,20},{20... | collective-permute-start | bytes 786440 | tf_op jit(solution)/shard_map/ppermute | solution.py:90
  24.7 1.4 %collective-permute-done.2 = f32[1,4,128,128]{3,2,1,0:T(8,128)S(1)} collective-permute-done((f32[1,4,128,128]{3,2,1,0:T(8,128)S(1)}, f32[1,4,128,128]{3,2,1,0:T(8,128)S(1)}, u32[]{:S(2)}, u32[]{:S(2)}) %collective-permute-start.2) | collective-permute-done | bytes 262176 | tf_op jit(solution)/shard_map/ppermute | solution.py:90
  26.2 0.6 copy-done.1
  26.9 0.9 copy.293
  27.8 6.0 %all-to-all-start.1 = ((f32[4,1,4,33,128]{4,2,3,1,0:T(4,128)}), f32[4,1,4,33,128]{4,2,3,1,0:T(4,128)S(1)}, u32[]{:S(2)}, u32[]{:S(2)}) async-start(f32[4,1,4,33,128]{4,2,3,1,0:T(4,128)} %copy.293), calls=%async_computation.1 | async-start | bytes 540672 | tf_op jit(solution)/shard_map/all_to_all | solution.py:116
  34.0 7.2 %all-to-all-done.1 = f32[4,1,4,33,128]{4,2,3,1,0:T(4,128)S(1)} async-done(((f32[4,1,4,33,128]{4,2,3,1,0:T(4,128)}), f32[4,1,4,33,128]{4,2,3,1,0:T(4,128)S(1)}, u32[]{:S(2)}, u32[]{:S(2)}) %all-to-all-start.1) | async-done | bytes 270368 | tf_op jit(solution)/shard_map/all_to_all | solution.py:116
  41.1 0.1 copy.355
  41.5 0.3 multiply_reduce_fusion
  42.0 0.7 copy.301
  42.7 12.9 %all-to-all-start.2 = ((f32[4,1,4,9,128]{4,2,3,1,0:T(4,128)}), f32[4,1,4,9,128]{4,2,3,1,0:T(4,128)S(1)}, u32[]{:S(2)}, u32[]{:S(2)}) async-start(f32[4,1,4,9,128]{4,2,3,1,0:T(4,128)} %copy.301), calls=%async_computation.2 | async-start | bytes 147456 | tf_op jit(solution)/shard_map/all_to_all | solution.py:138
  55.7 12.9 %all-to-all-done.2 = f32[4,1,4,9,128]{4,2,3,1,0:T(4,128)S(1)} async-done(((f32[4,1,4,9,128]{4,2,3,1,0:T(4,128)}), f32[4,1,4,9,128]{4,2,3,1,0:T(4,128)S(1)}, u32[]{:S(2)}, u32[]{:S(2)}) %all-to-all-start.2) | async-done | bytes 73760 | tf_op jit(solution)/shard_map/all_to_all | solution.py:138
  68.8 0.3 convolution_bitcast_fusion.11
  69.1 0.3 convolution_bitcast_fusion.12
  69.4 0.6 copy.306
  70.1 3.3 %all-to-all-start.3 = ((f32[4,2,1,4,4,128]{5,4,3,2,1,0:T(4,128)}), f32[4,2,1,4,4,128]{5,4,3,2,1,0:T(4,128)S(1)}, u32[]{:S(2)}, u32[]{:S(2)}) async-start(f32[4,2,1,4,4,128]{5,4,3,2,1,0:T(4,128)} %copy.306), calls=%async_computation.3 | async-start | bytes 131072 | tf_op jit(solution)/shard_map/all_to_all | solution.py:147
  73.5 13.2 %all-to-all-done.3 = f32[4,2,1,4,4,128]{5,4,3,2,1,0:T(4,128)S(1)} async-done(((f32[4,2,1,4,4,128]{5,4,3,2,1,0:T(4,128)}), f32[4,2,1,4,4,128]{5,4,3,2,1,0:T(4,128)S(1)}, u32[]{:S(2)}, u32[]{:S(2)}) %all-to-all-start.3) | async-done | bytes 65568 | tf_op jit(solution)/shard_map/all_to_all | solution.py:147
  86.6 0.4 fusion.14
  87.1 0.4 fusion.16
  87.6 0.7 copy.309
  88.3 5.0 %all-to-all-start.4 = ((f32[4,2,1,4,16,128]{5,4,3,2,1,0:T(8,128)}), f32[4,2,1,4,16,128]{5,4,3,2,1,0:T(8,128)S(1)}, u32[]{:S(2)}, u32[]{:S(2)}) async-start(f32[4,2,1,4,16,128]{5,4,3,2,1,0:T(8,128)} %copy.309), calls=%async_computation.4 | async-start | bytes 524288 | tf_op jit(solution)/shard_map/all_to_all | solution.py:153
  93.4 0.4 fusion
  93.8 0.3 convolution_bitcast_fusion.6
  94.0 0.3 convolution_bitcast_fusion.1
  94.4 0.4 fusion.1
  94.8 4.8 %all-to-all-done.4 = f32[4,2,1,4,16,128]{5,4,3,2,1,0:T(8,128)S(1)} async-done(((f32[4,2,1,4,16,128]{5,4,3,2,1,0:T(8,128)}), f32[4,2,1,4,16,128]{5,4,3,2,1,0:T(8,128)S(1)}, u32[]{:S(2)}, u32[]{:S(2)}) %all-to-all-start.4) | async-done | bytes 262176 | tf_op jit(solution)/shard_map/all_to_all | solution.py:153
  99.7 1.9 %collective-permute-start.3 = (f32[2,1,4,64,128]{4,3,2,1,0:T(8,128)S(1)}, f32[2,1,4,64,128]{4,3,2,1,0:T(8,128)S(1)}, u32[]{:S(2)}, u32[]{:S(2)}) collective-permute-start(f32[2,1,4,64,128]{4,3,2,1,0:T(8,128)S(1)} %pad_maximum_fusion.3), channel_id=1, source_target_pairs={{0,16},{16,0},{1,17},{17,1},{2,18},{18,2},{3,19},{19,3},{4,20},{20... | collective-permute-start | bytes 786440 | tf_op jit(solution)/shard_map/ppermute | solution.py:155
  101.6 0.3 convolution_bitcast_fusion.3
  102.0 1.3 convolution_bitcast_fusion.5
  103.4 0.9 copy-done.2
  104.2 0.1 select_convert_fusion.1
  104.4 0.3 fusion.8
  104.7 0.3 copy-done.3
  105.1 0.2 copy.333
  105.3 0.1 stack.46
  105.4 0.3 fusion.12
  105.7 0.2 copy.314
  106.0 0.8 copy-done.4
  106.8 0.2 fusion.9
  107.1 0.2 fusion.10
  107.3 0.2 copy.321
  107.6 0.2 copy.327
  108.0 0.1 maximum_bitcast_fusion
  108.2 21.2 %all_to_all.30 = bf16[16,4,1,16,512]{4,3,2,1,0:T(8,128)(2,1)S(1)} all-to-all(bf16[16,4,1,16,512]{4,3,2,1,0:T(8,128)(2,1)S(1)} %copy.334), channel_id=1, replica_groups=mesh['zg'=4,'zl'=4,'core'=2,'uly'=16] {'uly'}, dimensions={0} | all-to-all | bytes 2097152 | tf_op jit(solution)/shard_map/all_to_all | solution.py:193
  129.5 0.2 copy.338
  129.6 0.8 squeeze.53
  130.5 0.1 copy.337
  130.6 0.8 squeeze.52
  131.4 0.1 copy.336
  131.6 0.8 squeeze.51
  132.4 0.1 copy.335
  132.6 0.8 squeeze.50
  (76 shorter events, 2.8 us)
Async XLA Ops:
  2.6 2.3 %copy-start.5 = (bf16[1,16,8192]{2,1,0:T(8,128)(2,1)S(1)}, bf16[1,16,8192]{2,1,0:T(8,128)(2,1)}, u32[]{:S(2)}) copy-start(bf16[1,16,8192]{2,1,0:T(8,128)(2,1)} %param.8) | copy-start | bytes 786436
  3.0 14.5 %collective-permute-start = (f32[1,4]{1,0:T(1,128)S(1)}, f32[1,4]{1,0:T(1,128)S(1)}, u32[]{:S(2)}, u32[]{:S(2)}) collective-permute-start(f32[1,4]{1,0:T(1,128)S(1)} %get-tuple-element.22), channel_id=1, source_target_pairs={{0,16},{16,0},{1,17},{17,1},{2,18},{18,2},{3,19},{19,3},{4,20},{20... | collective-permute-start | bytes 56 | tf_op jit(solution)/shard_map/ppermute | solution.py:90
  5.9 16.2 %all-to-all-start = ((bf16[16,1,16,512]{3,2,1,0:T(8,128)(2,1)}), bf16[16,1,16,512]{3,2,1,0:T(8,128)(2,1)S(1)}, u32[]{:S(2)}, u32[]{:S(2)}) async-start(bf16[16,1,16,512]{3,2,1,0:T(8,128)(2,1)} %copy.290), calls=%async_computation | async-start | bytes 524288 | tf_op jit(solution)/shard_map/all_to_all | solution.py:71
  12.9 1.0 copy-start.6
  13.9 0.9 copy-start.7
  14.9 2.4 %copy-start.8 = (bf16[1,256,512]{2,1,0:T(8,128)(2,1)S(1)}, bf16[1,256,512]{2,1,0:T(8,128)(2,1)}, u32[]{:S(2)}) copy-start(bf16[1,256,512]{2,1,0:T(8,128)(2,1)} %param.5) | copy-start | bytes 786436
  15.2 9.4 %collective-permute-start.1 = (f32[1,4,128,128]{3,2,1,0:T(8,128)S(1)}, f32[1,4,128,128]{3,2,1,0:T(8,128)S(1)}, u32[]{:S(2)}, u32[]{:S(2)}) collective-permute-start(f32[1,4,128,128]{3,2,1,0:T(8,128)S(1)} %convolution_bitcast_fusion.8), channel_id=1, source_target_pairs={{0,16},{16,0},{1,17},{17,1},{2,18},{18,2},{3,19},{19,3},{4,20},{20... | collective-permute-start | bytes 786440 | tf_op jit(solution)/shard_map/ppermute | solution.py:90
  22.6 3.4 %collective-permute-start.2 = (f32[1,4,128,128]{3,2,1,0:T(8,128)S(1)}, f32[1,4,128,128]{3,2,1,0:T(8,128)S(1)}, u32[]{:S(2)}, u32[]{:S(2)}) collective-permute-start(f32[1,4,128,128]{3,2,1,0:T(8,128)S(1)} %convolution_bitcast_fusion.7), channel_id=1, source_target_pairs={{0,16},{16,0},{1,17},{17,1},{2,18},{18,2},{3,19},{19,3},{4,20},{20... | collective-permute-start | bytes 786440 | tf_op jit(solution)/shard_map/ppermute | solution.py:90
  26.1 0.7 copy-start.1
  27.8 13.3 %all-to-all-start.1 = ((f32[4,1,4,33,128]{4,2,3,1,0:T(4,128)}), f32[4,1,4,33,128]{4,2,3,1,0:T(4,128)S(1)}, u32[]{:S(2)}, u32[]{:S(2)}) async-start(f32[4,1,4,33,128]{4,2,3,1,0:T(4,128)} %copy.293), calls=%async_computation.1 | async-start | bytes 540672 | tf_op jit(solution)/shard_map/all_to_all | solution.py:116
  42.7 25.9 %all-to-all-start.2 = ((f32[4,1,4,9,128]{4,2,3,1,0:T(4,128)}), f32[4,1,4,9,128]{4,2,3,1,0:T(4,128)S(1)}, u32[]{:S(2)}, u32[]{:S(2)}) async-start(f32[4,1,4,9,128]{4,2,3,1,0:T(4,128)} %copy.301), calls=%async_computation.2 | async-start | bytes 147456 | tf_op jit(solution)/shard_map/all_to_all | solution.py:138
  70.1 16.6 %all-to-all-start.3 = ((f32[4,2,1,4,4,128]{5,4,3,2,1,0:T(4,128)}), f32[4,2,1,4,4,128]{5,4,3,2,1,0:T(4,128)S(1)}, u32[]{:S(2)}, u32[]{:S(2)}) async-start(f32[4,2,1,4,4,128]{5,4,3,2,1,0:T(4,128)} %copy.306), calls=%async_computation.3 | async-start | bytes 131072 | tf_op jit(solution)/shard_map/all_to_all | solution.py:147
  88.3 11.2 %all-to-all-start.4 = ((f32[4,2,1,4,16,128]{5,4,3,2,1,0:T(8,128)}), f32[4,2,1,4,16,128]{5,4,3,2,1,0:T(8,128)S(1)}, u32[]{:S(2)}, u32[]{:S(2)}) async-start(f32[4,2,1,4,16,128]{5,4,3,2,1,0:T(8,128)} %copy.309), calls=%async_computation.4 | async-start | bytes 524288 | tf_op jit(solution)/shard_map/all_to_all | solution.py:153
  94.8 6.8 %copy-start = (bf16[4,256,256]{2,1,0:T(8,128)(2,1)}, bf16[4,256,256]{2,1,0:T(8,128)(2,1)S(1)}, u32[]{:S(2)}) copy-start(bf16[4,256,256]{2,1,0:T(8,128)(2,1)S(1)} %fusion.1) | copy-start | bytes 1572868
  99.7 3.6 %collective-permute-start.3 = (f32[2,1,4,64,128]{4,3,2,1,0:T(8,128)S(1)}, f32[2,1,4,64,128]{4,3,2,1,0:T(8,128)S(1)}, u32[]{:S(2)}, u32[]{:S(2)}) collective-permute-start(f32[2,1,4,64,128]{4,3,2,1,0:T(8,128)S(1)} %pad_maximum_fusion.3), channel_id=1, source_target_pairs={{0,16},{16,0},{1,17},{17,1},{2,18},{18,2},{3,19},{19,3},{4,20},{20... | collective-permute-start | bytes 786440 | tf_op jit(solution)/shard_map/ppermute | solution.py:155
  103.3 1.0 copy-start.2
  104.4 0.7 copy-start.3
  105.9 0.9 copy-start.4

commit v8 on v6

--- a/solution.py
+++ b/solution.py
@@ -189,7 +189,7 @@
 
 def solution(mesh):
     ctx_count, uly_count = mesh.shape["ctx"], mesh.shape["uly"]
-    inner = 4 if ctx_count % 8 == 0 else 1
+    inner = 8 if ctx_count % 16 == 0 else 1
     grid = mesh.devices.reshape(ctx_count // (2 * inner), inner, 2, uly_count)
     chips = Mesh(grid, ("zg", "zl", "core", "uly"))
     placed = (

time: 130 us -> 137 us (1.054)
  waiting for transfers between devices: 27.9 us -> 48.7 us
  starting transfers between devices: 56.1 us -> 42.6 us
    ppermute x3 -> x1, starting transfers between devices: 26 us -> 8.2 us  [local(): lax.ppermute(group_keep * entering_group + group_state, 'zg', upward)]
    all_to_all x1, waiting for transfers between devices: 7.2 us -> 17.1 us  [local(): got = lax.all_to_all(send, 'zl', 0, 0, tiled=True)]
    all_to_all x1, waiting for transfers between devices: 4.77 us -> 13 us  [local(): back = lax.all_to_all(mixed, 'zl', 0, 0, tiled=True)]
    all_to_all x1, starting transfers between devices: 6 us -> 12.6 us  [local(): got = lax.all_to_all(send, 'zl', 0, 0, tiled=True)]
    ppermute x3 -> x1, waiting for transfers between devices: 7.98 us -> 12.6 us  [local(): lax.ppermute(group_keep * leaving_group + group_grad, 'zg', downward)]
    ppermute x3 -> x1, starting transfers between devices: 3.85 us -> 1.29 us  [local(): lax.ppermute(group_keep * leaving_group + group_grad, 'zg', downward)]
    ppermute x3 -> x1, waiting for transfers between devices: 2 us -> 0.11 us  [local(): lax.ppermute(group_keep * entering_group + group_state, 'zg', upward)]
  transfers between devices with their start and end apart: 13 -> 9, of which waited for: 8 -> 6; matrix products, arithmetic and copies ran while one was open for 5% -> 4% of each run, Pallas kernels for 0% -> 0%
where the time goes in v8:
time: 137 us; the launch traced here: 136 us
  waiting for transfers between devices  48.7 us (36%)
  starting transfers between devices  42.6 us (31%)
  blocking collectives  21.2 us (15%)
  local copies, waits for them, and re-layouts  14.3 us (10%)
  matrix products  5.6 us (4%)
  other arithmetic  2.55 us (2%)
    all_to_all x1, blocking collectives, local(): outs = lax.all_to_all(outs, 'uly', 0, 0, tiled=True)  21.2 us
    all_to_all x1, waiting for transfers between devices, local(): got = lax.all_to_all(send, 'zl', 0, 0, tiled=True)  17.1 us
    all_to_all x1, waiting for transfers between devices, local(): back = lax.all_to_all(mixed, 'zl', 0, 0, tiled=True)  13 us
    all_to_all x1, starting transfers between devices, local(): got = lax.all_to_all(send, 'zl', 0, 0, tiled=True)  12.6 us
    ppermute x1, waiting for transfers between devices, local(): lax.ppermute(group_keep * leaving_group + group_grad, 'zg', downward)  12.6 us
    ppermute x1, starting transfers between devices, local(): lax.ppermute(group_keep * entering_group + group_state, 'zg', upward)  8.2 us
    all_to_all x1, starting transfers between devices, local(): g_parts = lax.all_to_all(g_parts, 'uly', 0, 0, tiled=True)  7.03 us
    ppermute x3, starting transfers between devices, local(): lax.ppermute((update, local_grad, last), 'core', pairs)  5.97 us
  transfers between devices with their start and end apart: 9, of which 6 were waited for; matrix products, arithmetic and copies ran while one was open for 4% of the time, Pallas kernels for 0%

profile of v8, /device:TPU:32, one launch (start us, length us, event | category | flops | bytes accessed | tf_op | source)
XLA Modules:
  0.0 136.1 jit_solution(6615364549671408943)
XLA Ops:
  0.6 0.7 reshape.493
  1.3 1.2 reduce-window.6
  2.6 0.1 copy.280
  3.0 1.9 %collective-permute-start = (f32[1,4]{1,0:T(1,128)S(1)}, f32[1,4]{1,0:T(1,128)S(1)}, u32[]{:S(2)}, u32[]{:S(2)}) collective-permute-start(f32[1,4]{1,0:T(1,128)S(1)} %get-tuple-element.22), channel_id=1, source_target_pairs={{0,16},{16,0},{1,17},{17,1},{2,18},{18,2},{3,19},{19,3},{4,20},{20... | collective-permute-start | bytes 56 | tf_op jit(solution)/shard_map/ppermute | solution.py:90
  5.0 0.9 copy.231
  5.9 7.0 %all-to-all-start = ((bf16[16,1,16,512]{3,2,1,0:T(8,128)(2,1)}), bf16[16,1,16,512]{3,2,1,0:T(8,128)(2,1)S(1)}, u32[]{:S(2)}, u32[]{:S(2)}) async-start(bf16[16,1,16,512]{3,2,1,0:T(8,128)(2,1)} %copy.231), calls=%async_computation | async-start | bytes 524288 | tf_op jit(solution)/shard_map/all_to_all | solution.py:71
  13.0 0.8 copy-done.6
  13.9 0.9 copy-done.7
  14.8 0.1 copy.284
  15.0 0.2 convolution_bitcast_fusion.8
  15.2 2.1 %collective-permute-start.1 = (f32[1,4,128,128]{3,2,1,0:T(8,128)S(1)}, f32[1,4,128,128]{3,2,1,0:T(8,128)S(1)}, u32[]{:S(2)}, u32[]{:S(2)}) collective-permute-start(f32[1,4,128,128]{3,2,1,0:T(8,128)S(1)} %convolution_bitcast_fusion.8), channel_id=1, source_target_pairs={{0,16},{16,0},{1,17},{17,1},{2,18},{18,2},{3,19},{19,3},{4,20},{20... | collective-permute-start | bytes 786440 | tf_op jit(solution)/shard_map/ppermute | solution.py:90
  17.5 4.6 %all-to-all-done = bf16[16,1,16,512]{3,2,1,0:T(8,128)(2,1)S(1)} async-done(((bf16[16,1,16,512]{3,2,1,0:T(8,128)(2,1)}), bf16[16,1,16,512]{3,2,1,0:T(8,128)(2,1)S(1)}, u32[]{:S(2)}, u32[]{:S(2)}) %all-to-all-start) | async-done | bytes 262176 | tf_op jit(solution)/shard_map/all_to_all | solution.py:71
  22.1 0.5 convolution_bitcast_fusion.7
  22.6 1.9 %collective-permute-start.2 = (f32[1,4,128,128]{3,2,1,0:T(8,128)S(1)}, f32[1,4,128,128]{3,2,1,0:T(8,128)S(1)}, u32[]{:S(2)}, u32[]{:S(2)}) collective-permute-start(f32[1,4,128,128]{3,2,1,0:T(8,128)S(1)} %convolution_bitcast_fusion.7), channel_id=1, source_target_pairs={{0,16},{16,0},{1,17},{17,1},{2,18},{18,2},{3,19},{19,3},{4,20},{20... | collective-permute-start | bytes 786440 | tf_op jit(solution)/shard_map/ppermute | solution.py:90
  24.7 1.4 %collective-permute-done.2 = f32[1,4,128,128]{3,2,1,0:T(8,128)S(1)} collective-permute-done((f32[1,4,128,128]{3,2,1,0:T(8,128)S(1)}, f32[1,4,128,128]{3,2,1,0:T(8,128)S(1)}, u32[]{:S(2)}, u32[]{:S(2)}) %collective-permute-start.2) | collective-permute-done | bytes 262176 | tf_op jit(solution)/shard_map/ppermute | solution.py:90
  26.2 0.6 copy-done.1
  26.9 0.9 copy.234
  27.8 12.6 %all-to-all-start.1 = ((f32[8,1,4,17,128]{4,2,3,1,0:T(4,128)}), f32[8,1,4,17,128]{4,2,3,1,0:T(4,128)S(1)}, u32[]{:S(2)}, u32[]{:S(2)}) async-start(f32[8,1,4,17,128]{4,2,3,1,0:T(4,128)} %copy.234), calls=%async_computation.1 | async-start | bytes 557056 | tf_op jit(solution)/shard_map/all_to_all | solution.py:116
  40.6 17.1 %all-to-all-done.1 = f32[8,1,4,17,128]{4,2,3,1,0:T(4,128)S(1)} async-done(((f32[8,1,4,17,128]{4,2,3,1,0:T(4,128)}), f32[8,1,4,17,128]{4,2,3,1,0:T(4,128)S(1)}, u32[]{:S(2)}, u32[]{:S(2)}) %all-to-all-start.1) | async-done | bytes 278560 | tf_op jit(solution)/shard_map/all_to_all | solution.py:116
  57.6 0.1 copy.282
  57.8 0.2 reduce_window_sum.58
  57.9 0.2 slice_reduce_fusion
  58.3 0.2 multiply_reduce_fusion
  58.6 8.2 %collective-permute-start.3 = (f32[1,4,8,128]{3,2,1,0:T(8,128)S(1)}, f32[1,4,8,128]{3,2,1,0:T(8,128)S(1)}, u32[]{:S(2)}, u32[]{:S(2)}) collective-permute-start(f32[1,4,8,128]{3,2,1,0:T(8,128)S(1)} %get-tuple-element.23), channel_id=1, source_target_pairs={{0,256},{1,257},{2,258},{3,259},{4,260},{5,261},{6,262},{7,263},{8... | collective-permute-start | bytes 49160 | tf_op jit(solution)/shard_map/ppermute | solution.py:137
  66.8 1.3 collective-permute-start.4
  68.1 0.1 collective-permute-done.3
  68.2 0.3 add_bitcast_fusion.1
  68.5 12.6 %collective-permute-done.4 = f32[1,4,8,128]{3,2,1,0:T(8,128)S(1)} collective-permute-done((f32[1,4,8,128]{3,2,1,0:T(8,128)S(1)}, f32[1,4,8,128]{3,2,1,0:T(8,128)S(1)}, u32[]{:S(2)}, u32[]{:S(2)}) %collective-permute-start.4) | collective-permute-done | bytes 16416 | tf_op jit(solution)/shard_map/ppermute | solution.py:138
  81.1 0.3 add_bitcast_fusion
  81.5 0.8 copy.238
  82.2 5.6 %all-to-all-start.2 = ((f32[8,2,1,4,8,128]{5,4,3,2,1,0:T(8,128)}), f32[8,2,1,4,8,128]{5,4,3,2,1,0:T(8,128)S(1)}, u32[]{:S(2)}, u32[]{:S(2)}) async-start(f32[8,2,1,4,8,128]{5,4,3,2,1,0:T(8,128)} %copy.238), calls=%async_computation.2 | async-start | bytes 524288 | tf_op jit(solution)/shard_map/all_to_all | solution.py:143
  87.8 0.4 fusion
  88.2 0.3 convolution_bitcast_fusion.6
  88.5 0.3 convolution_bitcast_fusion.1
  88.9 0.4 fusion.1
  89.3 13.0 %all-to-all-done.2 = f32[8,2,1,4,8,128]{5,4,3,2,1,0:T(8,128)S(1)} async-done(((f32[8,2,1,4,8,128]{5,4,3,2,1,0:T(8,128)}), f32[8,2,1,4,8,128]{5,4,3,2,1,0:T(8,128)S(1)}, u32[]{:S(2)}, u32[]{:S(2)}) %all-to-all-start.2) | async-done | bytes 262176 | tf_op jit(solution)/shard_map/all_to_all | solution.py:143
  102.3 1.9 %collective-permute-start.5 = (f32[2,1,4,64,128]{4,3,2,1,0:T(8,128)S(1)}, f32[2,1,4,64,128]{4,3,2,1,0:T(8,128)S(1)}, u32[]{:S(2)}, u32[]{:S(2)}) collective-permute-start(f32[2,1,4,64,128]{4,3,2,1,0:T(8,128)S(1)} %pad_maximum_fusion.3), channel_id=1, source_target_pairs={{0,16},{16,0},{1,17},{17,1},{2,18},{18,2},{3,19},{19,3},{4,20},{20... | collective-permute-start | bytes 786440 | tf_op jit(solution)/shard_map/ppermute | solution.py:145
  104.3 0.3 convolution_bitcast_fusion.3
  104.6 1.3 convolution_bitcast_fusion.5
  106.0 0.9 copy-done.2
  106.9 0.1 select_convert_fusion.1
  107.1 0.3 fusion.8
  107.4 0.3 copy-done.3
  107.7 0.2 copy.262
  107.9 0.1 stack.34
  108.0 0.3 fusion.12
  108.4 0.2 copy.243
  108.6 0.1 stack.31
  108.7 0.8 copy-done.4
  109.5 0.2 fusion.9
  109.7 0.2 fusion.10
  110.0 0.2 copy.250
  110.2 0.1 stack.32
  110.3 0.2 copy.256
  110.6 0.1 maximum_bitcast_fusion
  110.9 21.2 %all_to_all.20 = bf16[16,4,1,16,512]{4,3,2,1,0:T(8,128)(2,1)S(1)} all-to-all(bf16[16,4,1,16,512]{4,3,2,1,0:T(8,128)(2,1)S(1)} %copy.263), channel_id=1, replica_groups=mesh['zg'=2,'zl'=8,'core'=2,'uly'=16] {'uly'}, dimensions={0} | all-to-all | bytes 2097152 | tf_op jit(solution)/shard_map/all_to_all | solution.py:183
  132.1 0.2 copy.267
  132.3 0.8 squeeze.45
  133.1 0.1 copy.266
  133.3 0.8 squeeze.44
  134.1 0.1 copy.265
  134.3 0.8 squeeze.43
  135.1 0.1 copy.264
  135.2 0.8 squeeze.42
  (58 shorter events, 1.9 us)
Async XLA Ops:
  2.6 2.3 %copy-start.5 = (bf16[1,16,8192]{2,1,0:T(8,128)(2,1)S(1)}, bf16[1,16,8192]{2,1,0:T(8,128)(2,1)}, u32[]{:S(2)}) copy-start(bf16[1,16,8192]{2,1,0:T(8,128)(2,1)} %param.8) | copy-start | bytes 786436
  3.0 14.5 %collective-permute-start = (f32[1,4]{1,0:T(1,128)S(1)}, f32[1,4]{1,0:T(1,128)S(1)}, u32[]{:S(2)}, u32[]{:S(2)}) collective-permute-start(f32[1,4]{1,0:T(1,128)S(1)} %get-tuple-element.22), channel_id=1, source_target_pairs={{0,16},{16,0},{1,17},{17,1},{2,18},{18,2},{3,19},{19,3},{4,20},{20... | collective-permute-start | bytes 56 | tf_op jit(solution)/shard_map/ppermute | solution.py:90
  5.9 16.2 %all-to-all-start = ((bf16[16,1,16,512]{3,2,1,0:T(8,128)(2,1)}), bf16[16,1,16,512]{3,2,1,0:T(8,128)(2,1)S(1)}, u32[]{:S(2)}, u32[]{:S(2)}) async-start(bf16[16,1,16,512]{3,2,1,0:T(8,128)(2,1)} %copy.231), calls=%async_computation | async-start | bytes 524288 | tf_op jit(solution)/shard_map/all_to_all | solution.py:71
  12.9 1.0 copy-start.6
  13.9 0.9 copy-start.7
  14.9 2.4 %copy-start.8 = (bf16[1,256,512]{2,1,0:T(8,128)(2,1)S(1)}, bf16[1,256,512]{2,1,0:T(8,128)(2,1)}, u32[]{:S(2)}) copy-start(bf16[1,256,512]{2,1,0:T(8,128)(2,1)} %param.5) | copy-start | bytes 786436
  15.2 9.4 %collective-permute-start.1 = (f32[1,4,128,128]{3,2,1,0:T(8,128)S(1)}, f32[1,4,128,128]{3,2,1,0:T(8,128)S(1)}, u32[]{:S(2)}, u32[]{:S(2)}) collective-permute-start(f32[1,4,128,128]{3,2,1,0:T(8,128)S(1)} %convolution_bitcast_fusion.8), channel_id=1, source_target_pairs={{0,16},{16,0},{1,17},{17,1},{2,18},{18,2},{3,19},{19,3},{4,20},{20... | collective-permute-start | bytes 786440 | tf_op jit(solution)/shard_map/ppermute | solution.py:90
  22.6 3.4 %collective-permute-start.2 = (f32[1,4,128,128]{3,2,1,0:T(8,128)S(1)}, f32[1,4,128,128]{3,2,1,0:T(8,128)S(1)}, u32[]{:S(2)}, u32[]{:S(2)}) collective-permute-start(f32[1,4,128,128]{3,2,1,0:T(8,128)S(1)} %convolution_bitcast_fusion.7), channel_id=1, source_target_pairs={{0,16},{16,0},{1,17},{17,1},{2,18},{18,2},{3,19},{19,3},{4,20},{20... | collective-permute-start | bytes 786440 | tf_op jit(solution)/shard_map/ppermute | solution.py:90
  26.1 0.7 copy-start.1
  27.8 29.8 %all-to-all-start.1 = ((f32[8,1,4,17,128]{4,2,3,1,0:T(4,128)}), f32[8,1,4,17,128]{4,2,3,1,0:T(4,128)S(1)}, u32[]{:S(2)}, u32[]{:S(2)}) async-start(f32[8,1,4,17,128]{4,2,3,1,0:T(4,128)} %copy.234), calls=%async_computation.1 | async-start | bytes 557056 | tf_op jit(solution)/shard_map/all_to_all | solution.py:116
  58.6 9.6 %collective-permute-start.3 = (f32[1,4,8,128]{3,2,1,0:T(8,128)S(1)}, f32[1,4,8,128]{3,2,1,0:T(8,128)S(1)}, u32[]{:S(2)}, u32[]{:S(2)}) collective-permute-start(f32[1,4,8,128]{3,2,1,0:T(8,128)S(1)} %get-tuple-element.23), channel_id=1, source_target_pairs={{0,256},{1,257},{2,258},{3,259},{4,260},{5,261},{6,262},{7,263},{8... | collective-permute-start | bytes 49160 | tf_op jit(solution)/shard_map/ppermute | solution.py:137
  66.8 14.3 %collective-permute-start.4 = (f32[1,4,8,128]{3,2,1,0:T(8,128)S(1)}, f32[1,4,8,128]{3,2,1,0:T(8,128)S(1)}, u32[]{:S(2)}, u32[]{:S(2)}) collective-permute-start(f32[1,4,8,128]{3,2,1,0:T(8,128)S(1)} %get-tuple-element.24), channel_id=1, source_target_pairs={{256,0},{257,1},{258,2},{259,3},{260,4},{261,5},{262,6},{263,7},{2... | collective-permute-start | bytes 49160 | tf_op jit(solution)/shard_map/ppermute | solution.py:138
  82.2 20.0 %all-to-all-start.2 = ((f32[8,2,1,4,8,128]{5,4,3,2,1,0:T(8,128)}), f32[8,2,1,4,8,128]{5,4,3,2,1,0:T(8,128)S(1)}, u32[]{:S(2)}, u32[]{:S(2)}) async-start(f32[8,2,1,4,8,128]{5,4,3,2,1,0:T(8,128)} %copy.238), calls=%async_computation.2 | async-start | bytes 524288 | tf_op jit(solution)/shard_map/all_to_all | solution.py:143
  89.3 15.0 %copy-start = (bf16[4,256,256]{2,1,0:T(8,128)(2,1)}, bf16[4,256,256]{2,1,0:T(8,128)(2,1)S(1)}, u32[]{:S(2)}) copy-start(bf16[4,256,256]{2,1,0:T(8,128)(2,1)S(1)} %fusion.1) | copy-start | bytes 1572868
  102.3 3.6 %collective-permute-start.5 = (f32[2,1,4,64,128]{4,3,2,1,0:T(8,128)S(1)}, f32[2,1,4,64,128]{4,3,2,1,0:T(8,128)S(1)}, u32[]{:S(2)}, u32[]{:S(2)}) collective-permute-start(f32[2,1,4,64,128]{4,3,2,1,0:T(8,128)S(1)} %pad_maximum_fusion.3), channel_id=1, source_target_pairs={{0,16},{16,0},{1,17},{17,1},{2,18},{18,2},{3,19},{19,3},{4,20},{20... | collective-permute-start | bytes 786440 | tf_op jit(solution)/shard_map/ppermute | solution.py:145
  106.0 1.0 copy-start.2
  107.1 0.7 copy-start.3
  108.6 0.9 copy-start.4

commit v9 on v4

--- a/solution.py
+++ b/solution.py
@@ -99,30 +99,27 @@
     chip_update = keep_hi * update_lo + update_hi
     chip_grad = keep_lo * grad_hi + grad_lo
     half = width // 2
-    band = half // chip_count
 
     def my_half(state):
         return lax.dynamic_slice_in_dim(state, core * half, half, axis=2)
 
-    chip_last = jnp.broadcast_to((last_lo + last_hi)[..., None], (batch_count, head_count, width))
-    last_piece = jnp.broadcast_to(
-        chip_last[None, :, :, None, :], (chip_count, batch_count, head_count, 1, width)
-    )
-    send = jnp.concatenate(
-        [to_pieces(my_half(chip_update), chip_count), to_pieces(my_half(chip_grad), chip_count), last_piece],
-        axis=3,
-    )
-    got = lax.all_to_all(send, "z", 0, 0, tiled=True)
-    forward_w, backward_w = block_weights(got[:, :, :, 2 * band, 0])
-    mixed = jnp.stack(
-        [
-            mix_blocks(forward_w, got[:, :, :, :band]),
-            mix_blocks(backward_w, got[:, :, :, band : 2 * band]),
-        ],
-        axis=1,
-    )
-    back = lax.all_to_all(mixed, "z", 0, 0, tiled=True)
-    halves = jnp.stack([from_pieces(back[:, 0]), from_pieces(back[:, 1])])
+    chip_index = lax.axis_index("z")
+    chip_ids = lax.broadcasted_iota(jnp.int32, (chip_count, 1, 1), 0)
+    chip_last = jnp.broadcast_to((last_lo + last_hi)[..., None, None], (batch_count, head_count, 1, width))
+    states_all = lax.all_gather(jnp.concatenate([my_half(chip_update), chip_last], axis=2), "z")
+    lasts_all = states_all[:, :, :, half, 0]
+    inclusive = jnp.cumsum(lasts_all, axis=0)
+    exclusive = inclusive - lasts_all
+    earlier = chip_ids < chip_index
+    forward_gap = jnp.where(earlier, exclusive[chip_index][None] - inclusive, 0.0)
+    forward_w = jnp.where(earlier, jnp.exp(forward_gap), 0.0)[..., None, None]
+    state_half = jnp.sum(forward_w * states_all[:, :, :, :half], axis=0)
+    grads_all = lax.all_gather(my_half(chip_grad), "z")
+    later = chip_ids > chip_index
+    backward_gap = jnp.where(later, exclusive - inclusive[chip_index][None], 0.0)
+    backward_w = jnp.where(later, jnp.exp(backward_gap), 0.0)[..., None, None]
+    grad_half = jnp.sum(backward_w * grads_all, axis=0)
+    halves = jnp.stack([state_half, grad_half])
     other_halves = lax.ppermute(halves, "core", pairs)
     low_rows, high_rows = order(halves, other_halves)
     entering = jnp.concatenate([low_rows, high_rows], axis=3)

time: 124 us -> 215 us (1.73)
  waiting for transfers between devices: 41.6 us -> 102 us
  starting transfers between devices: 36.8 us -> 15.3 us
  other arithmetic: 2.08 us -> 22 us
  local copies, waits for them, and re-layouts: 14.4 us -> 29.7 us
  between operations: 1.16 us -> 14.4 us
  blocking collectives: 21.2 us -> 24.4 us
    all_gather x0 -> x2, waiting for transfers between devices: none -> 92.3 us  [the longest x1 52.9 us: local(): lax.all_gather(jnp.concatenate([my_half(chip_update), chip_last], axis=2)...]
    all_to_all x2 -> x0, waiting for transfers between devices: 35.6 us -> none  [the longest x1 19.1 us: local(): got = lax.all_to_all(send, 'z', 0, 0, tiled=True)]
    all_to_all x2 -> x0, starting transfers between devices: 21.9 us -> none  [the longest x1 15.2 us: local(): got = lax.all_to_all(send, 'z', 0, 0, tiled=True)]
    reduce_sum x0 -> x2, other arithmetic: none -> 16.5 us  [the longest x1 14.7 us: local(): state_half = jnp.sum(forward_w * states_all[:, :, :, :half], axis=0)]
    all_gather x0 -> x1, local copies, waits for them, and re-layouts: none -> 12.4 us  [local(): lax.all_gather(jnp.concatenate([my_half(chip_update), chip_last], axis=2)...]
    all_to_all x1, waiting for transfers between devices: 4.56 us -> 7.82 us  [local(): g_parts = lax.all_to_all(g_parts, 'uly', 0, 0, tiled=True)]
    all_to_all x1, blocking collectives: 21.2 us -> 24.4 us  [local(): outs = lax.all_to_all(outs, 'uly', 0, 0, tiled=True)]
    unnamed x19 -> x7, local copies, waits for them, and re-layouts: 4.43 us -> 1.49 us
  transfers between devices with their start and end apart: 7 -> 7, of which waited for: 4 -> 5; matrix products, arithmetic and copies ran while one was open for 5% -> 19% of each run, Pallas kernels for 0% -> 0%
where the time goes in v9:
time: 215 us; the launch traced here: 214 us
  waiting for transfers between devices  102 us (47%)
  local copies, waits for them, and re-layouts  29.7 us (14%)
  blocking collectives  24.4 us (11%)
  other arithmetic  22 us (10%)
  starting transfers between devices  15.3 us (7%)
  between operations  14.4 us (7%)
  matrix products  5.73 us (3%)
    all_gather x1, waiting for transfers between devices, local(): lax.all_gather(jnp.concatenate([my_half(chip_update), chip_last], axis=2)...  52.9 us
    all_gather x1, waiting for transfers between devices, local(): grads_all = lax.all_gather(my_half(chip_grad), 'z')  39.4 us
    all_to_all x1, blocking collectives, local(): outs = lax.all_to_all(outs, 'uly', 0, 0, tiled=True)  24.4 us
    reduce_sum x1, other arithmetic, local(): state_half = jnp.sum(forward_w * states_all[:, :, :, :half], axis=0)  14.7 us
    all_gather x1, local copies, waits for them, and re-layouts, local(): lax.all_gather(jnp.concatenate([my_half(chip_update), chip_last], axis=2)...  12.4 us
    all_to_all x1, waiting for transfers between devices, local(): g_parts = lax.all_to_all(g_parts, 'uly', 0, 0, tiled=True)  7.82 us
    all_to_all x1, starting transfers between devices, local(): g_parts = lax.all_to_all(g_parts, 'uly', 0, 0, tiled=True)  7.03 us
    ppermute x3, starting transfers between devices, local(): lax.ppermute((update, local_grad, last), 'core', pairs)  6.25 us
  transfers between devices with their start and end apart: 7, of which 5 were waited for; matrix products, arithmetic and copies ran while one was open for 19% of the time, Pallas kernels for 0%

profile of v9, /device:TPU:32, one launch (start us, length us, event | category | flops | bytes accessed | tf_op | source)
XLA Modules:
  0.0 214.0 jit_solution(3144175026568393646)
XLA Ops:
  7.2 0.7 reshape.495
  7.9 1.2 reduce-window.6
  9.2 0.1 copy.293
  9.3 0.1 copy.236
  9.6 1.1 copy.294
  10.7 1.0 reshape.500
  11.8 0.2 convolution_bitcast_fusion.8
  12.0 1.9 collective-permute-start.1
  13.9 2.4 %collective-permute-start = (f32[1,4]{1,0:T(1,128)S(1)}, f32[1,4]{1,0:T(1,128)S(1)}, u32[]{:S(2)}, u32[]{:S(2)}) collective-permute-start(f32[1,4]{1,0:T(1,128)S(1)} %get-tuple-element.18), channel_id=1, source_target_pairs={{0,16},{16,0},{1,17},{17,1},{2,18},{18,2},{3,19},{19,3},{4,20},{20... | collective-permute-start | bytes 56 | tf_op jit(solution)/shard_map/ppermute | solution.py:89
  16.3 0.8 collective-permute-done
  17.2 0.1 fusion.33
  17.3 0.4 copy-done.1
  17.8 0.7 copy.243
  18.5 1.0 copy.296
  19.6 0.9 copy.253
  20.4 7.0 %all-to-all-start = ((bf16[16,1,16,512]{3,2,1,0:T(8,128)(2,1)}), bf16[16,1,16,512]{3,2,1,0:T(8,128)(2,1)S(1)}, u32[]{:S(2)}, u32[]{:S(2)}) async-start(bf16[16,1,16,512]{3,2,1,0:T(8,128)(2,1)} %copy.253), calls=%async_computation | async-start | bytes 524288 | tf_op jit(solution)/shard_map/all_to_all | solution.py:71
  27.6 1.0 reshape.493
  28.6 7.8 %all-to-all-done = bf16[16,1,16,512]{3,2,1,0:T(8,128)(2,1)S(1)} async-done(((bf16[16,1,16,512]{3,2,1,0:T(8,128)(2,1)}), bf16[16,1,16,512]{3,2,1,0:T(8,128)(2,1)S(1)}, u32[]{:S(2)}, u32[]{:S(2)}) %all-to-all-start) | async-done | bytes 262176 | tf_op jit(solution)/shard_map/all_to_all | solution.py:71
  36.5 0.5 convolution_bitcast_fusion.7
  37.0 1.9 collective-permute-start.2
  39.0 1.5 collective-permute-done.2
  40.5 0.7 fusion.32
  41.4 0.5 iota_compare_fusion.1
  42.0 0.4 fusion.2
  42.4 0.3 convolution_bitcast_fusion.6
  42.7 0.4 fusion.3
  43.1 0.3 convolution_bitcast_fusion.5
  43.4 52.9 %all-gather.5.cloned.1.call-done = f32[16,4,65,128]{3,1,2,0:T(4,128)} async-done(((f32[1,4,65,128]{3,1,2,0:T(4,128)}), f32[16,4,65,128]{3,1,2,0:T(4,128)}) %all-gather.5.cloned.1.call-update) | async-done | bytes 2129936 | tf_op jit(solution)/shard_map/all_gather | solution.py:109
  96.2 12.4 %copy.244 = f32[16,4,65,128]{0,1,3,2:T(4,128)} copy(f32[16,4,65,128]{3,1,2,0:T(4,128)} %all-gather.5.cloned.1.call-done) | data formatting | bytes 4259840 | tf_op jit(solution)/shard_map/all_gather | solution.py:109
  108.6 0.7 slice_bitcast_fusion
  109.3 0.1 copy.245
  109.6 14.7 %fusion = f32[4,64,128]{0,2,1:T(8,128)} fusion(f32[16,1,4,65,128]{0,2,4,3,1:T(4,128)} %bitcast.181, f32[16,4]{0,1:T(4,128)S(1)} %fusion.43), kind=kLoop, calls=%fused_computation.1 | loop fusion | flops 1015808 | bytes 2228480 | tf_op jit(solution)/shard_map/reduce_sum | solution.py:116
  124.2 2.9 %copy.248 = f32[4,64,128]{2,1,0:T(8,128)S(1)} copy(f32[4,64,128]{0,2,1:T(8,128)} %fusion) | data formatting | bytes 262144 | tf_op jit(solution)/shard_map/reduce_sum | solution.py:116
  127.1 1.3 fusion.40
  128.4 0.8 copy.250
  129.2 39.4 %all-gather.7.cloned.1.call-done = f32[16,4,64,128]{3,2,1,0:T(8,128)} async-done(((f32[1,4,64,128]{3,2,1,0:T(8,128)}), f32[16,4,64,128]{3,2,1,0:T(8,128)}) %all-gather.7.cloned.1.call-update) | async-done | bytes 2097168 | tf_op jit(solution)/shard_map/all_gather | solution.py:117
  168.6 1.8 fusion.1
  170.5 1.9 collective-permute-start.3
  172.4 1.2 convolution_bitcast_fusion.3
  173.5 0.3 convolution_bitcast_fusion.1
  174.0 1.1 select_convert_fusion.1
  175.1 0.2 fusion.12
  175.3 0.2 copy.265
  175.5 0.1 stack.28
  175.6 0.3 fusion.14
  176.0 0.2 copy.258
  176.2 0.1 stack.27
  176.3 1.3 fusion.11
  177.6 0.2 copy.271
  177.8 0.1 stack.29
  177.9 0.3 fusion.10
  178.2 0.2 copy.277
  178.4 0.1 stack.30
  178.5 0.1 maximum_bitcast_fusion
  178.7 0.1 copy.278
  178.8 24.4 %all_to_all.10 = bf16[16,4,1,16,512]{4,3,2,1,0:T(8,128)(2,1)S(1)} all-to-all(bf16[16,4,1,16,512]{4,3,2,1,0:T(8,128)(2,1)S(1)} %copy.278), channel_id=1, replica_groups=mesh['z'=16,'core'=2,'uly'=16] {'uly'}, dimensions={0} | all-to-all | bytes 2097152 | tf_op jit(solution)/shard_map/all_to_all | solution.py:161
  203.2 0.2 copy.279
  203.4 0.8 squeeze.30
  204.2 0.1 copy.280
  204.4 0.8 squeeze.31
  205.2 0.1 copy.281
  205.4 0.8 squeeze.32
  206.2 0.1 copy.282
  206.3 0.8 squeeze.33
  (37 shorter events, 1.1 us)
Async XLA Ops:
  7.2 89.1 %all-gather.5.cloned.1.call-start = ((), (), s32[]{:S(2)}) async-start(), calls=%async_computation.2 | async-start | bytes 2263040 | tf_op jit(solution)/shard_map/all_gather | solution.py:109
  12.0 5.2 %collective-permute-start.1 = (f32[1,4,128,128]{3,2,1,0:T(8,128)S(1)}, f32[1,4,128,128]{3,2,1,0:T(8,128)S(1)}, u32[]{:S(2)}, u32[]{:S(2)}) collective-permute-start(f32[1,4,128,128]{3,2,1,0:T(8,128)S(1)} %convolution_bitcast_fusion.8), channel_id=1, source_target_pairs={{0,16},{16,0},{1,17},{17,1},{2,18},{18,2},{3,19},{19,3},{4,20},{20... | collective-permute-start | bytes 786440 | tf_op jit(solution)/shard_map/ppermute | solution.py:89
  13.9 3.2 %collective-permute-start = (f32[1,4]{1,0:T(1,128)S(1)}, f32[1,4]{1,0:T(1,128)S(1)}, u32[]{:S(2)}, u32[]{:S(2)}) collective-permute-start(f32[1,4]{1,0:T(1,128)S(1)} %get-tuple-element.18), channel_id=1, source_target_pairs={{0,16},{16,0},{1,17},{17,1},{2,18},{18,2},{3,19},{19,3},{4,20},{20... | collective-permute-start | bytes 56 | tf_op jit(solution)/shard_map/ppermute | solution.py:89
  17.1 0.6 copy-start.1
  17.1 24.2 %copy-start.2 = (f32[4]{0:T(128)}, f32[4]{0:T(128)S(1)}, u32[]{:S(2)}) copy-start(f32[4]{0:T(128)S(1)} %get-tuple-element.16) | copy-start | bytes 52
  20.4 16.0 %all-to-all-start = ((bf16[16,1,16,512]{3,2,1,0:T(8,128)(2,1)}), bf16[16,1,16,512]{3,2,1,0:T(8,128)(2,1)S(1)}, u32[]{:S(2)}, u32[]{:S(2)}) async-start(bf16[16,1,16,512]{3,2,1,0:T(8,128)(2,1)} %copy.253), calls=%async_computation | async-start | bytes 524288 | tf_op jit(solution)/shard_map/all_to_all | solution.py:71
  27.5 141.1 %all-gather.7.cloned.1.call-start = ((), (), s32[]{:S(2)}) async-start(), calls=%async_computation.3 | async-start | bytes 2228224 | tf_op jit(solution)/shard_map/all_gather | solution.py:117
  37.0 3.4 %collective-permute-start.2 = (f32[1,4,128,128]{3,2,1,0:T(8,128)S(1)}, f32[1,4,128,128]{3,2,1,0:T(8,128)S(1)}, u32[]{:S(2)}, u32[]{:S(2)}) collective-permute-start(f32[1,4,128,128]{3,2,1,0:T(8,128)S(1)} %convolution_bitcast_fusion.7), channel_id=1, source_target_pairs={{0,16},{16,0},{1,17},{17,1},{2,18},{18,2},{3,19},{19,3},{4,20},{20... | collective-permute-start | bytes 786440 | tf_op jit(solution)/shard_map/ppermute | solution.py:89
  40.5 1.5 copy-start
  170.5 3.4 %collective-permute-start.3 = (f32[2,1,4,64,128]{4,3,2,1,0:T(8,128)S(1)}, f32[2,1,4,64,128]{4,3,2,1,0:T(8,128)S(1)}, u32[]{:S(2)}, u32[]{:S(2)}) collective-permute-start(f32[2,1,4,64,128]{4,3,2,1,0:T(8,128)S(1)} %pad_maximum_fusion.1), channel_id=1, source_target_pairs={{0,16},{16,0},{1,17},{17,1},{2,18},{18,2},{3,19},{19,3},{4,20},{20... | collective-permute-start | bytes 786440 | tf_op jit(solution)/shard_map/ppermute | solution.py:123
Sparse Core Ops, SparseCore 0:
  18.7 77.5 all-gather.4
  98.9 69.6 all-gather.6

commit v10 on v4

--- a/solution.py
+++ b/solution.py
@@ -86,7 +86,11 @@
     second = core == 1
     pairs = [(0, 1), (1, 0)]
     last = last_cum[..., 0]
-    other_update, other_grad, other_last = lax.ppermute((update, local_grad, last), "core", pairs)
+    last_row = jnp.broadcast_to(last[..., None, None], (batch_count, head_count, 1, width))
+    other_packed = lax.ppermute(jnp.concatenate([update, last_row], axis=2), "core", pairs)
+    other_update = other_packed[:, :, :width]
+    other_last = other_packed[:, :, width, 0]
+    other_grad = lax.ppermute(local_grad, "core", pairs)
 
     def order(mine, other):
         return jnp.where(second, other, mine), jnp.where(second, mine, other)
@@ -162,10 +166,13 @@
     outs = outs.reshape(4, batch_count, uly_count, positions // uly_count, width_heads)
     outs = jnp.transpose(outs, (2, 0, 1, 3, 4))
     outs = lax.all_to_all(outs, "uly", 0, 0, tiled=True)
-    outs = jnp.transpose(outs, (1, 2, 3, 0, 4)).reshape(
-        4, batch_count, positions // uly_count, uly_count * width_heads
-    )
-    return (outs[0], outs[1], outs[2], outs[3])
+
+    def to_tokens(index):
+        return jnp.transpose(outs[:, index], (1, 2, 0, 3)).reshape(
+            batch_count, positions // uly_count, uly_count * width_heads
+        )
+
+    return (to_tokens(0), to_tokens(1), to_tokens(2), to_tokens(3))
 
 
 def solution(mesh):

time: 124 us -> 121 us (0.976)
  waiting for transfers between devices: 41.6 us -> 39 us
  blocking collectives: 21.2 us -> 23.1 us
  starting transfers between devices: 36.8 us -> 35 us
    squeeze x4 -> x1, local copies, waits for them, and re-layouts: 3.31 us -> 0.09 us  [local(): last = last_cum[..., 0]]
    all_to_all x1, waiting for transfers between devices: 4.56 us -> 2.18 us  [local(): g_parts = lax.all_to_all(g_parts, 'uly', 0, 0, tiled=True)]
    reshape x1 -> x5, local copies, waits for them, and re-layouts: 0.7 us -> 2.89 us  [the longest x4 2.88 us: to_tokens(): jnp.transpose(outs[:, index], (1, 2, 0, 3))]
    ppermute x3 -> x2, starting transfers between devices: 5.97 us -> 3.97 us  [the longest x1 2.05 us: local(): lax.ppermute(jnp.concatenate([update, last_row], axis=2), 'core', pairs)]
    all_to_all x1, blocking collectives: 21.2 us -> 23.1 us  [local(): outs = lax.all_to_all(outs, 'uly', 0, 0, tiled=True)]
    unnamed x19 -> x20, local copies, waits for them, and re-layouts: 4.43 us -> 5.44 us
  transfers between devices with their start and end apart: 7 -> 6, of which waited for: 4 -> 4; matrix products, arithmetic and copies ran while one was open for 5% -> 5% of each run, Pallas kernels for 0% -> 0%
where the time goes in v10:
time: 121 us; the launch traced here: 120 us
  waiting for transfers between devices  39 us (32%)
  starting transfers between devices  35 us (29%)
  blocking collectives  23.1 us (19%)
  local copies, waits for them, and re-layouts  13.8 us (11%)
  matrix products  5.57 us (5%)
  other arithmetic  2.24 us (2%)
    all_to_all x1, blocking collectives, local(): outs = lax.all_to_all(outs, 'uly', 0, 0, tiled=True)  23.1 us
    all_to_all x1, waiting for transfers between devices, local(): got = lax.all_to_all(send, 'z', 0, 0, tiled=True)  19.1 us
    all_to_all x1, waiting for transfers between devices, local(): back = lax.all_to_all(mixed, 'z', 0, 0, tiled=True)  16.6 us
    all_to_all x1, starting transfers between devices, local(): got = lax.all_to_all(send, 'z', 0, 0, tiled=True)  15.2 us
    all_to_all x1, starting transfers between devices, local(): g_parts = lax.all_to_all(g_parts, 'uly', 0, 0, tiled=True)  7.17 us
    all_to_all x1, starting transfers between devices, local(): back = lax.all_to_all(mixed, 'z', 0, 0, tiled=True)  6.68 us
    unnamed x20, local copies, waits for them, and re-layouts  5.44 us
    reshape x4, local copies, waits for them, and re-layouts, to_tokens(): jnp.transpose(outs[:, index], (1, 2, 0, 3))  2.88 us
  transfers between devices with their start and end apart: 6, of which 4 were waited for; matrix products, arithmetic and copies ran while one was open for 5% of the time, Pallas kernels for 0%

profile of v10, /device:TPU:32, one launch (start us, length us, event | category | flops | bytes accessed | tf_op | source)
XLA Modules:
  0.0 119.9 jit_solution(7274016591886273640)
XLA Ops:
  0.6 1.0 copy.322
  1.7 0.9 copy.260
  2.5 7.2 %all-to-all-start = ((bf16[16,1,16,512]{3,2,1,0:T(8,128)(2,1)}), bf16[16,1,16,512]{3,2,1,0:T(8,128)(2,1)S(1)}, u32[]{:S(2)}, u32[]{:S(2)}) async-start(bf16[16,1,16,512]{3,2,1,0:T(8,128)(2,1)} %copy.260), calls=%async_computation | async-start | bytes 524288 | tf_op jit(solution)/shard_map/all_to_all | solution.py:71
  9.7 1.2 %reduce-window.6 = f32[1,4,2,128]{3,2,1,0:T(2,128)S(1)} reduce-window(f32[1,4,2,128]{3,2,1,0:T(2,128)S(1)} %reshape.454, f32[]{:T(128)} %constant.7.clone.1), window={size=1x1x1x128 pad=0_0x0_0x0_0x127_0}, to_apply=%region_0.0 | reduce-window | flops 130048 | bytes 8196 | tf_op jit(solution)/shard_map/reduce-window
  11.0 0.1 copy.313
  11.2 0.1 copy.249
  11.5 0.8 copy-done.5
  12.4 0.9 copy-done.6
  13.3 0.1 copy.316
  13.4 0.2 convolution_bitcast_fusion.8
  13.7 2.1 %collective-permute-start = (f32[1,4,129,128]{3,2,1,0:T(8,128)S(1)}, f32[1,4,129,128]{3,2,1,0:T(8,128)S(1)}, u32[]{:S(2)}, u32[]{:S(2)}) collective-permute-start(f32[1,4,129,128]{3,2,1,0:T(8,128)S(1)} %pad_maximum_fusion.1), channel_id=1, source_target_pairs={{0,16},{16,0},{1,17},{17,1},{2,18},{18,2},{3,19},{19,3},{4,20},{20... | collective-permute-start | bytes 792584 | tf_op jit(solution)/shard_map/ppermute | solution.py:90
  15.9 0.1 copy.256
  16.1 2.2 %all-to-all-done = bf16[16,1,16,512]{3,2,1,0:T(8,128)(2,1)S(1)} async-done(((bf16[16,1,16,512]{3,2,1,0:T(8,128)(2,1)}), bf16[16,1,16,512]{3,2,1,0:T(8,128)(2,1)S(1)}, u32[]{:S(2)}, u32[]{:S(2)}) %all-to-all-start) | async-done | bytes 262176 | tf_op jit(solution)/shard_map/all_to_all | solution.py:71
  18.3 0.5 convolution_bitcast_fusion.7
  18.8 1.9 %collective-permute-start.1 = (f32[1,4,128,128]{3,2,1,0:T(8,128)S(1)}, f32[1,4,128,128]{3,2,1,0:T(8,128)S(1)}, u32[]{:S(2)}, u32[]{:S(2)}) collective-permute-start(f32[1,4,128,128]{3,2,1,0:T(8,128)S(1)} %convolution_bitcast_fusion.7), channel_id=1, source_target_pairs={{0,16},{16,0},{1,17},{17,1},{2,18},{18,2},{3,19},{19,3},{4,20},{20... | collective-permute-start | bytes 786440 | tf_op jit(solution)/shard_map/ppermute | solution.py:93
  20.8 0.1 fusion.54
  20.9 0.1 fusion.31
  21.0 1.2 %collective-permute-done.1 = f32[1,4,128,128]{3,2,1,0:T(8,128)S(1)} collective-permute-done((f32[1,4,128,128]{3,2,1,0:T(8,128)S(1)}, f32[1,4,128,128]{3,2,1,0:T(8,128)S(1)}, u32[]{:S(2)}, u32[]{:S(2)}) %collective-permute-start.1) | collective-permute-done | bytes 262176 | tf_op jit(solution)/shard_map/ppermute | solution.py:93
  22.3 0.1 fusion.30
  22.4 0.6 copy-done.1
  23.0 0.1 broadcast_in_dim_broadcast_in_dim_broadcast_in_dim.2
  23.1 0.1 pad_maximum_fusion
  23.2 0.9 copy.263
  24.1 15.2 %all-to-all-start.1 = ((f32[16,1,4,9,128]{4,2,3,1,0:T(4,128)}), f32[16,1,4,9,128]{4,2,3,1,0:T(4,128)S(1)}, u32[]{:S(2)}, u32[]{:S(2)}) async-start(f32[16,1,4,9,128]{4,2,3,1,0:T(4,128)} %copy.263), calls=%async_computation.1 | async-start | bytes 589824 | tf_op jit(solution)/shard_map/all_to_all | solution.py:119
  39.4 19.1 %all-to-all-done.1 = f32[16,1,4,9,128]{4,2,3,1,0:T(4,128)S(1)} async-done(((f32[16,1,4,9,128]{4,2,3,1,0:T(4,128)}), f32[16,1,4,9,128]{4,2,3,1,0:T(4,128)S(1)}, u32[]{:S(2)}, u32[]{:S(2)}) %all-to-all-start.1) | async-done | bytes 294944 | tf_op jit(solution)/shard_map/all_to_all | solution.py:119
  58.5 0.1 copy.265
  58.6 0.1 copy.266
  58.7 0.1 copy.268
  58.9 0.3 convolution_bitcast_fusion.9
  59.2 0.3 convolution_bitcast_fusion.10
  59.6 0.8 copy.271
  60.4 6.7 %all-to-all-start.2 = ((f32[16,2,1,4,4,128]{5,4,3,2,1,0:T(4,128)}), f32[16,2,1,4,4,128]{5,4,3,2,1,0:T(4,128)S(1)}, u32[]{:S(2)}, u32[]{:S(2)}) async-start(f32[16,2,1,4,4,128]{5,4,3,2,1,0:T(4,128)} %copy.271), calls=%async_computation.2 | async-start | bytes 524288 | tf_op jit(solution)/shard_map/all_to_all | solution.py:128
  67.1 0.4 fusion
  67.5 0.3 convolution_bitcast_fusion.6
  67.8 0.3 convolution_bitcast_fusion.1
  68.1 0.4 fusion.1
  68.6 16.6 %all-to-all-done.2 = f32[16,2,1,4,4,128]{5,4,3,2,1,0:T(4,128)S(1)} async-done(((f32[16,2,1,4,4,128]{5,4,3,2,1,0:T(4,128)}), f32[16,2,1,4,4,128]{5,4,3,2,1,0:T(4,128)S(1)}, u32[]{:S(2)}, u32[]{:S(2)}) %all-to-all-start.2) | async-done | bytes 262176 | tf_op jit(solution)/shard_map/all_to_all | solution.py:128
  85.3 1.9 %collective-permute-start.2 = (f32[2,1,4,64,128]{4,3,2,1,0:T(8,128)S(1)}, f32[2,1,4,64,128]{4,3,2,1,0:T(8,128)S(1)}, u32[]{:S(2)}, u32[]{:S(2)}) collective-permute-start(f32[2,1,4,64,128]{4,3,2,1,0:T(8,128)S(1)} %pad_maximum_fusion.4), channel_id=1, source_target_pairs={{0,16},{16,0},{1,17},{17,1},{2,18},{18,2},{3,19},{19,3},{4,20},{20... | collective-permute-start | bytes 786440 | tf_op jit(solution)/shard_map/ppermute | solution.py:130
  87.2 0.3 convolution_bitcast_fusion.3
  87.5 1.3 %convolution_bitcast_fusion.5 = f32[1,256,4,128]{3,1,2,0:T(8,128)S(1)} fusion(bf16[4,256,256]{2,1,0:T(8,128)(2,1)} %copy-done, bf16[256,4,128]{0,2,1:T(8,128)(2,1)S(1)} %bitcast.202), kind=kOutput, calls=%fused_computation.9 | convolution fusion | flops 67108864 | bytes 1310720 | tf_op jit(solution)/shard_map/bhij,bjhd->bihd/dot_general | solution.py:146
  89.0 0.9 copy-done.2
  89.8 0.1 select_convert_fusion.1
  90.0 0.3 fusion.8
  90.3 0.3 copy-done.3
  90.6 0.2 copy.295
  90.9 0.1 stack.34
  91.0 0.3 fusion.12
  91.3 0.2 copy.276
  91.5 0.1 stack.31
  91.6 0.8 copy-done.4
  92.4 0.2 fusion.9
  92.7 0.2 fusion.10
  92.9 0.2 copy.283
  93.1 0.1 stack.32
  93.2 0.2 copy.289
  93.4 0.1 stack.33
  93.5 0.1 maximum_bitcast_fusion
  93.7 0.1 copy.296
  93.8 23.1 %all_to_all.20 = bf16[16,4,1,16,512]{4,3,2,1,0:T(8,128)(2,1)S(1)} all-to-all(bf16[16,4,1,16,512]{4,3,2,1,0:T(8,128)(2,1)S(1)} %copy.296), channel_id=1, replica_groups=mesh['z'=16,'core'=2,'uly'=16] {'uly'}, dimensions={0} | all-to-all | bytes 2097152 | tf_op jit(solution)/shard_map/all_to_all | solution.py:168
  116.9 0.1 slice_bitcast_fusion
  117.0 0.7 copy.320
  117.7 0.7 copy.319
  118.4 0.7 copy.318
  119.1 0.7 copy.317
  (49 shorter events, 1.2 us)
Async XLA Ops:
  2.5 7.2 %copy-start.8 = (f32[1,4,256]{2,1,0:T(4,128)S(1)}, f32[1,4,256]{2,1,0:T(4,128)}, u32[]{:S(2)}) copy-start(f32[1,4,256]{2,1,0:T(4,128)} %param.9) | copy-start | bytes 12292
  2.5 15.7 %all-to-all-start = ((bf16[16,1,16,512]{3,2,1,0:T(8,128)(2,1)}), bf16[16,1,16,512]{3,2,1,0:T(8,128)(2,1)S(1)}, u32[]{:S(2)}, u32[]{:S(2)}) async-start(bf16[16,1,16,512]{3,2,1,0:T(8,128)(2,1)} %copy.260), calls=%async_computation | async-start | bytes 524288 | tf_op jit(solution)/shard_map/all_to_all | solution.py:71
  11.4 1.0 copy-start.5
  12.3 0.9 copy-start.6
  13.7 2.3 %copy-start.7 = (bf16[1,256,512]{2,1,0:T(8,128)(2,1)S(1)}, bf16[1,256,512]{2,1,0:T(8,128)(2,1)}, u32[]{:S(2)}) copy-start(bf16[1,256,512]{2,1,0:T(8,128)(2,1)} %param.5) | copy-start | bytes 786436
  13.7 7.0 %collective-permute-start = (f32[1,4,129,128]{3,2,1,0:T(8,128)S(1)}, f32[1,4,129,128]{3,2,1,0:T(8,128)S(1)}, u32[]{:S(2)}, u32[]{:S(2)}) collective-permute-start(f32[1,4,129,128]{3,2,1,0:T(8,128)S(1)} %pad_maximum_fusion.1), channel_id=1, source_target_pairs={{0,16},{16,0},{1,17},{17,1},{2,18},{18,2},{3,19},{19,3},{4,20},{20... | collective-permute-start | bytes 792584 | tf_op jit(solution)/shard_map/ppermute | solution.py:90
  18.8 3.4 %collective-permute-start.1 = (f32[1,4,128,128]{3,2,1,0:T(8,128)S(1)}, f32[1,4,128,128]{3,2,1,0:T(8,128)S(1)}, u32[]{:S(2)}, u32[]{:S(2)}) collective-permute-start(f32[1,4,128,128]{3,2,1,0:T(8,128)S(1)} %convolution_bitcast_fusion.7), channel_id=1, source_target_pairs={{0,16},{16,0},{1,17},{17,1},{2,18},{18,2},{3,19},{19,3},{4,20},{20... | collective-permute-start | bytes 786440 | tf_op jit(solution)/shard_map/ppermute | solution.py:93
  22.3 0.7 copy-start.1
  24.1 34.4 %all-to-all-start.1 = ((f32[16,1,4,9,128]{4,2,3,1,0:T(4,128)}), f32[16,1,4,9,128]{4,2,3,1,0:T(4,128)S(1)}, u32[]{:S(2)}, u32[]{:S(2)}) async-start(f32[16,1,4,9,128]{4,2,3,1,0:T(4,128)} %copy.263), calls=%async_computation.1 | async-start | bytes 589824 | tf_op jit(solution)/shard_map/all_to_all | solution.py:119
  60.4 24.8 %all-to-all-start.2 = ((f32[16,2,1,4,4,128]{5,4,3,2,1,0:T(4,128)}), f32[16,2,1,4,4,128]{5,4,3,2,1,0:T(4,128)S(1)}, u32[]{:S(2)}, u32[]{:S(2)}) async-start(f32[16,2,1,4,4,128]{5,4,3,2,1,0:T(4,128)} %copy.271), calls=%async_computation.2 | async-start | bytes 524288 | tf_op jit(solution)/shard_map/all_to_all | solution.py:128
  68.5 18.6 %copy-start = (bf16[4,256,256]{2,1,0:T(8,128)(2,1)}, bf16[4,256,256]{2,1,0:T(8,128)(2,1)S(1)}, u32[]{:S(2)}) copy-start(bf16[4,256,256]{2,1,0:T(8,128)(2,1)S(1)} %fusion.1) | copy-start | bytes 1572868
  85.3 3.6 %collective-permute-start.2 = (f32[2,1,4,64,128]{4,3,2,1,0:T(8,128)S(1)}, f32[2,1,4,64,128]{4,3,2,1,0:T(8,128)S(1)}, u32[]{:S(2)}, u32[]{:S(2)}) collective-permute-start(f32[2,1,4,64,128]{4,3,2,1,0:T(8,128)S(1)} %pad_maximum_fusion.4), channel_id=1, source_target_pairs={{0,16},{16,0},{1,17},{17,1},{2,18},{18,2},{3,19},{19,3},{4,20},{20... | collective-permute-start | bytes 786440 | tf_op jit(solution)/shard_map/ppermute | solution.py:130
  88.9 1.0 copy-start.2
  90.0 0.7 copy-start.3
  91.5 0.9 copy-start.4

commit v11 on v10

--- a/solution.py
+++ b/solution.py
@@ -125,7 +125,7 @@
         ],
         axis=1,
     )
-    back = lax.all_to_all(mixed, "z", 0, 0, tiled=True)
+    back = lax.all_to_all(mixed.astype(jnp.bfloat16), "z", 0, 0, tiled=True)
     halves = jnp.stack([from_pieces(back[:, 0]), from_pieces(back[:, 1])])
     other_halves = lax.ppermute(halves, "core", pairs)
     low_rows, high_rows = order(halves, other_halves)

time: 121 us -> 115 us (0.950)
  waiting for transfers between devices: 39 us -> 34.8 us
    all_to_all x1, waiting for transfers between devices: 16.6 us -> 12.6 us  [local(): back = lax.all_to_all(mixed.astype(jnp.bfloat16), 'z', 0, 0, tiled=True)]
    unnamed x20 -> x26, local copies, waits for them, and re-layouts: 5.44 us -> 5.83 us
  transfers between devices with their start and end apart: 6 -> 6, of which waited for: 4 -> 5; matrix products, arithmetic and copies ran while one was open for 5% -> 5% of each run, Pallas kernels for 0% -> 0%
where the time goes in v11:
time: 115 us
  starting transfers between devices  35.1 us (31%)
  waiting for transfers between devices  34.8 us (30%)
  blocking collectives  22.6 us (20%)
  local copies, waits for them, and re-layouts  14.1 us (12%)
  matrix products  4.54 us (4%)
  other arithmetic  2.25 us (2%)
    all_to_all x1, blocking collectives, local(): outs = lax.all_to_all(outs, 'uly', 0, 0, tiled=True)  22.6 us
    all_to_all x1, waiting for transfers between devices, local(): got = lax.all_to_all(send, 'z', 0, 0, tiled=True)  18.3 us
    all_to_all x1, starting transfers between devices, local(): got = lax.all_to_all(send, 'z', 0, 0, tiled=True)  15.2 us
    all_to_all x1, waiting for transfers between devices, local(): back = lax.all_to_all(mixed.astype(jnp.bfloat16), 'z', 0, 0, tiled=True)  12.6 us
    all_to_all x1, starting transfers between devices, local(): g_parts = lax.all_to_all(g_parts, 'uly', 0, 0, tiled=True)  7.17 us
    all_to_all x1, starting transfers between devices, local(): back = lax.all_to_all(mixed.astype(jnp.bfloat16), 'z', 0, 0, tiled=True)  6.68 us
    unnamed x26, local copies, waits for them, and re-layouts  5.83 us
    reshape x4, local copies, waits for them, and re-layouts, to_tokens(): jnp.transpose(outs[:, index], (1, 2, 0, 3))  2.88 us
  transfers between devices with their start and end apart: 6, of which 5 were waited for; matrix products, arithmetic and copies ran while one was open for 5% of the time, Pallas kernels for 0%

profile of v11, /device:TPU:32, one launch (start us, length us, event | category | flops | bytes accessed | tf_op | source)
XLA Modules:
  0.0 114.5 jit_solution(6759978566294303756)
XLA Ops:
  0.6 1.0 copy.322
  1.7 0.9 copy.260
  2.5 7.2 %all-to-all-start = ((bf16[16,1,16,512]{3,2,1,0:T(8,128)(2,1)}), bf16[16,1,16,512]{3,2,1,0:T(8,128)(2,1)S(1)}, u32[]{:S(2)}, u32[]{:S(2)}) async-start(bf16[16,1,16,512]{3,2,1,0:T(8,128)(2,1)} %copy.260), calls=%async_computation | async-start | bytes 524288 | tf_op jit(solution)/shard_map/all_to_all | solution.py:71
  9.7 1.2 %reduce-window.6 = f32[1,4,2,128]{3,2,1,0:T(2,128)S(1)} reduce-window(f32[1,4,2,128]{3,2,1,0:T(2,128)S(1)} %reshape.514, f32[]{:T(128)} %constant.7.clone.1), window={size=1x1x1x128 pad=0_0x0_0x0_0x127_0}, to_apply=%region_0.0 | reduce-window | flops 130048 | bytes 8196 | tf_op jit(solution)/shard_map/reduce-window
  11.0 0.1 copy.313
  11.2 0.1 copy.249
  11.5 0.8 copy-done.8
  12.4 0.9 copy-done.9
  13.3 0.1 copy.316
  13.4 0.2 convolution_bitcast_fusion.8
  13.7 2.1 %collective-permute-start = (f32[1,4,129,128]{3,2,1,0:T(8,128)S(1)}, f32[1,4,129,128]{3,2,1,0:T(8,128)S(1)}, u32[]{:S(2)}, u32[]{:S(2)}) collective-permute-start(f32[1,4,129,128]{3,2,1,0:T(8,128)S(1)} %pad_maximum_fusion.1), channel_id=1, source_target_pairs={{0,16},{16,0},{1,17},{17,1},{2,18},{18,2},{3,19},{19,3},{4,20},{20... | collective-permute-start | bytes 792584 | tf_op jit(solution)/shard_map/ppermute | solution.py:90
  15.9 0.1 copy.256
  16.1 2.2 %all-to-all-done = bf16[16,1,16,512]{3,2,1,0:T(8,128)(2,1)S(1)} async-done(((bf16[16,1,16,512]{3,2,1,0:T(8,128)(2,1)}), bf16[16,1,16,512]{3,2,1,0:T(8,128)(2,1)S(1)}, u32[]{:S(2)}, u32[]{:S(2)}) %all-to-all-start) | async-done | bytes 262176 | tf_op jit(solution)/shard_map/all_to_all | solution.py:71
  18.3 0.5 convolution_bitcast_fusion.7
  18.8 1.9 %collective-permute-start.1 = (f32[1,4,128,128]{3,2,1,0:T(8,128)S(1)}, f32[1,4,128,128]{3,2,1,0:T(8,128)S(1)}, u32[]{:S(2)}, u32[]{:S(2)}) collective-permute-start(f32[1,4,128,128]{3,2,1,0:T(8,128)S(1)} %convolution_bitcast_fusion.7), channel_id=1, source_target_pairs={{0,16},{16,0},{1,17},{17,1},{2,18},{18,2},{3,19},{19,3},{4,20},{20... | collective-permute-start | bytes 786440 | tf_op jit(solution)/shard_map/ppermute | solution.py:93
  20.8 0.1 fusion.60
  20.9 0.1 fusion.37
  21.0 0.5 copy-done.2
  21.5 0.7 collective-permute-done.1
  22.3 0.1 fusion.36
  22.4 0.6 copy-done.4
  23.0 0.1 broadcast_in_dim_broadcast_in_dim_broadcast_in_dim.2
  23.1 0.1 pad_maximum_fusion
  23.2 0.9 copy.263
  24.1 15.2 %all-to-all-start.1 = ((f32[16,1,4,9,128]{4,2,3,1,0:T(4,128)}), f32[16,1,4,9,128]{4,2,3,1,0:T(4,128)S(1)}, u32[]{:S(2)}, u32[]{:S(2)}) async-start(f32[16,1,4,9,128]{4,2,3,1,0:T(4,128)} %copy.263), calls=%async_computation.1 | async-start | bytes 589824 | tf_op jit(solution)/shard_map/all_to_all | solution.py:119
  39.5 0.4 fusion
  39.9 0.3 convolution_bitcast_fusion.6
  40.1 18.3 %all-to-all-done.1 = f32[16,1,4,9,128]{4,2,3,1,0:T(4,128)S(1)} async-done(((f32[16,1,4,9,128]{4,2,3,1,0:T(4,128)}), f32[16,1,4,9,128]{4,2,3,1,0:T(4,128)S(1)}, u32[]{:S(2)}, u32[]{:S(2)}) %all-to-all-start.1) | async-done | bytes 294944 | tf_op jit(solution)/shard_map/all_to_all | solution.py:119
  58.5 0.1 copy.265
  58.6 0.1 copy.266
  58.9 0.3 fusion.14
  59.2 0.3 fusion.13
  59.6 0.7 copy.271
  60.3 6.7 %all-to-all-start.2 = ((bf16[16,2,1,4,4,128]{5,4,3,2,1,0:T(4,128)(2,1)}), bf16[16,2,1,4,4,128]{5,4,3,2,1,0:T(4,128)(2,1)S(1)}, u32[]{:S(2)}, u32[]{:S(2)}) async-start(bf16[16,2,1,4,4,128]{5,4,3,2,1,0:T(4,128)(2,1)} %copy.271), calls=%async_computation.2 | async-start | bytes 262144 | tf_op jit(solution)/shard_map/all_to_all | solution.py:128
  67.0 0.3 convolution_bitcast_fusion.1
  67.3 0.4 fusion.1
  67.7 0.8 copy-done
  68.5 0.3 convolution_bitcast_fusion.3
  68.9 12.6 %all-to-all-done.2 = bf16[16,2,1,4,4,128]{5,4,3,2,1,0:T(4,128)(2,1)S(1)} async-done(((bf16[16,2,1,4,4,128]{5,4,3,2,1,0:T(4,128)(2,1)}), bf16[16,2,1,4,4,128]{5,4,3,2,1,0:T(4,128)(2,1)S(1)}, u32[]{:S(2)}, u32[]{:S(2)}) %all-to-all-start.2) | async-done | bytes 131104 | tf_op jit(solution)/shard_map/all_to_all | solution.py:128
  81.6 2.1 %collective-permute-start.2 = (bf16[2,1,4,64,128]{4,3,2,1,0:T(8,128)(2,1)S(1)}, bf16[2,1,4,64,128]{4,3,2,1,0:T(8,128)(2,1)S(1)}, u32[]{:S(2)}, u32[]{:S(2)}) collective-permute-start(bf16[2,1,4,64,128]{4,3,2,1,0:T(8,128)(2,1)S(1)} %pad_maximum_fusion.4), channel_id=1, source_target_pairs={{0,16},{16,0},{1,17},{17,1},{2,18},{18,2},{3,19},{19,3},{4,20},{20... | collective-permute-start | bytes 393224 | tf_op jit(solution)/shard_map/ppermute | solution.py:130
  83.7 0.3 convolution_bitcast_fusion.5
  84.0 1.0 collective-permute-done.2
  85.0 0.2 fusion.18
  85.2 0.3 fusion.8
  85.5 0.3 copy-done.6
  85.9 0.2 copy.295
  86.1 0.1 stack.34
  86.2 0.3 fusion.12
  86.5 0.2 copy.276
  86.7 0.1 stack.31
  86.8 0.8 copy-done.7
  87.6 0.2 fusion.9
  87.9 0.2 fusion.10
  88.1 0.2 copy.283
  88.3 0.1 stack.32
  88.4 0.2 copy.289
  88.6 0.1 stack.33
  88.7 0.1 maximum_bitcast_fusion
  88.9 0.1 copy.296
  89.0 22.6 %all_to_all.20 = bf16[16,4,1,16,512]{4,3,2,1,0:T(8,128)(2,1)S(1)} all-to-all(bf16[16,4,1,16,512]{4,3,2,1,0:T(8,128)(2,1)S(1)} %copy.296), channel_id=1, replica_groups=mesh['z'=16,'core'=2,'uly'=16] {'uly'}, dimensions={0} | all-to-all | bytes 2097152 | tf_op jit(solution)/shard_map/all_to_all | solution.py:168
  111.6 0.7 copy.320
  112.4 0.7 copy.319
  113.1 0.7 copy.318
  113.8 0.7 copy.317
  (55 shorter events, 1.4 us)
Async XLA Ops:
  2.5 7.2 %copy-start.11 = (f32[1,4,256]{2,1,0:T(4,128)S(1)}, f32[1,4,256]{2,1,0:T(4,128)}, u32[]{:S(2)}) copy-start(f32[1,4,256]{2,1,0:T(4,128)} %param.9) | copy-start | bytes 12292
  2.5 15.7 %all-to-all-start = ((bf16[16,1,16,512]{3,2,1,0:T(8,128)(2,1)}), bf16[16,1,16,512]{3,2,1,0:T(8,128)(2,1)S(1)}, u32[]{:S(2)}, u32[]{:S(2)}) async-start(bf16[16,1,16,512]{3,2,1,0:T(8,128)(2,1)} %copy.260), calls=%async_computation | async-start | bytes 524288 | tf_op jit(solution)/shard_map/all_to_all | solution.py:71
  11.4 1.0 copy-start.8
  12.3 0.9 copy-start.9
  13.7 2.3 %copy-start.10 = (bf16[1,256,512]{2,1,0:T(8,128)(2,1)S(1)}, bf16[1,256,512]{2,1,0:T(8,128)(2,1)}, u32[]{:S(2)}) copy-start(bf16[1,256,512]{2,1,0:T(8,128)(2,1)} %param.5) | copy-start | bytes 786436
  13.7 7.0 %collective-permute-start = (f32[1,4,129,128]{3,2,1,0:T(8,128)S(1)}, f32[1,4,129,128]{3,2,1,0:T(8,128)S(1)}, u32[]{:S(2)}, u32[]{:S(2)}) collective-permute-start(f32[1,4,129,128]{3,2,1,0:T(8,128)S(1)} %pad_maximum_fusion.1), channel_id=1, source_target_pairs={{0,16},{16,0},{1,17},{17,1},{2,18},{18,2},{3,19},{19,3},{4,20},{20... | collective-permute-start | bytes 792584 | tf_op jit(solution)/shard_map/ppermute | solution.py:90
  18.8 3.4 %collective-permute-start.1 = (f32[1,4,128,128]{3,2,1,0:T(8,128)S(1)}, f32[1,4,128,128]{3,2,1,0:T(8,128)S(1)}, u32[]{:S(2)}, u32[]{:S(2)}) collective-permute-start(f32[1,4,128,128]{3,2,1,0:T(8,128)S(1)} %convolution_bitcast_fusion.7), channel_id=1, source_target_pairs={{0,16},{16,0},{1,17},{17,1},{2,18},{18,2},{3,19},{19,3},{4,20},{20... | collective-permute-start | bytes 786440 | tf_op jit(solution)/shard_map/ppermute | solution.py:93
  20.8 0.7 copy-start.2
  22.3 0.7 copy-start.4
  24.1 34.4 %all-to-all-start.1 = ((f32[16,1,4,9,128]{4,2,3,1,0:T(4,128)}), f32[16,1,4,9,128]{4,2,3,1,0:T(4,128)S(1)}, u32[]{:S(2)}, u32[]{:S(2)}) async-start(f32[16,1,4,9,128]{4,2,3,1,0:T(4,128)} %copy.263), calls=%async_computation.1 | async-start | bytes 589824 | tf_op jit(solution)/shard_map/all_to_all | solution.py:119
  60.3 21.2 %all-to-all-start.2 = ((bf16[16,2,1,4,4,128]{5,4,3,2,1,0:T(4,128)(2,1)}), bf16[16,2,1,4,4,128]{5,4,3,2,1,0:T(4,128)(2,1)S(1)}, u32[]{:S(2)}, u32[]{:S(2)}) async-start(bf16[16,2,1,4,4,128]{5,4,3,2,1,0:T(4,128)(2,1)} %copy.271), calls=%async_computation.2 | async-start | bytes 262144 | tf_op jit(solution)/shard_map/all_to_all | solution.py:128
  67.7 0.8 copy-start
  81.4 2.2 %copy-start.1 = (bf16[4,256,256]{2,1,0:T(8,128)(2,1)S(1)}, bf16[4,256,256]{2,1,0:T(8,128)(2,1)}, u32[]{:S(2)}) copy-start(bf16[4,256,256]{2,1,0:T(8,128)(2,1)} %copy-done) | copy-start | bytes 1572868
  81.6 3.4 %collective-permute-start.2 = (bf16[2,1,4,64,128]{4,3,2,1,0:T(8,128)(2,1)S(1)}, bf16[2,1,4,64,128]{4,3,2,1,0:T(8,128)(2,1)S(1)}, u32[]{:S(2)}, u32[]{:S(2)}) collective-permute-start(bf16[2,1,4,64,128]{4,3,2,1,0:T(8,128)(2,1)S(1)} %pad_maximum_fusion.4), channel_id=1, source_target_pairs={{0,16},{16,0},{1,17},{17,1},{2,18},{18,2},{3,19},{19,3},{4,20},{20... | collective-permute-start | bytes 393224 | tf_op jit(solution)/shard_map/ppermute | solution.py:130
  84.0 1.0 copy-start.3
  84.0 1.0 copy-start.5
  85.2 0.7 copy-start.6
  86.7 0.9 copy-start.7

commit v12 on v11

--- a/solution.py
+++ b/solution.py
@@ -86,52 +86,30 @@
     second = core == 1
     pairs = [(0, 1), (1, 0)]
     last = last_cum[..., 0]
+    own = jnp.where(second, update, local_grad)
     last_row = jnp.broadcast_to(last[..., None, None], (batch_count, head_count, 1, width))
-    other_packed = lax.ppermute(jnp.concatenate([update, last_row], axis=2), "core", pairs)
-    other_update = other_packed[:, :, :width]
+    given = jnp.where(second, local_grad, update)
+    other_packed = lax.ppermute(jnp.concatenate([given, last_row], axis=2), "core", pairs)
+    other = other_packed[:, :, :width]
     other_last = other_packed[:, :, width, 0]
-    other_grad = lax.ppermute(local_grad, "core", pairs)
-
-    def order(mine, other):
-        return jnp.where(second, other, mine), jnp.where(second, mine, other)
-
-    update_lo, update_hi = order(update, other_update)
-    grad_lo, grad_hi = order(local_grad, other_grad)
-    last_lo, last_hi = order(last, other_last)
-    keep_lo = jnp.exp(last_lo)[..., None, None]
-    keep_hi = jnp.exp(last_hi)[..., None, None]
-    chip_update = keep_hi * update_lo + update_hi
-    chip_grad = keep_lo * grad_hi + grad_lo
-    half = width // 2
-    band = half // chip_count
-
-    def my_half(state):
-        return lax.dynamic_slice_in_dim(state, core * half, half, axis=2)
-
-    chip_last = jnp.broadcast_to((last_lo + last_hi)[..., None], (batch_count, head_count, width))
+    keep_mine = jnp.exp(last)[..., None, None]
+    keep_other = jnp.exp(other_last)[..., None, None]
+    chip_state = keep_mine * other + own
+    band = width // chip_count
+    chip_last = jnp.broadcast_to((last + other_last)[..., None], (batch_count, head_count, width))
     last_piece = jnp.broadcast_to(
         chip_last[None, :, :, None, :], (chip_count, batch_count, head_count, 1, width)
     )
-    send = jnp.concatenate(
-        [to_pieces(my_half(chip_update), chip_count), to_pieces(my_half(chip_grad), chip_count), last_piece],
-        axis=3,
-    )
+    send = jnp.concatenate([to_pieces(chip_state, chip_count), last_piece], axis=3)
     got = lax.all_to_all(send, "z", 0, 0, tiled=True)
-    forward_w, backward_w = block_weights(got[:, :, :, 2 * band, 0])
-    mixed = jnp.stack(
-        [
-            mix_blocks(forward_w, got[:, :, :, :band]),
-            mix_blocks(backward_w, got[:, :, :, band : 2 * band]),
-        ],
-        axis=1,
-    )
-    back = lax.all_to_all(mixed.astype(jnp.bfloat16), "z", 0, 0, tiled=True)
-    halves = jnp.stack([from_pieces(back[:, 0]), from_pieces(back[:, 1])])
-    other_halves = lax.ppermute(halves, "core", pairs)
-    low_rows, high_rows = order(halves, other_halves)
-    entering = jnp.concatenate([low_rows, high_rows], axis=3)
-    state_b = jnp.where(second, keep_lo * entering[0] + update_lo, entering[0]).astype(jnp.bfloat16)
-    carried_b = jnp.where(second, entering[1], keep_hi * entering[1] + grad_hi).astype(jnp.bfloat16)
+    forward_w, backward_w = block_weights(got[:, :, :, band, 0])
+    weights = jnp.where(second, forward_w, backward_w)
+    back = lax.all_to_all(mix_blocks(weights, got[:, :, :, :band]), "z", 0, 0, tiled=True)
+    entering = from_pieces(back)
+    fixed = (keep_other * entering + other).astype(jnp.bfloat16)
+    other_entering = lax.ppermute(entering.astype(jnp.bfloat16), "core", pairs)
+    state_b = jnp.where(second, fixed, other_entering)
+    carried_b = jnp.where(second, other_entering, fixed)
 
     scores = jnp.einsum("bihd,bjhd->bhij", q_split, k_split, preferred_element_type=jnp.float32)
     attn_weights = (scores * decay_mask).astype(jnp.bfloat16)

time: 115 us -> 115 us (level)
  waiting for transfers between devices: 34.8 us -> 40.6 us
  local copies, waits for them, and re-layouts: 14.1 us -> 11.2 us
  starting transfers between devices: 35.1 us -> 33 us
  blocking collectives: 22.6 us -> 20.8 us
    all_to_all x1, waiting for transfers between devices: 12.6 us -> 15.2 us  [local(): lax.all_to_all(mix_blocks(weights, got[:, :, :, :band]), 'z', 0, 0, tiled...]
    unnamed x26 -> x12, local copies, waits for them, and re-layouts: 5.83 us -> 3.62 us
    ppermute x3 -> x2, starting transfers between devices: 6.02 us -> 3.97 us  [the longest x1 2.05 us: local(): other_entering = lax.ppermute(entering.astype(jnp.bfloat16), 'core', pairs)]
    all_to_all x1, blocking collectives: 22.6 us -> 20.8 us  [local(): outs = lax.all_to_all(outs, 'uly', 0, 0, tiled=True)]
    all_to_all x1, waiting for transfers between devices: 2.18 us -> 3.64 us  [local(): g_parts = lax.all_to_all(g_parts, 'uly', 0, 0, tiled=True)]
    ppermute x3 -> x2, waiting for transfers between devices: 1.72 us -> 2.73 us  [the longest x1 1.52 us: local(): lax.ppermute(jnp.concatenate([given, last_row], axis=2), 'core', pairs)]
  transfers between devices with their start and end apart: 6 -> 5, of which waited for: 5 -> 5; matrix products, arithmetic and copies ran while one was open for 5% -> 5% of each run, Pallas kernels for 0% -> 0%
where the time goes in v12:
time: 115 us; the launch traced here: 114 us
  waiting for transfers between devices  40.6 us (35%)
  starting transfers between devices  33 us (29%)
  blocking collectives  20.8 us (18%)
  local copies, waits for them, and re-layouts  11.2 us (10%)
  matrix products  5.22 us (5%)
  other arithmetic  2.58 us (2%)
    all_to_all x1, blocking collectives, local(): outs = lax.all_to_all(outs, 'uly', 0, 0, tiled=True)  20.8 us
    all_to_all x1, waiting for transfers between devices, local(): got = lax.all_to_all(send, 'z', 0, 0, tiled=True)  19 us
    all_to_all x1, starting transfers between devices, local(): got = lax.all_to_all(send, 'z', 0, 0, tiled=True)  15.2 us
    all_to_all x1, waiting for transfers between devices, local(): lax.all_to_all(mix_blocks(weights, got[:, :, :, :band]), 'z', 0, 0, tiled...  15.2 us
    all_to_all x1, starting transfers between devices, local(): g_parts = lax.all_to_all(g_parts, 'uly', 0, 0, tiled=True)  7.17 us
    all_to_all x1, starting transfers between devices, local(): lax.all_to_all(mix_blocks(weights, got[:, :, :, :band]), 'z', 0, 0, tiled...  6.68 us
    all_to_all x1, waiting for transfers between devices, local(): g_parts = lax.all_to_all(g_parts, 'uly', 0, 0, tiled=True)  3.64 us
    unnamed x12, local copies, waits for them, and re-layouts  3.62 us
  transfers between devices with their start and end apart: 5, of which 5 were waited for; matrix products, arithmetic and copies ran while one was open for 5% of the time, Pallas kernels for 0%

profile of v12, /device:TPU:32, one launch (start us, length us, event | category | flops | bytes accessed | tf_op | source)
XLA Modules:
  0.0 114.5 jit_solution(7805453534346446457)
XLA Ops:
  0.6 1.0 copy.298
  1.7 0.9 copy.237
  2.5 7.2 %all-to-all-start = ((bf16[16,1,16,512]{3,2,1,0:T(8,128)(2,1)}), bf16[16,1,16,512]{3,2,1,0:T(8,128)(2,1)S(1)}, u32[]{:S(2)}, u32[]{:S(2)}) async-start(bf16[16,1,16,512]{3,2,1,0:T(8,128)(2,1)} %copy.237), calls=%async_computation | async-start | bytes 524288 | tf_op jit(solution)/shard_map/all_to_all | solution.py:71
  9.7 1.2 %reduce-window.6 = f32[1,4,2,128]{3,2,1,0:T(2,128)S(1)} reduce-window(f32[1,4,2,128]{3,2,1,0:T(2,128)S(1)} %reshape.441, f32[]{:T(128)} %constant.12.clone.1), window={size=1x1x1x128 pad=0_0x0_0x0_0x127_0}, to_apply=%region_0.0 | reduce-window | flops 130048 | bytes 8196 | tf_op jit(solution)/shard_map/reduce-window
  11.0 0.1 slice.44
  11.0 0.1 copy.290
  11.2 0.1 copy.231
  11.4 0.1 copy.235
  11.5 0.1 copy.240
  11.6 0.7 copy-done.1
  12.4 0.9 copy-done.2
  13.4 0.9 copy-done.3
  14.2 0.1 copy.292
  14.4 0.2 fusion.13
  14.6 3.6 %all-to-all-done = bf16[16,1,16,512]{3,2,1,0:T(8,128)(2,1)S(1)} async-done(((bf16[16,1,16,512]{3,2,1,0:T(8,128)(2,1)}), bf16[16,1,16,512]{3,2,1,0:T(8,128)(2,1)S(1)}, u32[]{:S(2)}, u32[]{:S(2)}) %all-to-all-start) | async-done | bytes 262176 | tf_op jit(solution)/shard_map/all_to_all | solution.py:71
  18.3 0.5 fusion.18
  18.8 0.1 broadcast_in_dim.50
  18.9 1.9 %collective-permute-start = (f32[1,4,129,128]{3,2,1,0:T(8,128)S(1)}, f32[1,4,129,128]{3,2,1,0:T(8,128)S(1)}, u32[]{:S(2)}, u32[]{:S(2)}) collective-permute-start(f32[1,4,129,128]{3,2,1,0:T(8,128)S(1)} %pad_maximum_fusion.1), channel_id=1, source_target_pairs={{0,16},{16,0},{1,17},{17,1},{2,18},{18,2},{3,19},{19,3},{4,20},{20... | collective-permute-start | bytes 792584 | tf_op jit(solution)/shard_map/ppermute | solution.py:92
  20.9 1.5 %collective-permute-done = f32[1,4,129,128]{3,2,1,0:T(8,128)S(1)} collective-permute-done((f32[1,4,129,128]{3,2,1,0:T(8,128)S(1)}, f32[1,4,129,128]{3,2,1,0:T(8,128)S(1)}, u32[]{:S(2)}, u32[]{:S(2)}) %collective-permute-start) | collective-permute-done | bytes 264224 | tf_op jit(solution)/shard_map/ppermute | solution.py:92
  22.4 0.1 exponential_reduce_fusion
  22.5 0.1 fusion.16
  22.6 0.2 copy.333
  22.8 0.1 broadcast_in_dim_broadcast_in_dim_broadcast_in_dim.2
  22.9 0.8 pad_maximum_fusion
  23.7 15.2 %all-to-all-start.1 = ((f32[16,1,4,9,128]{4,2,3,1,0:T(4,128)}), f32[16,1,4,9,128]{4,2,3,1,0:T(4,128)S(1)}, u32[]{:S(2)}, u32[]{:S(2)}) async-start(f32[16,1,4,9,128]{4,2,3,1,0:T(4,128)} %pad_maximum_fusion), calls=%async_computation.1 | async-start | bytes 589824 | tf_op jit(solution)/shard_map/all_to_all | solution.py:104
  38.9 0.1 copy.289
  39.0 19.0 %all-to-all-done.1 = f32[16,1,4,9,128]{4,2,3,1,0:T(4,128)S(1)} async-done(((f32[16,1,4,9,128]{4,2,3,1,0:T(4,128)}), f32[16,1,4,9,128]{4,2,3,1,0:T(4,128)S(1)}, u32[]{:S(2)}, u32[]{:S(2)}) %all-to-all-start.1) | async-done | bytes 294944 | tf_op jit(solution)/shard_map/all_to_all | solution.py:104
  58.1 0.1 copy.245
  58.2 0.1 copy.246
  58.3 0.1 copy.248
  58.4 0.1 copy.249
  58.5 0.5 convolution_bitcast_fusion.7
  59.0 0.8 copy.250
  59.8 6.7 %all-to-all-start.2 = ((f32[16,1,4,8,128]{4,3,2,1,0:T(8,128)}), f32[16,1,4,8,128]{4,3,2,1,0:T(8,128)S(1)}, u32[]{:S(2)}, u32[]{:S(2)}) async-start(f32[16,1,4,8,128]{4,3,2,1,0:T(8,128)} %copy.250), calls=%async_computation.2 | async-start | bytes 524288 | tf_op jit(solution)/shard_map/all_to_all | solution.py:107
  66.5 0.4 fusion
  66.9 0.3 convolution_bitcast_fusion.6
  67.2 1.1 convolution_bitcast_fusion.1
  68.3 0.4 fusion.1
  68.7 0.3 convolution_bitcast_fusion.3
  69.1 0.3 convolution_bitcast_fusion.5
  69.4 15.2 %all-to-all-done.2 = f32[16,1,4,8,128]{4,3,2,1,0:T(8,128)S(1)} async-done(((f32[16,1,4,8,128]{4,3,2,1,0:T(8,128)}), f32[16,1,4,8,128]{4,3,2,1,0:T(8,128)S(1)}, u32[]{:S(2)}, u32[]{:S(2)}) %all-to-all-start.2) | async-done | bytes 262176 | tf_op jit(solution)/shard_map/all_to_all | solution.py:107
  84.6 2.1 %collective-permute-start.1 = (bf16[1,4,128,128]{3,2,1,0:T(8,128)(2,1)S(1)}, bf16[1,4,128,128]{3,2,1,0:T(8,128)(2,1)S(1)}, u32[]{:S(2)}, u32[]{:S(2)}) collective-permute-start(bf16[1,4,128,128]{3,2,1,0:T(8,128)(2,1)S(1)} %bitcast_convert_fusion), channel_id=1, source_target_pairs={{0,16},{16,0},{1,17},{17,1},{2,18},{18,2},{3,19},{19,3},{4,20},{20... | collective-permute-start | bytes 393224 | tf_op jit(solution)/shard_map/ppermute | solution.py:110
  86.7 0.1 fusion.15
  86.8 1.2 %collective-permute-done.1 = bf16[1,4,128,128]{3,2,1,0:T(8,128)(2,1)S(1)} collective-permute-done((bf16[1,4,128,128]{3,2,1,0:T(8,128)(2,1)S(1)}, bf16[1,4,128,128]{3,2,1,0:T(8,128)(2,1)S(1)}, u32[]{:S(2)}, u32[]{:S(2)}) %collective-permute-start.1) | collective-permute-done | bytes 131104 | tf_op jit(solution)/shard_map/ppermute | solution.py:110
  88.0 0.3 fusion.8
  88.3 0.2 copy.273
  88.5 0.1 stack.18
  88.6 0.3 fusion.12
  89.0 0.2 copy.254
  89.2 0.1 stack.15
  89.3 0.2 fusion.10
  89.5 0.2 copy.261
  89.7 0.1 stack.16
  89.9 0.2 fusion.9
  90.1 0.2 copy.267
  90.3 0.1 stack.17
  90.4 0.1 maximum_bitcast_fusion
  90.6 0.1 copy.274
  90.7 20.8 %all_to_all.20 = bf16[16,4,1,16,512]{4,3,2,1,0:T(8,128)(2,1)S(1)} all-to-all(bf16[16,4,1,16,512]{4,3,2,1,0:T(8,128)(2,1)S(1)} %copy.274), channel_id=1, replica_groups=mesh['z'=16,'core'=2,'uly'=16] {'uly'}, dimensions={0} | all-to-all | bytes 2097152 | tf_op jit(solution)/shard_map/all_to_all | solution.py:146
  111.5 0.1 slice_bitcast_fusion
  111.6 0.7 copy.296
  112.3 0.7 copy.295
  113.0 0.7 copy.294
  113.8 0.7 copy.293
  (29 shorter events, 0.6 us)
Async XLA Ops:
  2.5 7.2 %copy-start.4 = (f32[1,4,256]{2,1,0:T(4,128)S(1)}, f32[1,4,256]{2,1,0:T(4,128)}, u32[]{:S(2)}) copy-start(f32[1,4,256]{2,1,0:T(4,128)} %param.9) | copy-start | bytes 12292
  2.5 15.7 %all-to-all-start = ((bf16[16,1,16,512]{3,2,1,0:T(8,128)(2,1)}), bf16[16,1,16,512]{3,2,1,0:T(8,128)(2,1)S(1)}, u32[]{:S(2)}, u32[]{:S(2)}) async-start(bf16[16,1,16,512]{3,2,1,0:T(8,128)(2,1)} %copy.237), calls=%async_computation | async-start | bytes 524288 | tf_op jit(solution)/shard_map/all_to_all | solution.py:71
  11.4 1.0 copy-start.1
  12.3 0.9 copy-start.2
  13.3 0.9 copy-start.3
  18.9 3.5 %collective-permute-start = (f32[1,4,129,128]{3,2,1,0:T(8,128)S(1)}, f32[1,4,129,128]{3,2,1,0:T(8,128)S(1)}, u32[]{:S(2)}, u32[]{:S(2)}) collective-permute-start(f32[1,4,129,128]{3,2,1,0:T(8,128)S(1)} %pad_maximum_fusion.1), channel_id=1, source_target_pairs={{0,16},{16,0},{1,17},{17,1},{2,18},{18,2},{3,19},{19,3},{4,20},{20... | collective-permute-start | bytes 792584 | tf_op jit(solution)/shard_map/ppermute | solution.py:92
  23.7 34.4 %all-to-all-start.1 = ((f32[16,1,4,9,128]{4,2,3,1,0:T(4,128)}), f32[16,1,4,9,128]{4,2,3,1,0:T(4,128)S(1)}, u32[]{:S(2)}, u32[]{:S(2)}) async-start(f32[16,1,4,9,128]{4,2,3,1,0:T(4,128)} %pad_maximum_fusion), calls=%async_computation.1 | async-start | bytes 589824 | tf_op jit(solution)/shard_map/all_to_all | solution.py:104
  59.8 24.8 %all-to-all-start.2 = ((f32[16,1,4,8,128]{4,3,2,1,0:T(8,128)}), f32[16,1,4,8,128]{4,3,2,1,0:T(8,128)S(1)}, u32[]{:S(2)}, u32[]{:S(2)}) async-start(f32[16,1,4,8,128]{4,3,2,1,0:T(8,128)} %copy.250), calls=%async_computation.2 | async-start | bytes 524288 | tf_op jit(solution)/shard_map/all_to_all | solution.py:107
  84.6 3.4 %copy-start = (f32[1,256,4,128]{3,1,2,0:T(8,128)S(1)}, f32[1,256,4,128]{3,1,2,0:T(8,128)}, u32[]{:S(2)}) copy-start(f32[1,256,4,128]{3,1,2,0:T(8,128)} %convolution_bitcast_fusion.1) | copy-start | bytes 1572868
  84.6 3.4 %collective-permute-start.1 = (bf16[1,4,128,128]{3,2,1,0:T(8,128)(2,1)S(1)}, bf16[1,4,128,128]{3,2,1,0:T(8,128)(2,1)S(1)}, u32[]{:S(2)}, u32[]{:S(2)}) collective-permute-start(bf16[1,4,128,128]{3,2,1,0:T(8,128)(2,1)S(1)} %bitcast_convert_fusion), channel_id=1, source_target_pairs={{0,16},{16,0},{1,17},{17,1},{2,18},{18,2},{3,19},{19,3},{4,20},{20... | collective-permute-start | bytes 393224 | tf_op jit(solution)/shard_map/ppermute | solution.py:110

commit v13 on v12

--- a/solution.py
+++ b/solution.py
@@ -107,50 +107,63 @@
     back = lax.all_to_all(mix_blocks(weights, got[:, :, :, :band]), "z", 0, 0, tiled=True)
     entering = from_pieces(back)
     fixed = (keep_other * entering + other).astype(jnp.bfloat16)
-    other_entering = lax.ppermute(entering.astype(jnp.bfloat16), "core", pairs)
-    state_b = jnp.where(second, fixed, other_entering)
-    carried_b = jnp.where(second, other_entering, fixed)
-
     scores = jnp.einsum("bihd,bjhd->bhij", q_split, k_split, preferred_element_type=jnp.float32)
     attn_weights = (scores * decay_mask).astype(jnp.bfloat16)
     grad_raw = jnp.einsum("bihe,bjhe->bhij", g_split, v_split, preferred_element_type=jnp.float32)
     grad_scores = (grad_raw * decay_mask).astype(jnp.bfloat16)
-    attended = jnp.einsum(
+    attended_inner = jnp.einsum(
         "bhij,bjhd->bihd", attn_weights, v_split, preferred_element_type=jnp.float32
     )
-    attended = attended + jnp.einsum(
-        "bihd,bhde->bihe", scaled_query, state_b, preferred_element_type=jnp.float32
-    )
-    query_part = jnp.einsum(
+    query_inner = jnp.einsum(
         "bhij,bjhd->bihd", grad_scores, k_split, preferred_element_type=jnp.float32
     )
-    query_part = query_part + rise_rows * jnp.einsum(
-        "bihe,bhde->bihd", g_split, state_b, preferred_element_type=jnp.float32
-    )
-    key_part = jnp.einsum(
+    key_inner = jnp.einsum(
         "bhij,bihd->bjhd", grad_scores, q_split, preferred_element_type=jnp.float32
     )
-    key_part = key_part + fall_rows * jnp.einsum(
-        "bjhe,bhde->bjhd", v_split, carried_b, preferred_element_type=jnp.float32
-    )
-    value_part = jnp.einsum(
+    value_inner = jnp.einsum(
         "bhij,bihe->bjhe", attn_weights, g_split, preferred_element_type=jnp.float32
     )
-    value_part = value_part + fall_rows * jnp.einsum(
-        "bjhd,bhde->bjhe", k_split, carried_b, preferred_element_type=jnp.float32
-    )
 
-    outs = jnp.stack([attended, query_part, key_part, value_part]).astype(jnp.bfloat16)
-    outs = outs.reshape(4, batch_count, uly_count, positions // uly_count, width_heads)
-    outs = jnp.transpose(outs, (2, 0, 1, 3, 4))
-    outs = lax.all_to_all(outs, "uly", 0, 0, tiled=True)
+    def forward_pair(state_b):
+        attended = attended_inner + jnp.einsum(
+            "bihd,bhde->bihe", scaled_query, state_b, preferred_element_type=jnp.float32
+        )
+        query_part = query_inner + rise_rows * jnp.einsum(
+            "bihe,bhde->bihd", g_split, state_b, preferred_element_type=jnp.float32
+        )
+        return jnp.stack([attended, query_part]).astype(jnp.bfloat16)
 
-    def to_tokens(index):
-        return jnp.transpose(outs[:, index], (1, 2, 0, 3)).reshape(
+    def backward_pair(carried_b):
+        key_part = key_inner + fall_rows * jnp.einsum(
+            "bjhe,bhde->bjhd", v_split, carried_b, preferred_element_type=jnp.float32
+        )
+        value_part = value_inner + fall_rows * jnp.einsum(
+            "bjhd,bhde->bjhe", k_split, carried_b, preferred_element_type=jnp.float32
+        )
+        return jnp.stack([key_part, value_part]).astype(jnp.bfloat16)
+
+    def to_tokens(pair):
+        outs = pair.reshape(2, batch_count, uly_count, positions // uly_count, width_heads)
+        outs = jnp.transpose(outs, (2, 0, 1, 3, 4))
+        return lax.all_to_all(outs, "uly", 0, 0, tiled=True)
+
+    ready = to_tokens(jnp.where(second, forward_pair(fixed), backward_pair(fixed)))
+    other_entering = lax.ppermute(entering.astype(jnp.bfloat16), "core", pairs)
+    later = to_tokens(jnp.where(second, backward_pair(other_entering), forward_pair(other_entering)))
+    forward_rows = jnp.where(second, ready, later)
+    backward_rows = jnp.where(second, later, ready)
+
+    def rows_of(received, index):
+        return jnp.transpose(received[:, index], (1, 2, 0, 3)).reshape(
             batch_count, positions // uly_count, uly_count * width_heads
         )
 
-    return (to_tokens(0), to_tokens(1), to_tokens(2), to_tokens(3))
+    return (
+        rows_of(forward_rows, 0),
+        rows_of(forward_rows, 1),
+        rows_of(backward_rows, 0),
+        rows_of(backward_rows, 1),
+    )
 
 
 def solution(mesh):

time: 115 us -> 136 us (1.18)
  waiting for transfers between devices: 40.6 us -> 50 us
  local copies, waits for them, and re-layouts: 11.2 us -> 20 us
  blocking collectives: 20.8 us -> 14.4 us
  starting transfers between devices: 33 us -> 37.1 us
  matrix products: 5.22 us -> 7.65 us
  other arithmetic: 2.58 us -> 4.95 us
    all_to_all x0 -> x1, waiting for transfers between devices: none -> 9.86 us  [to_tokens(): return lax.all_to_all(outs, 'uly', 0, 0, tiled=True)]
    another operation x15 -> x22, local copies, waits for them, and re-layouts: 1.58 us -> 8.26 us
    all_to_all x1, blocking collectives: 20.8 us -> 14.4 us  [to_tokens(): return lax.all_to_all(outs, 'uly', 0, 0, tiled=True)]
    all_to_all x0 -> x1, starting transfers between devices: none -> 4.24 us  [to_tokens(): return lax.all_to_all(outs, 'uly', 0, 0, tiled=True)]
    dot_general x4 -> x8, matrix products: 1.13 us -> 4.35 us  [the longest x2 1.33 us: backward_pair(): jnp.einsum('bjhd,bhde->bjhe', k_split, carried_b, preferred_element_type=...]
    unnamed x12 -> x15, local copies, waits for them, and re-layouts: 3.62 us -> 4.08 us
  transfers between devices with their start and end apart: 5 -> 6, of which waited for: 5 -> 5; matrix products, arithmetic and copies ran while one was open for 5% -> 14% of each run, Pallas kernels for 0% -> 0%
where the time goes in v13:
time: 136 us; the launch traced here: 135 us
  waiting for transfers between devices  50 us (37%)
  starting transfers between devices  37.1 us (27%)
  local copies, waits for them, and re-layouts  20 us (15%)
  blocking collectives  14.4 us (11%)
  matrix products  7.65 us (6%)
  other arithmetic  4.95 us (4%)
    all_to_all x1, waiting for transfers between devices, local(): got = lax.all_to_all(send, 'z', 0, 0, tiled=True)  19 us
    all_to_all x1, waiting for transfers between devices, local(): lax.all_to_all(mix_blocks(weights, got[:, :, :, :band]), 'z', 0, 0, tiled...  16 us
    all_to_all x1, starting transfers between devices, local(): got = lax.all_to_all(send, 'z', 0, 0, tiled=True)  15.2 us
    all_to_all x1, blocking collectives, to_tokens(): return lax.all_to_all(outs, 'uly', 0, 0, tiled=True)  14.4 us
    all_to_all x1, waiting for transfers between devices, to_tokens(): return lax.all_to_all(outs, 'uly', 0, 0, tiled=True)  9.86 us
    all_to_all x1, starting transfers between devices, local(): g_parts = lax.all_to_all(g_parts, 'uly', 0, 0, tiled=True)  7.17 us
    all_to_all x1, starting transfers between devices, local(): lax.all_to_all(mix_blocks(weights, got[:, :, :, :band]), 'z', 0, 0, tiled...  6.68 us
    another operation x14, local copies, waits for them, and re-layouts  4.63 us
  transfers between devices with their start and end apart: 6, of which 5 were waited for; matrix products, arithmetic and copies ran while one was open for 14% of the time, Pallas kernels for 0%

profile of v13, /device:TPU:32, one launch (start us, length us, event | category | flops | bytes accessed | tf_op | source)
XLA Modules:
  0.0 135.3 jit_solution(7734332044076693158)
XLA Ops:
  0.6 1.0 copy.380
  1.7 0.9 copy.299
  2.5 7.2 %all-to-all-start = ((bf16[16,1,16,512]{3,2,1,0:T(8,128)(2,1)}), bf16[16,1,16,512]{3,2,1,0:T(8,128)(2,1)S(1)}, u32[]{:S(2)}, u32[]{:S(2)}) async-start(bf16[16,1,16,512]{3,2,1,0:T(8,128)(2,1)} %copy.299), calls=%async_computation | async-start | bytes 524288 | tf_op jit(solution)/shard_map/all_to_all | solution.py:71
  9.7 1.2 reduce-window.6
  11.0 0.1 copy.372
  11.6 0.7 copy-done.2
  12.4 0.9 copy-done.3
  13.4 0.9 copy-done.4
  14.2 0.1 copy.374
  14.4 0.2 fusion.26
  14.6 3.6 %all-to-all-done = bf16[16,1,16,512]{3,2,1,0:T(8,128)(2,1)S(1)} async-done(((bf16[16,1,16,512]{3,2,1,0:T(8,128)(2,1)}), bf16[16,1,16,512]{3,2,1,0:T(8,128)(2,1)S(1)}, u32[]{:S(2)}, u32[]{:S(2)}) %all-to-all-start) | async-done | bytes 262176 | tf_op jit(solution)/shard_map/all_to_all | solution.py:71
  18.3 0.5 fusion.37
  18.9 1.9 %collective-permute-start = (f32[1,4,129,128]{3,2,1,0:T(8,128)S(1)}, f32[1,4,129,128]{3,2,1,0:T(8,128)S(1)}, u32[]{:S(2)}, u32[]{:S(2)}) collective-permute-start(f32[1,4,129,128]{3,2,1,0:T(8,128)S(1)} %pad_maximum_fusion.1), channel_id=1, source_target_pairs={{0,16},{16,0},{1,17},{17,1},{2,18},{18,2},{3,19},{19,3},{4,20},{20... | collective-permute-start | bytes 792584 | tf_op jit(solution)/shard_map/ppermute | solution.py:92
  20.9 1.5 %collective-permute-done = f32[1,4,129,128]{3,2,1,0:T(8,128)S(1)} collective-permute-done((f32[1,4,129,128]{3,2,1,0:T(8,128)S(1)}, f32[1,4,129,128]{3,2,1,0:T(8,128)S(1)}, u32[]{:S(2)}, u32[]{:S(2)}) %collective-permute-start) | collective-permute-done | bytes 264224 | tf_op jit(solution)/shard_map/ppermute | solution.py:92
  22.4 0.1 exponential_reduce_fusion
  22.6 0.5 copy-done
  23.1 0.2 copy.417
  23.3 0.8 pad_maximum_fusion
  24.1 15.2 %all-to-all-start.1 = ((f32[16,1,4,9,128]{4,2,3,1,0:T(4,128)}), f32[16,1,4,9,128]{4,2,3,1,0:T(4,128)S(1)}, u32[]{:S(2)}, u32[]{:S(2)}) async-start(f32[16,1,4,9,128]{4,2,3,1,0:T(4,128)} %pad_maximum_fusion), calls=%async_computation.1 | async-start | bytes 589824 | tf_op jit(solution)/shard_map/all_to_all | solution.py:104
  39.5 19.0 %all-to-all-done.1 = f32[16,1,4,9,128]{4,2,3,1,0:T(4,128)S(1)} async-done(((f32[16,1,4,9,128]{4,2,3,1,0:T(4,128)}), f32[16,1,4,9,128]{4,2,3,1,0:T(4,128)S(1)}, u32[]{:S(2)}, u32[]{:S(2)}) %all-to-all-start.1) | async-done | bytes 294944 | tf_op jit(solution)/shard_map/all_to_all | solution.py:104
  59.0 0.5 convolution_bitcast_fusion.10
  59.5 0.8 copy.312
  60.3 6.7 %all-to-all-start.2 = ((f32[16,1,4,8,128]{4,3,2,1,0:T(8,128)}), f32[16,1,4,8,128]{4,3,2,1,0:T(8,128)S(1)}, u32[]{:S(2)}, u32[]{:S(2)}) async-start(f32[16,1,4,8,128]{4,3,2,1,0:T(8,128)} %copy.312), calls=%async_computation.2 | async-start | bytes 524288 | tf_op jit(solution)/shard_map/all_to_all | solution.py:107
  67.0 0.4 fusion
  67.4 0.3 convolution_bitcast_fusion.9
  67.7 0.3 convolution_bitcast_fusion.4
  68.0 0.4 fusion.1
  68.4 0.3 convolution_bitcast_fusion.6
  68.8 0.3 convolution_bitcast_fusion.8
  69.1 16.0 %all-to-all-done.2 = f32[16,1,4,8,128]{4,3,2,1,0:T(8,128)S(1)} async-done(((f32[16,1,4,8,128]{4,3,2,1,0:T(8,128)}), f32[16,1,4,8,128]{4,3,2,1,0:T(8,128)S(1)}, u32[]{:S(2)}, u32[]{:S(2)}) %all-to-all-start.2) | async-done | bytes 262176 | tf_op jit(solution)/shard_map/all_to_all | solution.py:107
  85.1 0.7 bitcast_convert_fusion
  85.7 1.9 %collective-permute-start.1 = (bf16[1,4,128,128]{3,2,1,0:T(8,128)(2,1)}, bf16[1,4,128,128]{3,2,1,0:T(8,128)(2,1)S(1)}, u32[]{:S(2)}, u32[]{:S(2)}) collective-permute-start(bf16[1,4,128,128]{3,2,1,0:T(8,128)(2,1)} %bitcast_convert_fusion), channel_id=1, source_target_pairs={{0,16},{16,0},{1,17},{17,1},{2,18},{18,2},{3,19},{19,3},{4,20},{20... | collective-permute-start | bytes 393224 | tf_op jit(solution)/shard_map/ppermute | solution.py:151
  87.7 0.1 fusion.44
  87.8 0.9 fusion.19
  88.7 0.9 fusion.18
  89.7 1.0 fusion.15
  90.7 0.3 fusion.23
  91.0 0.2 copy.316
  91.2 0.8 stack.36
  92.0 1.2 copy.323
  93.2 0.8 stack.37
  94.0 1.2 copy.329
  95.2 0.8 stack.39
  96.0 1.2 copy.335
  97.1 0.8 stack.40
  97.9 1.3 fusion.24
  99.2 0.8 copy.336
  100.0 4.2 %all-to-all-start.3 = ((bf16[16,2,1,16,512]{4,3,2,1,0:T(8,128)(2,1)}), bf16[16,2,1,16,512]{4,3,2,1,0:T(8,128)(2,1)}, u32[]{:S(2)}, u32[]{:S(2)}) async-start(bf16[16,2,1,16,512]{4,3,2,1,0:T(8,128)(2,1)} %copy.336), calls=%async_computation.3 | async-start | bytes 1048576 | tf_op jit(solution)/shard_map/all_to_all | solution.py:148
  104.3 0.2 fusion.16
  104.5 0.2 fusion.17
  104.8 0.3 fusion.22
  105.1 0.2 copy.346
  105.4 0.2 copy.349
  105.8 0.2 copy.339
  106.0 0.1 stack.42
  106.1 0.3 fusion.14
  106.4 0.2 copy.343
  106.9 9.9 %all-to-all-done.3 = bf16[16,2,1,16,512]{4,3,2,1,0:T(8,128)(2,1)} async-done(((bf16[16,2,1,16,512]{4,3,2,1,0:T(8,128)(2,1)}), bf16[16,2,1,16,512]{4,3,2,1,0:T(8,128)(2,1)}, u32[]{:S(2)}, u32[]{:S(2)}) %all-to-all-start.3) | async-done | bytes 524320 | tf_op jit(solution)/shard_map/all_to_all | solution.py:148
  116.7 14.4 %all_to_all.25 = bf16[16,2,1,16,512]{4,3,2,1,0:T(8,128)(2,1)S(1)} all-to-all(bf16[16,2,1,16,512]{4,3,2,1,0:T(8,128)(2,1)S(1)} %copy.350), channel_id=1, replica_groups=mesh['z'=16,'core'=2,'uly'=16] {'uly'}, dimensions={0} | all-to-all | bytes 1048576 | tf_op jit(solution)/shard_map/all_to_all | solution.py:148
  131.2 1.1 broadcast_select_fusion
  132.3 0.7 copy.378
  133.1 0.7 copy.377
  133.8 0.7 copy.376
  134.5 0.7 copy.375
  (49 shorter events, 2.0 us)
Async XLA Ops:
  2.5 7.2 %copy-start.5 = (f32[1,4,256]{2,1,0:T(4,128)S(1)}, f32[1,4,256]{2,1,0:T(4,128)}, u32[]{:S(2)}) copy-start(f32[1,4,256]{2,1,0:T(4,128)} %param.9) | copy-start | bytes 12292
  2.5 15.7 %all-to-all-start = ((bf16[16,1,16,512]{3,2,1,0:T(8,128)(2,1)}), bf16[16,1,16,512]{3,2,1,0:T(8,128)(2,1)S(1)}, u32[]{:S(2)}, u32[]{:S(2)}) async-start(bf16[16,1,16,512]{3,2,1,0:T(8,128)(2,1)} %copy.299), calls=%async_computation | async-start | bytes 524288 | tf_op jit(solution)/shard_map/all_to_all | solution.py:71
  11.4 1.0 copy-start.2
  12.3 0.9 copy-start.3
  13.3 0.9 copy-start.4
  18.9 3.5 %collective-permute-start = (f32[1,4,129,128]{3,2,1,0:T(8,128)S(1)}, f32[1,4,129,128]{3,2,1,0:T(8,128)S(1)}, u32[]{:S(2)}, u32[]{:S(2)}) collective-permute-start(f32[1,4,129,128]{3,2,1,0:T(8,128)S(1)} %pad_maximum_fusion.1), channel_id=1, source_target_pairs={{0,16},{16,0},{1,17},{17,1},{2,18},{18,2},{3,19},{19,3},{4,20},{20... | collective-permute-start | bytes 792584 | tf_op jit(solution)/shard_map/ppermute | solution.py:92
  22.4 0.7 copy-start
  24.1 34.4 %all-to-all-start.1 = ((f32[16,1,4,9,128]{4,2,3,1,0:T(4,128)}), f32[16,1,4,9,128]{4,2,3,1,0:T(4,128)S(1)}, u32[]{:S(2)}, u32[]{:S(2)}) async-start(f32[16,1,4,9,128]{4,2,3,1,0:T(4,128)} %pad_maximum_fusion), calls=%async_computation.1 | async-start | bytes 589824 | tf_op jit(solution)/shard_map/all_to_all | solution.py:104
  60.3 24.8 %all-to-all-start.2 = ((f32[16,1,4,8,128]{4,3,2,1,0:T(8,128)}), f32[16,1,4,8,128]{4,3,2,1,0:T(8,128)S(1)}, u32[]{:S(2)}, u32[]{:S(2)}) async-start(f32[16,1,4,8,128]{4,3,2,1,0:T(8,128)} %copy.312), calls=%async_computation.2 | async-start | bytes 524288 | tf_op jit(solution)/shard_map/all_to_all | solution.py:107
  85.0 2.6 %copy-start.1 = (f32[1,4,129,128]{3,2,1,0:T(8,128)S(1)}, f32[1,4,129,128]{3,2,1,0:T(8,128)}, u32[]{:S(2)}) copy-start(f32[1,4,129,128]{3,2,1,0:T(8,128)} %copy-done) | copy-start | bytes 792580
  85.7 18.6 %collective-permute-start.1 = (bf16[1,4,128,128]{3,2,1,0:T(8,128)(2,1)}, bf16[1,4,128,128]{3,2,1,0:T(8,128)(2,1)S(1)}, u32[]{:S(2)}, u32[]{:S(2)}) collective-permute-start(bf16[1,4,128,128]{3,2,1,0:T(8,128)(2,1)} %bitcast_convert_fusion), channel_id=1, source_target_pairs={{0,16},{16,0},{1,17},{17,1},{2,18},{18,2},{3,19},{19,3},{4,20},{20... | collective-permute-start | bytes 393224 | tf_op jit(solution)/shard_map/ppermute | solution.py:151
  100.0 16.7 %all-to-all-start.3 = ((bf16[16,2,1,16,512]{4,3,2,1,0:T(8,128)(2,1)}), bf16[16,2,1,16,512]{4,3,2,1,0:T(8,128)(2,1)}, u32[]{:S(2)}, u32[]{:S(2)}) async-start(bf16[16,2,1,16,512]{4,3,2,1,0:T(8,128)(2,1)} %copy.336), calls=%async_computation.3 | async-start | bytes 1048576 | tf_op jit(solution)/shard_map/all_to_all | solution.py:148

commit v14 on v12

--- a/solution.py
+++ b/solution.py
@@ -96,15 +96,14 @@
     keep_other = jnp.exp(other_last)[..., None, None]
     chip_state = keep_mine * other + own
     band = width // chip_count
-    chip_last = jnp.broadcast_to((last + other_last)[..., None], (batch_count, head_count, width))
-    last_piece = jnp.broadcast_to(
-        chip_last[None, :, :, None, :], (chip_count, batch_count, head_count, 1, width)
-    )
-    send = jnp.concatenate([to_pieces(chip_state, chip_count), last_piece], axis=3)
-    got = lax.all_to_all(send, "z", 0, 0, tiled=True)
-    forward_w, backward_w = block_weights(got[:, :, :, band, 0])
+    chip_last = jnp.pad(last + other_last, ((0, 0), (0, width - head_count)))
+    last_piece = jnp.broadcast_to(chip_last[None, :, None, :], (chip_count, batch_count, 1, width))
+    bands = to_pieces(chip_state, chip_count).reshape(chip_count, batch_count, head_count * band, width)
+    got = lax.all_to_all(jnp.concatenate([bands, last_piece], axis=2), "z", 0, 0, tiled=True)
+    forward_w, backward_w = block_weights(got[:, :, head_count * band, :head_count])
     weights = jnp.where(second, forward_w, backward_w)
-    back = lax.all_to_all(mix_blocks(weights, got[:, :, :, :band]), "z", 0, 0, tiled=True)
+    got_bands = got[:, :, : head_count * band].reshape(chip_count, batch_count, head_count, band, width)
+    back = lax.all_to_all(mix_blocks(weights, got_bands), "z", 0, 0, tiled=True)
     entering = from_pieces(back)
     fixed = (keep_other * entering + other).astype(jnp.bfloat16)
     other_entering = lax.ppermute(entering.astype(jnp.bfloat16), "core", pairs)

time: 115 us -> 114 us (level)
  no operation moved by 1% of the time
where the time goes in v14:
time: 114 us; the launch traced here: 113 us
  waiting for transfers between devices  39.8 us (35%)
  starting transfers between devices  32.7 us (29%)
  blocking collectives  20.9 us (18%)
  local copies, waits for them, and re-layouts  12.1 us (11%)
  matrix products  5.14 us (5%)
  other arithmetic  1.81 us (2%)
    all_to_all x1, blocking collectives, local(): outs = lax.all_to_all(outs, 'uly', 0, 0, tiled=True)  20.9 us
    all_to_all x1, waiting for transfers between devices, local(): lax.all_to_all(jnp.concatenate([bands, last_piece], axis=2), 'z', 0, 0, t...  18.3 us
    all_to_all x1, starting transfers between devices, local(): lax.all_to_all(jnp.concatenate([bands, last_piece], axis=2), 'z', 0, 0, t...  15.2 us
    all_to_all x1, waiting for transfers between devices, local(): back = lax.all_to_all(mix_blocks(weights, got_bands), 'z', 0, 0, tiled=True)  15.2 us
    all_to_all x1, starting transfers between devices, local(): g_parts = lax.all_to_all(g_parts, 'uly', 0, 0, tiled=True)  7.17 us
    all_to_all x1, starting transfers between devices, local(): back = lax.all_to_all(mix_blocks(weights, got_bands), 'z', 0, 0, tiled=True)  6.33 us
    all_to_all x1, waiting for transfers between devices, local(): g_parts = lax.all_to_all(g_parts, 'uly', 0, 0, tiled=True)  3.64 us
    unnamed x12, local copies, waits for them, and re-layouts  3.62 us
  transfers between devices with their start and end apart: 5, of which 5 were waited for; matrix products, arithmetic and copies ran while one was open for 5% of the time, Pallas kernels for 0%

profile of v14, /device:TPU:32, one launch (start us, length us, event | category | flops | bytes accessed | tf_op | source)
XLA Modules:
  0.0 113.5 jit_solution(3772110622629510060)
XLA Ops:
  0.6 1.0 copy.252
  1.7 0.9 copy.191
  2.5 7.2 %all-to-all-start = ((bf16[16,1,16,512]{3,2,1,0:T(8,128)(2,1)}), bf16[16,1,16,512]{3,2,1,0:T(8,128)(2,1)S(1)}, u32[]{:S(2)}, u32[]{:S(2)}) async-start(bf16[16,1,16,512]{3,2,1,0:T(8,128)(2,1)} %copy.191), calls=%async_computation | async-start | bytes 524288 | tf_op jit(solution)/shard_map/all_to_all | solution.py:71
  9.7 1.2 %reduce-window.6 = f32[1,4,2,128]{3,2,1,0:T(2,128)S(1)} reduce-window(f32[1,4,2,128]{3,2,1,0:T(2,128)S(1)} %reshape.456, f32[]{:T(128)} %constant.14.clone.1), window={size=1x1x1x128 pad=0_0x0_0x0_0x127_0}, to_apply=%region_0.0 | reduce-window | flops 130048 | bytes 8196 | tf_op jit(solution)/shard_map/reduce-window
  11.0 0.1 slice.44
  11.0 0.1 copy.245
  11.2 0.1 copy.185
  11.4 0.1 copy.189
  11.5 0.1 copy.194
  11.6 0.7 copy-done.1
  12.3 0.1 reshape.454
  12.4 0.9 copy-done.2
  13.4 0.9 copy-done.3
  14.2 0.1 copy.246
  14.4 0.2 fusion.13
  14.6 3.6 %all-to-all-done = bf16[16,1,16,512]{3,2,1,0:T(8,128)(2,1)S(1)} async-done(((bf16[16,1,16,512]{3,2,1,0:T(8,128)(2,1)}), bf16[16,1,16,512]{3,2,1,0:T(8,128)(2,1)S(1)}, u32[]{:S(2)}, u32[]{:S(2)}) %all-to-all-start) | async-done | bytes 262176 | tf_op jit(solution)/shard_map/all_to_all | solution.py:71
  18.3 0.5 fusion.18
  18.8 0.1 broadcast_in_dim.57
  18.9 1.9 %collective-permute-start = (f32[1,4,129,128]{3,2,1,0:T(8,128)S(1)}, f32[1,4,129,128]{3,2,1,0:T(8,128)S(1)}, u32[]{:S(2)}, u32[]{:S(2)}) collective-permute-start(f32[1,4,129,128]{3,2,1,0:T(8,128)S(1)} %pad_maximum_fusion), channel_id=1, source_target_pairs={{0,16},{16,0},{1,17},{17,1},{2,18},{18,2},{3,19},{19,3},{4,20},{20... | collective-permute-start | bytes 792584 | tf_op jit(solution)/shard_map/ppermute | solution.py:92
  20.9 1.5 %collective-permute-done = f32[1,4,129,128]{3,2,1,0:T(8,128)S(1)} collective-permute-done((f32[1,4,129,128]{3,2,1,0:T(8,128)S(1)}, f32[1,4,129,128]{3,2,1,0:T(8,128)S(1)}, u32[]{:S(2)}, u32[]{:S(2)}) %collective-permute-start) | collective-permute-done | bytes 264224 | tf_op jit(solution)/shard_map/ppermute | solution.py:92
  22.4 0.1 fusion.16
  22.5 0.1 exponential_reduce_fusion
  22.7 1.0 copy.198
  23.7 15.2 %all-to-all-start.1 = ((f32[16,1,33,128]{3,1,2,0:T(1,128)}), f32[16,1,33,128]{3,1,2,0:T(1,128)S(1)}, u32[]{:S(2)}, u32[]{:S(2)}) async-start(f32[16,1,33,128]{3,1,2,0:T(1,128)} %copy.198), calls=%async_computation.1 | async-start | bytes 540672 | tf_op jit(solution)/shard_map/all_to_all | solution.py:102
  38.9 0.1 copy.244
  39.1 18.3 %all-to-all-done.1 = f32[16,1,33,128]{3,1,2,0:T(1,128)S(1)} async-done(((f32[16,1,33,128]{3,1,2,0:T(1,128)}), f32[16,1,33,128]{3,1,2,0:T(1,128)S(1)}, u32[]{:S(2)}, u32[]{:S(2)}) %all-to-all-start.1) | async-done | bytes 270368 | tf_op jit(solution)/shard_map/all_to_all | solution.py:102
  57.4 0.1 copy.200
  57.5 0.2 copy.199
  57.7 0.1 copy.201
  57.8 0.1 copy.203
  57.9 0.1 copy.204
  57.9 0.4 convolution_bitcast_fusion.7
  58.4 0.8 copy.205
  59.2 6.3 %all-to-all-start.2 = ((f32[16,1,4,8,128]{4,3,2,1,0:T(8,128)}), f32[16,1,4,8,128]{4,3,2,1,0:T(8,128)S(1)}, u32[]{:S(2)}, u32[]{:S(2)}) async-start(f32[16,1,4,8,128]{4,3,2,1,0:T(8,128)} %copy.205), calls=%async_computation.2 | async-start | bytes 524288 | tf_op jit(solution)/shard_map/all_to_all | solution.py:106
  65.5 0.4 fusion
  65.9 0.3 convolution_bitcast_fusion.6
  66.2 1.1 %convolution_bitcast_fusion.1 = f32[1,256,4,128]{3,1,2,0:T(8,128)} fusion(bf16[4,256,256]{2,1,0:T(8,128)(2,1)S(1)} %fusion, bf16[256,4,128]{2,1,0:T(4,128)(2,1)S(1)} %reshape.465), kind=kOutput, calls=%fused_computation.5 | convolution fusion | flops 67108864 | bytes 1310720 | tf_op jit(solution)/shard_map/bhij,bihe->bjhe/dot_general | solution.py:135
  67.3 0.4 fusion.1
  67.8 0.3 convolution_bitcast_fusion.3
  68.1 0.3 convolution_bitcast_fusion.5
  68.4 15.2 %all-to-all-done.2 = f32[16,1,4,8,128]{4,3,2,1,0:T(8,128)S(1)} async-done(((f32[16,1,4,8,128]{4,3,2,1,0:T(8,128)}), f32[16,1,4,8,128]{4,3,2,1,0:T(8,128)S(1)}, u32[]{:S(2)}, u32[]{:S(2)}) %all-to-all-start.2) | async-done | bytes 262176 | tf_op jit(solution)/shard_map/all_to_all | solution.py:106
  83.6 2.1 %collective-permute-start.1 = (bf16[1,4,128,128]{3,2,1,0:T(8,128)(2,1)S(1)}, bf16[1,4,128,128]{3,2,1,0:T(8,128)(2,1)S(1)}, u32[]{:S(2)}, u32[]{:S(2)}) collective-permute-start(bf16[1,4,128,128]{3,2,1,0:T(8,128)(2,1)S(1)} %bitcast_convert_fusion), channel_id=1, source_target_pairs={{0,16},{16,0},{1,17},{17,1},{2,18},{18,2},{3,19},{19,3},{4,20},{20... | collective-permute-start | bytes 393224 | tf_op jit(solution)/shard_map/ppermute | solution.py:109
  85.7 0.1 fusion.15
  85.8 1.2 %collective-permute-done.1 = bf16[1,4,128,128]{3,2,1,0:T(8,128)(2,1)S(1)} collective-permute-done((bf16[1,4,128,128]{3,2,1,0:T(8,128)(2,1)S(1)}, bf16[1,4,128,128]{3,2,1,0:T(8,128)(2,1)S(1)}, u32[]{:S(2)}, u32[]{:S(2)}) %collective-permute-start.1) | collective-permute-done | bytes 131104 | tf_op jit(solution)/shard_map/ppermute | solution.py:109
  87.0 0.3 fusion.8
  87.3 0.2 copy.228
  87.5 0.1 stack.18
  87.6 0.3 fusion.12
  87.9 0.2 copy.209
  88.2 0.1 stack.15
  88.3 0.2 fusion.10
  88.5 0.2 copy.216
  88.7 0.1 stack.16
  88.8 0.2 fusion.9
  89.1 0.2 copy.222
  89.3 0.1 stack.17
  89.4 0.1 maximum_bitcast_fusion
  89.6 0.1 copy.229
  89.6 20.9 %all_to_all.20 = bf16[16,4,1,16,512]{4,3,2,1,0:T(8,128)(2,1)S(1)} all-to-all(bf16[16,4,1,16,512]{4,3,2,1,0:T(8,128)(2,1)S(1)} %copy.229), channel_id=1, replica_groups=mesh['z'=16,'core'=2,'uly'=16] {'uly'}, dimensions={0} | all-to-all | bytes 2097152 | tf_op jit(solution)/shard_map/all_to_all | solution.py:145
  110.5 0.1 slice_bitcast_fusion
  110.6 0.7 copy.250
  111.3 0.7 copy.249
  112.0 0.7 copy.248
  112.8 0.7 copy.247
  (33 shorter events, 0.6 us)
Async XLA Ops:
  2.5 7.2 %copy-start.4 = (f32[1,4,256]{2,1,0:T(4,128)S(1)}, f32[1,4,256]{2,1,0:T(4,128)}, u32[]{:S(2)}) copy-start(f32[1,4,256]{2,1,0:T(4,128)} %param.9) | copy-start | bytes 12292
  2.5 15.7 %all-to-all-start = ((bf16[16,1,16,512]{3,2,1,0:T(8,128)(2,1)}), bf16[16,1,16,512]{3,2,1,0:T(8,128)(2,1)S(1)}, u32[]{:S(2)}, u32[]{:S(2)}) async-start(bf16[16,1,16,512]{3,2,1,0:T(8,128)(2,1)} %copy.191), calls=%async_computation | async-start | bytes 524288 | tf_op jit(solution)/shard_map/all_to_all | solution.py:71
  11.4 1.0 copy-start.1
  12.3 0.9 copy-start.2
  13.3 0.9 copy-start.3
  18.9 3.5 %collective-permute-start = (f32[1,4,129,128]{3,2,1,0:T(8,128)S(1)}, f32[1,4,129,128]{3,2,1,0:T(8,128)S(1)}, u32[]{:S(2)}, u32[]{:S(2)}) collective-permute-start(f32[1,4,129,128]{3,2,1,0:T(8,128)S(1)} %pad_maximum_fusion), channel_id=1, source_target_pairs={{0,16},{16,0},{1,17},{17,1},{2,18},{18,2},{3,19},{19,3},{4,20},{20... | collective-permute-start | bytes 792584 | tf_op jit(solution)/shard_map/ppermute | solution.py:92
  23.7 33.7 %all-to-all-start.1 = ((f32[16,1,33,128]{3,1,2,0:T(1,128)}), f32[16,1,33,128]{3,1,2,0:T(1,128)S(1)}, u32[]{:S(2)}, u32[]{:S(2)}) async-start(f32[16,1,33,128]{3,1,2,0:T(1,128)} %copy.198), calls=%async_computation.1 | async-start | bytes 540672 | tf_op jit(solution)/shard_map/all_to_all | solution.py:102
  59.2 24.4 %all-to-all-start.2 = ((f32[16,1,4,8,128]{4,3,2,1,0:T(8,128)}), f32[16,1,4,8,128]{4,3,2,1,0:T(8,128)S(1)}, u32[]{:S(2)}, u32[]{:S(2)}) async-start(f32[16,1,4,8,128]{4,3,2,1,0:T(8,128)} %copy.205), calls=%async_computation.2 | async-start | bytes 524288 | tf_op jit(solution)/shard_map/all_to_all | solution.py:106
  83.6 3.4 %copy-start = (f32[1,256,4,128]{3,1,2,0:T(8,128)S(1)}, f32[1,256,4,128]{3,1,2,0:T(8,128)}, u32[]{:S(2)}) copy-start(f32[1,256,4,128]{3,1,2,0:T(8,128)} %convolution_bitcast_fusion.1) | copy-start | bytes 1572868
  83.6 3.4 %collective-permute-start.1 = (bf16[1,4,128,128]{3,2,1,0:T(8,128)(2,1)S(1)}, bf16[1,4,128,128]{3,2,1,0:T(8,128)(2,1)S(1)}, u32[]{:S(2)}, u32[]{:S(2)}) collective-permute-start(bf16[1,4,128,128]{3,2,1,0:T(8,128)(2,1)S(1)} %bitcast_convert_fusion), channel_id=1, source_target_pairs={{0,16},{16,0},{1,17},{17,1},{2,18},{18,2},{3,19},{19,3},{4,20},{20... | collective-permute-start | bytes 393224 | tf_op jit(solution)/shard_map/ppermute | solution.py:109
